TPU v7x, 512 devices: a whole 4x4x16 slice. The times are simulated.
512 devices in a mesh: template: 16 (over y, x_hi, core), fsdp: 16 (over z), dp: 2 (over x_lo).
Axes of the slice: x: 4 (x_hi: 2, x_lo: 2; x = x_hi * 2 + x_lo), y: 4, z: 16, core: 2. Of those that a mesh axis runs over, the one named last changes fastest.
Arguments:
- hidden: bfloat16 [16, 4096, 8192], P('template', ('fsdp', 'dp')), may hold values from -6 to 6
- target: bfloat16 [16, 4096, 512], P('template', ('fsdp', 'dp')), may hold values from -6 to 6
- weight: bfloat16 [16, 8192, 512], P('template', 'fsdp'), may hold values from -6 to 6
- gain: bfloat16 [16, 8192], P('template', 'fsdp'), may hold values from 0.099609375 to 1.8984375
Outputs:
- merged_weight: float32 [8192, 512], P(('fsdp', 'dp'))
- merged_gain: float32 [8192], P(('fsdp', 'dp'))
All inputs are finite; a program needn't handle non-finite values.
Results may differ from a plain program's by a relative error of at most 0.0018.
Values may be sent and summed in bfloat16 or wider, within the bound.
No kernel may reach another device: no remote copies, remote signals or barrier semaphores. Data moves between devices by JAX's collectives and lax.ppermute only.
A program may use at most 64 MiB of HBM per device.

v0:
```python
import math

import jax
import jax.numpy as jnp
from jax import lax
from jax.sharding import PartitionSpec as P


def body(hidden, target, weight, gain):
    token_batch = hidden[0]
    goal = target[0]
    w_shard = weight[0]
    g_shard = gain[0]
    width = token_batch.shape[1]
    scale = 1.0 / math.sqrt(width)
    merge_quotient = lax.rsqrt(
        jnp.mean(jnp.square(token_batch.astype(jnp.float32)), axis=1, keepdims=True) + 1e-05
    )
    w_full, complete_gain = (
        lax.all_gather(w_shard, "fsdp", axis=0, tiled=True),
        lax.all_gather(g_shard, "fsdp", axis=0, tiled=True),
    )
    normalized_activation = token_batch.astype(jnp.float32) * merge_quotient
    normalized_input = (normalized_activation * complete_gain.astype(jnp.float32)[None, :]).astype(
        jnp.bfloat16
    )
    values = jnp.dot(normalized_input, w_full, preferred_element_type=jnp.float32) * scale
    delta = (values - goal.astype(jnp.float32)).astype(jnp.bfloat16)
    backward_pass = (
        jnp.einsum("th,dh->td", delta, w_full, preferred_element_type=jnp.float32) * scale
    )
    gain_information = jnp.sum(jnp.square(backward_pass * normalized_activation), axis=0)
    sq_normed = jnp.square(normalized_input.astype(jnp.float32)).astype(jnp.bfloat16)
    sq_delta = jnp.square(delta.astype(jnp.float32)).astype(jnp.bfloat16)
    mine = width // lax.axis_size(("fsdp", "dp"))
    columns = lax.all_to_all(sq_normed, ("fsdp", "dp"), split_axis=1, concat_axis=0, tiled=True)
    fisher = jnp.einsum(
        "td,th->dh",
        columns,
        lax.all_gather(sq_delta, ("fsdp", "dp"), axis=0, tiled=True),
        preferred_element_type=jnp.float32,
    )
    gain_total = lax.psum(gain_information.astype(jnp.bfloat16), ("fsdp", "dp")).astype(jnp.float32)
    where = lax.axis_index(("fsdp", "dp")) * mine
    gain_information_sum = lax.dynamic_slice_in_dim(gain_total, where, mine, 0)
    offset = lax.axis_index("dp") * mine
    theta = lax.dynamic_slice_in_dim(w_shard, offset, mine, 0).astype(jnp.float32)
    gmine = lax.dynamic_slice_in_dim(g_shard, offset, mine, 0).astype(jnp.float32)
    weighted = fisher * theta
    gain_weighted = (gain_information_sum * gmine)[:, None]
    gain_column = gain_information_sum[:, None]
    num, den, gnum, gden = lax.psum((weighted, fisher, gain_weighted, gain_column), "template")
    return (num / den, gnum[:, 0] / gden[:, 0])


def solution(mesh):
    in_specs = (
        P("template", ("fsdp", "dp"), None),
        P("template", ("fsdp", "dp"), None),
        P("template", "fsdp", None),
        P("template", "fsdp"),
    )
    out_specs = (P(("fsdp", "dp"), None), P(("fsdp", "dp")))
    return jax.shard_map(body, mesh=mesh, in_specs=in_specs, out_specs=out_specs, check_vma=False)
```

profile of v0, /device:TPU:1, one launch (start us, length us, event | category | flops | bytes accessed | tf_op | source)
XLA Modules:
  0.0 532.3 jit_solution(14916185869821254216)
XLA Ops:
  7.2 0.0 copy-start
  7.2 0.0 all-gather.7.cloned.1.call-start
  7.2 0.7 all-gather.7.cloned.1.call-update
  7.9 30.4 %all-gather = bf16[1,8192]{1,0:T(2,128)(2,1)S(1)} all-gather(bf16[1,512]{1,0:T(2,128)(2,1)} %param.7), channel_id=2, replica_groups=mesh['template'=16,'fsdp'=16,'dp'=2] {'fsdp'}, dimensions={1}, use_global_device_ids=true | all-gather | bytes 17408 | tf_op jit(solution)/shard_map/all_gather | solution.py:21
  38.3 0.1 convert_reduce_fusion
  38.4 2.2 copy.7
  40.7 0.0 copy-done
  40.7 0.5 fusion.5
  41.2 0.0 copy-start.3
  41.2 3.9 multiply_convert_fusion.1
  45.1 6.8 %all-to-all-start = ((bf16[128,32,256]{2,0,1:T(8,128)(2,1)}), bf16[128,32,256]{2,0,1:T(8,128)(2,1)}, u32[]{:S(2)}, u32[]{:S(2)}) async-start(bf16[128,32,256]{2,0,1:T(8,128)(2,1)} %multiply_convert_fusion.1), calls=%async_computation | async-start | bytes 4194304 | tf_op jit(solution)/shard_map/all_to_all | solution.py:36
  52.0 0.0 all-gather.5.cloned.1.call-start
  52.1 159.3 %all-gather.7.cloned.1.call-done = bf16[1,8192,512]{2,1,0:T(8,128)(2,1)} async-done(((bf16[1,512,512]{2,1,0:T(8,128)(2,1)}), bf16[1,8192,512]{2,1,0:T(8,128)(2,1)}) %all-gather.7.cloned.1.call-update) | async-done | bytes 8388624 | tf_op jit(solution)/shard_map/all_gather | solution.py:20
  211.3 0.0 copy-done.3
  211.3 0.0 copy-start.2
  211.3 0.0 copy-start.1
  211.3 5.4 %multiply_convert_fusion.9 = (bf16[128,512]{1,0:T(8,128)(2,1)}, bf16[128,512]{1,0:T(8,128)(2,1)S(1)}) fusion(bf16[1,128,512]{2,1,0:T(8,128)(2,1)S(1)} %copy-done.3, bf16[1,8192,512]{2,1,0:T(8,128)(2,1)} %all-gather.7.cloned.1.call-done, bf16[1,128,8192]{2,1,0:T(8,128)(2,1)S(1)} %copy-done, f32[8192]{0:T(1024)S(1)} %bitcast.58, f32[128]{0:T(128)S(1)} %add_rsqrt_fusion), kind=kOutput, calls=%fused_computation.21 | convolution fusion | flops 1078394880 | bytes 10912256 | tf_op jit(solution)/shard_map/dot_general | solution.py:27
  216.8 0.0 all-gather.5.cloned.1.call-update
  216.8 0.0 all-reduce.4.cloned.1.call-start
  216.8 0.0 copy-done.2
  216.9 0.0 all-to-all-done
  216.9 119.9 %all-gather.5.cloned.1.call-done = bf16[4096,512]{1,0:T(8,128)(2,1)} async-done(((bf16[128,512]{1,0:T(8,128)(2,1)}), bf16[4096,512]{1,0:T(8,128)(2,1)}) %all-gather.5.cloned.1.call-update) | async-done | bytes 4194320 | tf_op jit(solution)/shard_map/all_gather | solution.py:40
  336.8 0.0 copy-done.1
  336.8 5.1 convert_multiply_fusion
  341.8 0.0 all-reduce.4.cloned.1.call-update
  341.9 6.2 %fusion.10 = bf16[8192]{0:T(1024)(128)(2,1)S(1)} fusion(f32[128]{0:T(128)S(1)} %add_rsqrt_fusion, bf16[1,128,8192]{2,1,0:T(8,128)(2,1)S(1)} %copy-done, bf16[128,512]{1,0:T(8,128)(2,1)S(1)} %get-tuple-element.7, bf16[1,8192,512]{2,1,0:T(8,128)(2,1)} %all-gather.7.cloned.1.call-done), kind=kOutput, calls=%fused_computation.16 | convolution fusion | flops 1080025088 | bytes 10633728 | tf_op jit(solution)/shard_map/th,dh->td/dot_general | solution.py:30
  348.1 95.7 %psum.37 = bf16[8192]{0:T(1024)(128)(2,1)S(1)} all-reduce(bf16[8192]{0:T(1024)(128)(2,1)S(1)} %fusion.10), channel_id=1, replica_groups=mesh['template'=16,'fsdp'=16,'dp'=2] {'fsdp','dp'}, use_global_device_ids=true, to_apply=%region_4.0 | all-reduce | flops 8192 | bytes 32768 | tf_op jit(solution)/shard_map/psum | solution.py:43
  443.8 0.1 dynamic-slice_convert_fusion.1
  443.9 0.1 fusion.22
  443.9 79.2 %all-reduce = (f32[256,1]{0,1:T(1,128)S(1)}, f32[256,1]{0,1:T(1,128)S(1)}) all-reduce(f32[256,1]{0,1:T(1,128)S(1)} %bitcast.60, f32[256,1]{0,1:T(1,128)S(1)} %bitcast.61), channel_id=1, replica_groups=mesh['template'=16,'fsdp'=16,'dp'=2] {'template'}, use_global_device_ids=true, to_apply=%region_5.0 | all-reduce | flops 512 | bytes 4096 | tf_op jit(solution)/shard_map/psum | solution.py:52
  523.1 0.6 div.18
  523.7 0.0 all-reduce.4.cloned.1.call-done
  523.7 2.1 div.17
  (4 shorter events, 0.1 us)
Async XLA Ops:
  7.2 33.5 %copy-start = (bf16[1,128,8192]{2,1,0:T(8,128)(2,1)S(1)}, bf16[1,128,8192]{2,1,0:T(8,128)(2,1)}, u32[]{:S(2)}) copy-start(bf16[1,128,8192]{2,1,0:T(8,128)(2,1)} %param.4) | copy-start | bytes 6291460
  7.2 204.2 %all-gather.7.cloned.1.call-start = ((), (), s32[]{:S(2)}) async-start(), calls=%async_computation.2 | async-start | bytes 8912896 | tf_op jit(solution)/shard_map/all_gather | solution.py:20
  41.2 170.1 %copy-start.3 = (bf16[1,128,512]{2,1,0:T(8,128)(2,1)S(1)}, bf16[1,128,512]{2,1,0:T(8,128)(2,1)}, u32[]{:S(2)}) copy-start(bf16[1,128,512]{2,1,0:T(8,128)(2,1)} %param.5) | copy-start | bytes 393220
  45.1 171.7 %all-to-all-start = ((bf16[128,32,256]{2,0,1:T(8,128)(2,1)}), bf16[128,32,256]{2,0,1:T(8,128)(2,1)}, u32[]{:S(2)}, u32[]{:S(2)}) async-start(bf16[128,32,256]{2,0,1:T(8,128)(2,1)} %multiply_convert_fusion.1), calls=%async_computation | async-start | bytes 4194304 | tf_op jit(solution)/shard_map/all_to_all | solution.py:36
  52.0 284.8 %all-gather.5.cloned.1.call-start = ((), (), s32[]{:S(2)}) async-start(), calls=%async_computation.1 | async-start | bytes 4325376 | tf_op jit(solution)/shard_map/all_gather | solution.py:40
  211.3 5.5 %copy-start.2 = (bf16[1,512]{1,0:T(2,128)(2,1)S(1)}, bf16[1,512]{1,0:T(2,128)(2,1)}, u32[]{:S(2)}) copy-start(bf16[1,512]{1,0:T(2,128)(2,1)} %param.7) | copy-start | bytes 3076
  211.3 125.4 %copy-start.1 = (bf16[1,512,512]{2,1,0:T(8,128)(2,1)S(1)}, bf16[1,512,512]{2,1,0:T(8,128)(2,1)}, u32[]{:S(2)}) copy-start(bf16[1,512,512]{2,1,0:T(8,128)(2,1)} %param.6) | copy-start | bytes 1572868
  216.8 306.9 %all-reduce.4.cloned.1.call-start = ((), (), s32[]{:S(2)}) async-start(), calls=%async_computation.3 | async-start | bytes 2097152 | tf_op jit(solution)/shard_map/psum | solution.py:52
Sparse Core Ops, SparseCore 0:
  10.1 201.2 all-gather.6
  216.9 119.8 all-gather.4
  342.0 171.5 all-reduce.3
where the time goes:
time: 533 us; the launch traced here: 532 us
  waiting for transfers between devices  280 us (53%)
  blocking collectives  205 us (38%)
  matrix products  16.7 us (3%)
  between operations  13.8 us (3%)
  other arithmetic  7.36 us (1%)
  starting transfers between devices  6.94 us (1%)
    all_gather x1, waiting for transfers between devices, body(): lax.all_gather(w_shard, 'fsdp', axis=0, tiled=True)  159 us
    all_gather x1, waiting for transfers between devices, body(): lax.all_gather(sq_delta, ('fsdp', 'dp'), axis=0, tiled=True)  120 us
    psum x1, blocking collectives, body(): lax.psum(gain_information.astype(jnp.bfloat16), ('fsdp', 'dp'))  95.7 us
    psum x1, blocking collectives, body(): lax.psum((weighted, fisher, gain_weighted, gain_column), 'template')  79.2 us
    all_gather x1, blocking collectives, body(): lax.all_gather(g_shard, 'fsdp', axis=0, tiled=True)  30.4 us
  transfers between devices with their start and end apart: 4, of which 2 were waited for; matrix products, arithmetic and copies ran while one was open for 4% of the time, Pallas kernels for 0%

commit v1 on v0

v1 whole, which is shorter than its diff:
```python
import math

import jax
import jax.numpy as jnp
from jax import lax
from jax.sharding import PartitionSpec as P


def body(hidden, target, weight, gain):
    token_batch = hidden[0]
    goal = target[0]
    w_shard = weight[0]
    g_shard = gain[0]
    width = token_batch.shape[1]
    rows = w_shard.shape[0]
    heads = w_shard.shape[1]
    scale = 1.0 / math.sqrt(width)
    n_t = lax.axis_size("template")
    n_dp = lax.axis_size("dp")

    hidden_f = token_batch.astype(jnp.float32)
    ratio = lax.rsqrt(jnp.mean(jnp.square(hidden_f), axis=1, keepdims=True) + 1e-05)
    w_full = lax.all_gather(w_shard, "fsdp", axis=0, tiled=True)
    g_full = lax.all_gather(g_shard, "fsdp", axis=0, tiled=True)
    xhat = hidden_f * ratio
    normed = (xhat * g_full.astype(jnp.float32)[None, :]).astype(jnp.bfloat16)
    values = jnp.dot(normed, w_full, preferred_element_type=jnp.float32) * scale
    delta = (values - goal.astype(jnp.float32)).astype(jnp.bfloat16)

    local_hidden = lax.all_to_all(token_batch, "fsdp", 1, 0, tiled=True)
    local_ratio = lax.all_gather(ratio, "fsdp", axis=0, tiled=True)
    local_delta = lax.all_gather(delta, "fsdp", axis=0, tiled=True)
    local_xhat = local_hidden.astype(jnp.float32) * local_ratio
    g_f = g_shard.astype(jnp.float32)
    local_normed = (local_xhat * g_f[None, :]).astype(jnp.bfloat16)
    sq_normed = jnp.square(local_normed.astype(jnp.float32)).astype(jnp.bfloat16)
    sq_delta = jnp.square(local_delta.astype(jnp.float32)).astype(jnp.bfloat16)
    fisher = jnp.einsum("td,th->dh", sq_normed, sq_delta, preferred_element_type=jnp.float32)
    back = jnp.einsum("th,dh->td", local_delta, w_shard, preferred_element_type=jnp.float32) * scale
    gain_info = jnp.sum(jnp.square(back * local_xhat), axis=0)

    extra = jnp.zeros((rows, 128), jnp.float32)
    extra = extra.at[:, 0].set(gain_info * g_f).at[:, 1].set(gain_info)
    pack = jnp.concatenate([fisher * w_shard.astype(jnp.float32), fisher, extra], axis=1)
    cols = pack.shape[1]
    piece = rows // (n_t * n_dp)
    pack = pack.reshape(n_dp, n_t, piece, cols).transpose(1, 0, 2, 3).reshape(n_t * n_dp, piece, cols)
    parts = lax.all_to_all(pack, ("template", "dp"), 0, 0, tiled=True)
    total = jnp.sum(parts, axis=0, keepdims=True)
    spread = lax.all_to_all(jnp.broadcast_to(total, (n_t, piece, cols)), "template", 0, 0, tiled=True)
    full = spread.reshape(n_t * piece, cols)
    merged = full[:, :heads] / full[:, heads : 2 * heads]
    merged_gain = full[:, 2 * heads] / full[:, 2 * heads + 1]
    return merged, merged_gain


def solution(mesh):
    in_specs = (
        P("template", ("fsdp", "dp"), None),
        P("template", ("fsdp", "dp"), None),
        P("template", "fsdp", None),
        P("template", "fsdp"),
    )
    out_specs = (P(("fsdp", "dp"), None), P(("fsdp", "dp")))
    return jax.shard_map(body, mesh=mesh, in_specs=in_specs, out_specs=out_specs, check_vma=False)
```

time: 533 us -> 368 us (0.69)
  waiting for transfers between devices: 280 us -> 84.6 us
  blocking collectives: 205 us -> 224 us
  starting transfers between devices: 6.94 us -> 16 us
  local copies, waits for them, and re-layouts: 2.28 us -> 9.14 us
    all_gather x2, waiting for transfers between devices: 279 us -> 83.9 us  [the longest x1 45.9 us: body(): w_full = lax.all_gather(w_shard, 'fsdp', axis=0, tiled=True)]
    psum x2 -> x0, blocking collectives: 175 us -> none  [the longest x1 95.7 us: body(): lax.psum(gain_information.astype(jnp.bfloat16), ('fsdp', 'dp'))]
    all_gather x1 -> x2, blocking collectives: 30.4 us -> 154 us  [the longest x1 133 us: body(): g_full = lax.all_gather(g_shard, 'fsdp', axis=0, tiled=True)]
    all_to_all x0 -> x2, blocking collectives: none -> 70.5 us  [the longest x1 47.1 us: body(): parts = lax.all_to_all(pack, ('template', 'dp'), 0, 0, tiled=True)]
    all_to_all x1, starting transfers between devices: 6.82 us -> 15.9 us  [body(): local_hidden = lax.all_to_all(token_batch, 'fsdp', 1, 0, tiled=True)]
  transfers between devices with their start and end apart: 4 -> 3, of which waited for: 2 -> 2; matrix products, arithmetic and copies ran while one was open for 4% -> 4% of each run, Pallas kernels for 0% -> 0%
where the time goes in v1:
time: 368 us
  blocking collectives  224 us (61%)
  waiting for transfers between devices  84.6 us (23%)
  starting transfers between devices  16 us (4%)
  between operations  14.2 us (4%)
  matrix products  12.1 us (3%)
  local copies, waits for them, and re-layouts  9.14 us (2%)
  other arithmetic  7.33 us (2%)
    all_gather x1, blocking collectives, body(): g_full = lax.all_gather(g_shard, 'fsdp', axis=0, tiled=True)  133 us
    all_to_all x1, blocking collectives, body(): parts = lax.all_to_all(pack, ('template', 'dp'), 0, 0, tiled=True)  47.1 us
    all_gather x1, waiting for transfers between devices, body(): w_full = lax.all_gather(w_shard, 'fsdp', axis=0, tiled=True)  45.9 us
    all_gather x1, waiting for transfers between devices, body(): local_delta = lax.all_gather(delta, 'fsdp', axis=0, tiled=True)  38 us
    all_to_all x1, blocking collectives, body(): lax.all_to_all(jnp.broadcast_to(total, (n_t, piece, cols)), 'template', 0...  23.4 us
    all_gather x1, blocking collectives, body(): local_ratio = lax.all_gather(ratio, 'fsdp', axis=0, tiled=True)  20.9 us
    all_to_all x1, starting transfers between devices, body(): local_hidden = lax.all_to_all(token_batch, 'fsdp', 1, 0, tiled=True)  15.9 us
  transfers between devices with their start and end apart: 3, of which 2 were waited for; matrix products, arithmetic and copies ran while one was open for 4% of the time, Pallas kernels for 0%

profile of v1, /device:TPU:1, one launch (start us, length us, event | category | flops | bytes accessed | tf_op | source)
XLA Modules:
  0.0 367.7 jit_solution(5478946949696858458)
XLA Ops:
  7.2 0.0 all-gather.9.cloned.1.call-start
  7.2 0.7 all-gather.9.cloned.1.call-update
  7.9 2.4 copy.16
  10.3 2.5 copy.12
  12.8 0.0 copy-start.2
  12.8 0.0 copy-start
  12.8 0.0 copy-start.3
  12.8 15.9 %all-to-all-start = ((bf16[128,16,512]{2,0,1:T(8,128)(2,1)}), bf16[128,16,512]{2,0,1:T(8,128)(2,1)}, u32[]{:S(2)}, u32[]{:S(2)}) async-start(bf16[128,16,512]{2,0,1:T(8,128)(2,1)} %copy.12), calls=%async_computation | async-start | bytes 4194304 | tf_op jit(solution)/shard_map/all_to_all | solution.py:30
  28.7 0.0 all-gather.7.cloned.1.call-start
  28.8 0.0 copy-done.2
  28.8 132.9 %all-gather.1 = bf16[1,8192]{1,0:T(2,128)(2,1)S(1)} all-gather(bf16[1,512]{1,0:T(2,128)(2,1)S(1)} %copy-done.2), channel_id=3, replica_groups=mesh['template'=16,'fsdp'=16,'dp'=2] {'fsdp'}, dimensions={1}, use_global_device_ids=true | all-gather | bytes 17408 | tf_op jit(solution)/shard_map/all_gather | solution.py:24
  161.8 0.0 copy-done
  161.8 0.5 fusion.2
  162.3 45.9 %all-gather.9.cloned.1.call-done = bf16[1,8192,512]{2,1,0:T(8,128)(2,1)} async-done(((bf16[1,512,512]{2,1,0:T(8,128)(2,1)}), bf16[1,8192,512]{2,1,0:T(8,128)(2,1)}) %all-gather.9.cloned.1.call-update) | async-done | bytes 8388624 | tf_op jit(solution)/shard_map/all_gather | solution.py:23
  208.2 0.0 copy-done.3
  208.2 0.0 copy-start.1
  208.2 5.4 %fusion.20 = bf16[128,512]{1,0:T(8,128)(2,1)} fusion(bf16[1,8192,512]{2,1,0:T(8,128)(2,1)} %all-gather.9.cloned.1.call-done, bf16[1,128,8192]{2,1,0:T(8,128)(2,1)S(1)} %copy-done, f32[8192]{0:T(1024)S(1)} %bitcast.68, f32[128]{0:T(128)S(1)} %get-tuple-element.29, bf16[1,128,512]{2,1,0:T(8,128)(2,1)S(1)} %copy-done.3), kind=kOutput, calls=%fused_computation.19 | convolution fusion | flops 1078198272 | bytes 10781184 | tf_op jit(solution)/shard_map/dot_general | solution.py:27
  213.6 0.0 all-gather.7.cloned.1.call-update
  213.6 0.0 copy-done.1
  213.6 0.2 copy.13
  213.8 0.6 compare_reduce_fusion
  214.5 0.6 compare_reduce_fusion.1
  215.1 20.9 %all-gather.3 = f32[16,1,128]{2,1,0:T(1,128)S(1)} all-gather(f32[1,1,128]{2,1,0:T(1,128)S(1)} %get-tuple-element.28), channel_id=2, replica_groups=mesh['template'=16,'fsdp'=16,'dp'=2] {'fsdp'}, dimensions={0}, use_global_device_ids=true | all-gather | bytes 8704 | tf_op jit(solution)/shard_map/all_gather | solution.py:31
  236.1 0.0 all-to-all-done
  236.1 2.3 multiply_convert_fusion.1
  238.4 38.0 %all-gather.7.cloned.1.call-done = bf16[2048,512]{1,0:T(8,128)(2,1)} async-done(((bf16[128,512]{1,0:T(8,128)(2,1)}), bf16[2048,512]{1,0:T(8,128)(2,1)}) %all-gather.7.cloned.1.call-update) | async-done | bytes 2097168 | tf_op jit(solution)/shard_map/all_gather | solution.py:32
  276.4 3.8 %multiply_reduce_fusion = f32[512]{0:T(512)S(1)} fusion(bf16[128,16,512]{2,0,1:T(8,128)(2,1)} %all-to-all-done, bf16[2048,512]{1,0:T(8,128)(2,1)} %all-gather.7.cloned.1.call-done, f32[2048]{0:T(1024)S(1)} %bitcast.67, bf16[1,512,512]{2,1,0:T(8,128)(2,1)S(1)} %copy-done.1), kind=kOutput, calls=%fused_computation.8 | convolution fusion | flops 1080032768 | bytes 4728832 | tf_op jit(solution)/shard_map/th,dh->td/dot_general | solution.py:39
  280.2 1.3 broadcast_select_fusion
  281.5 0.1 scatter.9
  281.6 2.9 convert_multiply_fusion.2
  284.5 0.2 pad_maximum_fusion
  284.7 2.0 copy.14
  286.7 1.9 copy.15
  288.6 47.1 %all_to_all.23 = f32[32,16,1152]{2,1,0:T(8,128)S(1)} all-to-all(f32[32,16,1152]{2,1,0:T(8,128)S(1)} %bitcast.61), channel_id=1, replica_groups=mesh['template'=16,'fsdp'=16,'dp'=2] {'template','dp'}, dimensions={0} | all-to-all | bytes 4718592 | tf_op jit(solution)/shard_map/all_to_all | solution.py:48
  335.6 0.1 reduce_sum.32
  335.8 0.1 broadcast_in_dim.2
  335.9 23.4 %all_to_all.24 = f32[16,16,1152]{2,1,0:T(8,128)S(1)} all-to-all(f32[16,16,1152]{2,1,0:T(8,128)S(1)} %broadcast_in_dim.2), channel_id=1, replica_groups=mesh['template'=16,'fsdp'=16,'dp'=2] {'template'}, dimensions={0} | all-to-all | bytes 2359296 | tf_op jit(solution)/shard_map/all_to_all | solution.py:50
  359.3 0.9 slice_divide_fusion
  360.1 0.8 fusion.26
  (4 shorter events, 0.1 us)
Async XLA Ops:
  7.2 201.0 %all-gather.9.cloned.1.call-start = ((), (), s32[]{:S(2)}) async-start(), calls=%async_computation.4 | async-start | bytes 8912896 | tf_op jit(solution)/shard_map/all_gather | solution.py:23
  12.8 16.0 %copy-start.2 = (bf16[1,512]{1,0:T(2,128)(2,1)S(1)}, bf16[1,512]{1,0:T(2,128)(2,1)}, u32[]{:S(2)}) copy-start(bf16[1,512]{1,0:T(2,128)(2,1)} %param.11) | copy-start | bytes 3076
  12.8 149.0 %copy-start = (bf16[1,128,8192]{2,1,0:T(8,128)(2,1)S(1)}, bf16[1,128,8192]{2,1,0:T(8,128)(2,1)}, u32[]{:S(2)}) copy-start(bf16[1,128,8192]{2,1,0:T(8,128)(2,1)} %param.8) | copy-start | bytes 6291460
  12.8 195.4 %copy-start.3 = (bf16[1,128,512]{2,1,0:T(8,128)(2,1)S(1)}, bf16[1,128,512]{2,1,0:T(8,128)(2,1)}, u32[]{:S(2)}) copy-start(bf16[1,128,512]{2,1,0:T(8,128)(2,1)} %param.9) | copy-start | bytes 393220
  12.8 223.3 %all-to-all-start = ((bf16[128,16,512]{2,0,1:T(8,128)(2,1)}), bf16[128,16,512]{2,0,1:T(8,128)(2,1)}, u32[]{:S(2)}, u32[]{:S(2)}) async-start(bf16[128,16,512]{2,0,1:T(8,128)(2,1)} %copy.12), calls=%async_computation | async-start | bytes 4194304 | tf_op jit(solution)/shard_map/all_to_all | solution.py:30
  28.7 247.6 %all-gather.7.cloned.1.call-start = ((), (), s32[]{:S(2)}) async-start(), calls=%async_computation.3 | async-start | bytes 2228224 | tf_op jit(solution)/shard_map/all_gather | solution.py:32
  208.2 5.4 %copy-start.1 = (bf16[1,512,512]{2,1,0:T(8,128)(2,1)S(1)}, bf16[1,512,512]{2,1,0:T(8,128)(2,1)}, u32[]{:S(2)}) copy-start(bf16[1,512,512]{2,1,0:T(8,128)(2,1)} %param.10) | copy-start | bytes 1572868
Sparse Core Ops, SparseCore 0:
  10.1 198.0 all-gather.8
  213.7 62.6 all-gather.6

commit v2 on v1

--- a/solution.py
+++ b/solution.py
@@ -20,8 +20,10 @@
 
     hidden_f = token_batch.astype(jnp.float32)
     ratio = lax.rsqrt(jnp.mean(jnp.square(hidden_f), axis=1, keepdims=True) + 1e-05)
-    w_full = lax.all_gather(w_shard, "fsdp", axis=0, tiled=True)
-    g_full = lax.all_gather(g_shard, "fsdp", axis=0, tiled=True)
+    w_ext = jnp.concatenate([w_shard, g_shard[None, :]], axis=0)
+    gathered = lax.all_gather(w_ext, "fsdp", axis=0, tiled=False)
+    w_full = gathered[:, :rows, :].reshape(-1, heads)
+    g_full = gathered[:, rows, :].reshape(-1)
     xhat = hidden_f * ratio
     normed = (xhat * g_full.astype(jnp.float32)[None, :]).astype(jnp.bfloat16)
     values = jnp.dot(normed, w_full, preferred_element_type=jnp.float32) * scale

time: 368 us -> 378 us (1.027)
  waiting for transfers between devices: 84.6 us -> 218 us
  blocking collectives: 224 us -> 91 us
  local copies, waits for them, and re-layouts: 9.14 us -> 18 us
    all_gather x1, waiting for transfers between devices: 45.9 us -> 180 us  [body(): gathered = lax.all_gather(w_ext, 'fsdp', axis=0, tiled=False)]
    all_gather x1 -> x0, blocking collectives: 133 us -> none  [body(): g_full = lax.all_gather(g_shard, 'fsdp', axis=0, tiled=True)]
    slice x0 -> x1, local copies, waits for them, and re-layouts: none -> 7.35 us  [body(): w_full = gathered[:, :rows, :].reshape(-1, heads)]
  transfers between devices with their start and end apart: 3 -> 3, of which waited for: 2 -> 2; matrix products, arithmetic and copies ran while one was open for 4% -> 6% of each run, Pallas kernels for 0% -> 0%
where the time goes in v2:
time: 378 us
  waiting for transfers between devices  218 us (58%)
  blocking collectives  91 us (24%)
  local copies, waits for them, and re-layouts  18 us (5%)
  starting transfers between devices  15.9 us (4%)
  between operations  14.2 us (4%)
  matrix products  12.1 us (3%)
  other arithmetic  8.28 us (2%)
    all_gather x1, waiting for transfers between devices, body(): gathered = lax.all_gather(w_ext, 'fsdp', axis=0, tiled=False)  180 us
    all_to_all x1, blocking collectives, body(): parts = lax.all_to_all(pack, ('template', 'dp'), 0, 0, tiled=True)  46.6 us
    all_gather x1, waiting for transfers between devices, body(): local_delta = lax.all_gather(delta, 'fsdp', axis=0, tiled=True)  38.6 us
    all_to_all x1, blocking collectives, body(): lax.all_to_all(jnp.broadcast_to(total, (n_t, piece, cols)), 'template', 0...  23.4 us
    all_gather x1, blocking collectives, body(): local_ratio = lax.all_gather(ratio, 'fsdp', axis=0, tiled=True)  21 us
    all_to_all x1, starting transfers between devices, body(): local_hidden = lax.all_to_all(token_batch, 'fsdp', 1, 0, tiled=True)  15.8 us
  transfers between devices with their start and end apart: 3, of which 2 were waited for; matrix products, arithmetic and copies ran while one was open for 6% of the time, Pallas kernels for 0%

profile of v2, /device:TPU:1, one launch (start us, length us, event | category | flops | bytes accessed | tf_op | source)
XLA Modules:
  0.0 377.8 jit_solution(11770526453611650669)
XLA Ops:
  7.2 0.0 copy-start
  7.2 0.0 all-gather.9.cloned.1.call-start
  7.2 1.4 copy.16
  8.6 0.9 copy.17
  9.5 0.1 maximum_bitcast_fusion
  9.5 1.1 copy.18
  10.6 0.0 all-gather.9.cloned.1.call-update
  10.6 0.0 copy-done
  10.6 0.8 copy.21
  11.5 2.5 copy.15
  14.0 15.8 %all-to-all-start = ((bf16[128,16,512]{2,0,1:T(8,128)(2,1)}), bf16[128,16,512]{2,0,1:T(8,128)(2,1)}, u32[]{:S(2)}, u32[]{:S(2)}) async-start(bf16[128,16,512]{2,0,1:T(8,128)(2,1)} %copy.15), calls=%async_computation | async-start | bytes 4194304 | tf_op jit(solution)/shard_map/all_to_all | solution.py:32
  29.8 0.0 all-gather.7.cloned.1.call-start
  29.8 0.5 fusion
  30.3 0.0 copy-start.3
  30.3 179.8 %all-gather.9.cloned.1.call-done = bf16[16,513,512]{2,1,0:T(8,128)(2,1)} async-done(((bf16[1,513,512]{2,1,0:T(8,128)(2,1)}), bf16[16,513,512]{2,1,0:T(8,128)(2,1)}) %all-gather.9.cloned.1.call-update) | async-done | bytes 8405008 | tf_op jit(solution)/shard_map/all_gather | solution.py:24
  210.1 7.3 %slice.54 = bf16[16,512,512]{2,1,0:T(8,128)(2,1)} slice(bf16[16,513,512]{2,1,0:T(8,128)(2,1)} %all-gather.9.cloned.1.call-done), slice={[0:16], [0:512], [0:512]} | slice | bytes 16777216 | tf_op jit(solution)/shard_map/slice | solution.py:25
  217.5 0.9 slice_convert_fusion
  218.4 0.0 copy-done.3
  218.4 0.0 copy-start.2
  218.4 5.4 %fusion.15 = bf16[128,512]{1,0:T(8,128)(2,1)} fusion(bf16[8192,512]{1,0:T(8,128)(2,1)} %bitcast.53, bf16[1,128,8192]{2,1,0:T(8,128)(2,1)S(1)} %copy-done, f32[8192]{0:T(1024)S(1)} %bitcast.61, f32[128]{0:T(128)S(1)} %get-tuple-element.29, bf16[1,128,512]{2,1,0:T(8,128)(2,1)S(1)} %copy-done.3), kind=kOutput, calls=%fused_computation.18 | convolution fusion | flops 1078198272 | bytes 10781184 | tf_op jit(solution)/shard_map/dot_general | solution.py:29
  223.8 0.0 copy-start.1
  223.8 0.0 all-gather.7.cloned.1.call-update
  223.8 0.0 copy-done.2
  223.8 0.6 compare_reduce_fusion
  224.5 0.6 compare_reduce_fusion.1
  225.1 21.0 %all-gather.2 = f32[16,1,128]{2,1,0:T(1,128)S(1)} all-gather(f32[1,1,128]{2,1,0:T(1,128)S(1)} %get-tuple-element.28), channel_id=2, replica_groups=mesh['template'=16,'fsdp'=16,'dp'=2] {'fsdp'}, dimensions={0}, use_global_device_ids=true | all-gather | bytes 8704 | tf_op jit(solution)/shard_map/all_gather | solution.py:33
  246.1 0.0 all-to-all-done
  246.1 2.3 multiply_convert_fusion.1
  248.4 38.6 %all-gather.7.cloned.1.call-done = bf16[2048,512]{1,0:T(8,128)(2,1)} async-done(((bf16[128,512]{1,0:T(8,128)(2,1)}), bf16[2048,512]{1,0:T(8,128)(2,1)}) %all-gather.7.cloned.1.call-update) | async-done | bytes 2097168 | tf_op jit(solution)/shard_map/all_gather | solution.py:34
  287.0 0.0 copy-done.1
  287.0 3.8 %multiply_reduce_fusion = f32[512]{0:T(512)S(1)} fusion(bf16[128,16,512]{2,0,1:T(8,128)(2,1)} %all-to-all-done, bf16[2048,512]{1,0:T(8,128)(2,1)} %all-gather.7.cloned.1.call-done, f32[2048]{0:T(1024)S(1)} %bitcast.60, bf16[1,512,512]{2,1,0:T(8,128)(2,1)S(1)} %copy-done.1), kind=kOutput, calls=%fused_computation.6 | convolution fusion | flops 1080032768 | bytes 4728832 | tf_op jit(solution)/shard_map/th,dh->td/dot_general | solution.py:41
  290.8 1.3 broadcast_select_fusion
  292.1 0.1 scatter.9
  292.2 2.9 convert_multiply_fusion.2
  295.1 0.2 pad_maximum_fusion
  295.3 2.0 copy.19
  297.2 1.9 copy.20
  299.1 46.6 %all_to_all.23 = f32[32,16,1152]{2,1,0:T(8,128)S(1)} all-to-all(f32[32,16,1152]{2,1,0:T(8,128)S(1)} %bitcast.52), channel_id=1, replica_groups=mesh['template'=16,'fsdp'=16,'dp'=2] {'template','dp'}, dimensions={0} | all-to-all | bytes 4718592 | tf_op jit(solution)/shard_map/all_to_all | solution.py:50
  345.8 0.1 reduce_sum.32
  345.9 0.1 broadcast_in_dim.2
  346.0 23.4 %all_to_all.24 = f32[16,16,1152]{2,1,0:T(8,128)S(1)} all-to-all(f32[16,16,1152]{2,1,0:T(8,128)S(1)} %broadcast_in_dim.2), channel_id=1, replica_groups=mesh['template'=16,'fsdp'=16,'dp'=2] {'template'}, dimensions={0} | all-to-all | bytes 2359296 | tf_op jit(solution)/shard_map/all_to_all | solution.py:52
  369.4 0.9 slice_divide_fusion
  370.3 0.8 fusion.19
  (3 shorter events, 0.0 us)
Async XLA Ops:
  7.2 3.5 copy-start
  7.2 203.0 %all-gather.9.cloned.1.call-start = ((), (), s32[]{:S(2)}) async-start(), calls=%async_computation.4 | async-start | bytes 9052160 | tf_op jit(solution)/shard_map/all_gather | solution.py:24
  14.0 232.2 %all-to-all-start = ((bf16[128,16,512]{2,0,1:T(8,128)(2,1)}), bf16[128,16,512]{2,0,1:T(8,128)(2,1)}, u32[]{:S(2)}, u32[]{:S(2)}) async-start(bf16[128,16,512]{2,0,1:T(8,128)(2,1)} %copy.15), calls=%async_computation | async-start | bytes 4194304 | tf_op jit(solution)/shard_map/all_to_all | solution.py:32
  29.8 257.2 %all-gather.7.cloned.1.call-start = ((), (), s32[]{:S(2)}) async-start(), calls=%async_computation.3 | async-start | bytes 2228224 | tf_op jit(solution)/shard_map/all_gather | solution.py:34
  30.3 188.1 %copy-start.3 = (bf16[1,128,512]{2,1,0:T(8,128)(2,1)S(1)}, bf16[1,128,512]{2,1,0:T(8,128)(2,1)}, u32[]{:S(2)}) copy-start(bf16[1,128,512]{2,1,0:T(8,128)(2,1)} %param.9) | copy-start | bytes 393220
  218.4 5.4 %copy-start.2 = (bf16[1,512]{1,0:T(2,128)(2,1)S(1)}, bf16[1,512]{1,0:T(2,128)(2,1)}, u32[]{:S(2)}) copy-start(bf16[1,512]{1,0:T(2,128)(2,1)} %param.11) | copy-start | bytes 3076
  223.8 63.2 %copy-start.1 = (bf16[1,512,512]{2,1,0:T(8,128)(2,1)S(1)}, bf16[1,512,512]{2,1,0:T(8,128)(2,1)}, u32[]{:S(2)}) copy-start(bf16[1,512,512]{2,1,0:T(8,128)(2,1)} %param.10) | copy-start | bytes 1572868
Sparse Core Ops, SparseCore 0:
  10.8 199.3 all-gather.8
  223.9 62.9 all-gather.6

commit v3 on v2

--- a/solution.py
+++ b/solution.py
@@ -20,13 +20,26 @@
 
     hidden_f = token_batch.astype(jnp.float32)
     ratio = lax.rsqrt(jnp.mean(jnp.square(hidden_f), axis=1, keepdims=True) + 1e-05)
-    w_ext = jnp.concatenate([w_shard, g_shard[None, :]], axis=0)
+    swap = [(i, (i + 1) % n_dp) for i in range(n_dp)]
+    other_hidden = lax.ppermute(token_batch, "dp", swap)
+    other_ratio = lax.ppermute(ratio, "dp", swap)
+    half = heads // n_dp
+    dp_at = lax.axis_index("dp")
+    w_cols = lax.dynamic_slice_in_dim(w_shard, dp_at * half, half, 1)
+    w_ext = jnp.concatenate([w_cols, g_shard.reshape(-1, half)], axis=0)
     gathered = lax.all_gather(w_ext, "fsdp", axis=0, tiled=False)
-    w_full = gathered[:, :rows, :].reshape(-1, heads)
-    g_full = gathered[:, rows, :].reshape(-1)
+    w_half = gathered[:, :rows, :].reshape(-1, half)
+    g_full = gathered[:, rows:, :].reshape(-1).astype(jnp.float32)
     xhat = hidden_f * ratio
-    normed = (xhat * g_full.astype(jnp.float32)[None, :]).astype(jnp.bfloat16)
-    values = jnp.dot(normed, w_full, preferred_element_type=jnp.float32) * scale
+    normed = (xhat * g_full[None, :]).astype(jnp.bfloat16)
+    other_normed = (other_hidden.astype(jnp.float32) * other_ratio * g_full[None, :]).astype(jnp.bfloat16)
+    mine_half = jnp.dot(normed, w_half, preferred_element_type=jnp.float32)
+    theirs_half = jnp.dot(other_normed, w_half, preferred_element_type=jnp.float32)
+    from_other = lax.ppermute(theirs_half, "dp", swap)
+    both = jnp.stack([mine_half, from_other])
+    first = jnp.where(dp_at == 0, both[0], both[1])
+    second = jnp.where(dp_at == 0, both[1], both[0])
+    values = jnp.concatenate([first, second], axis=1) * scale
     delta = (values - goal.astype(jnp.float32)).astype(jnp.bfloat16)
 
     local_hidden = lax.all_to_all(token_batch, "fsdp", 1, 0, tiled=True)

time: 378 us -> 344 us (0.910)
  waiting for transfers between devices: 218 us -> 181 us
  starting transfers between devices: 15.9 us -> 24.5 us
  local copies, waits for them, and re-layouts: 18 us -> 12.7 us
    all_gather x1, waiting for transfers between devices: 180 us -> 136 us  [body(): gathered = lax.all_gather(w_ext, 'fsdp', axis=0, tiled=False)]
    ppermute x0 -> x3, starting transfers between devices: none -> 8.54 us  [the longest x1 3.25 us: body(): from_other = lax.ppermute(theirs_half, 'dp', swap)]
    slice x1, local copies, waits for them, and re-layouts: 7.35 us -> 2.46 us  [body(): w_half = gathered[:, :rows, :].reshape(-1, half)]
    all_gather x1, waiting for transfers between devices: 38.6 us -> 43.2 us  [body(): local_delta = lax.all_gather(delta, 'fsdp', axis=0, tiled=True)]
  transfers between devices with their start and end apart: 3 -> 6, of which waited for: 2 -> 3; matrix products, arithmetic and copies ran while one was open for 6% -> 5% of each run, Pallas kernels for 0% -> 0%
where the time goes in v3:
time: 344 us; the launch traced here: 343 us
  waiting for transfers between devices  181 us (53%)
  blocking collectives  90.7 us (26%)
  starting transfers between devices  24.5 us (7%)
  between operations  14.3 us (4%)
  local copies, waits for them, and re-layouts  12.7 us (4%)
  other arithmetic  10.3 us (3%)
  matrix products  9.91 us (3%)
    all_gather x1, waiting for transfers between devices, body(): gathered = lax.all_gather(w_ext, 'fsdp', axis=0, tiled=False)  136 us
    all_to_all x1, blocking collectives, body(): parts = lax.all_to_all(pack, ('template', 'dp'), 0, 0, tiled=True)  46.4 us
    all_gather x1, waiting for transfers between devices, body(): local_delta = lax.all_gather(delta, 'fsdp', axis=0, tiled=True)  43.2 us
    all_to_all x1, blocking collectives, body(): lax.all_to_all(jnp.broadcast_to(total, (n_t, piece, cols)), 'template', 0...  23.4 us
    all_gather x1, blocking collectives, body(): local_ratio = lax.all_gather(ratio, 'fsdp', axis=0, tiled=True)  20.9 us
    all_to_all x1, starting transfers between devices, body(): local_hidden = lax.all_to_all(token_batch, 'fsdp', 1, 0, tiled=True)  15.9 us
  transfers between devices with their start and end apart: 6, of which 3 were waited for; matrix products, arithmetic and copies ran while one was open for 5% of the time, Pallas kernels for 0%

profile of v3, /device:TPU:1, one launch (start us, length us, event | category | flops | bytes accessed | tf_op | source)
XLA Modules:
  0.0 343.1 jit_solution(4625389663575992984)
XLA Ops:
  7.2 0.0 all-gather.9.cloned.1.call-start
  7.2 0.8 fusion.13
  8.0 1.0 dynamic-slice_bitcast_fusion
  9.0 0.7 maximum_bitcast_fusion
  9.7 0.0 all-gather.9.cloned.1.call-update
  9.7 2.4 copy.16
  12.2 2.5 copy.12
  14.7 15.9 %all-to-all-start = ((bf16[128,16,512]{2,0,1:T(8,128)(2,1)}), bf16[128,16,512]{2,0,1:T(8,128)(2,1)}, u32[]{:S(2)}, u32[]{:S(2)}) async-start(bf16[128,16,512]{2,0,1:T(8,128)(2,1)} %copy.12), calls=%async_computation | async-start | bytes 4194304 | tf_op jit(solution)/shard_map/all_to_all | solution.py:45
  30.6 0.0 all-gather.7.cloned.1.call-start
  30.7 0.0 copy-done
  30.7 3.1 collective-permute-start
  33.8 0.5 multiply_reduce_fusion.1
  34.3 2.2 collective-permute-start.1
  36.5 135.6 %all-gather.9.cloned.1.call-done = bf16[16,514,256]{2,1,0:T(8,128)(2,1)} async-done(((bf16[1,514,256]{2,1,0:T(8,128)(2,1)}), bf16[16,514,256]{2,1,0:T(8,128)(2,1)}) %all-gather.9.cloned.1.call-update) | async-done | bytes 4210704 | tf_op jit(solution)/shard_map/all_gather | solution.py:30
  172.1 0.8 convert_bitcast_fusion
  173.0 2.5 slice.54
  175.5 0.0 collective-permute-done.1
  175.5 0.0 collective-permute-done
  175.5 2.4 fusion.3
  177.9 0.0 copy-start.2
  177.9 0.0 copy-start.1
  178.0 3.3 collective-permute-start.2
  181.2 0.8 fusion.1
  182.0 1.8 collective-permute-done.2
  183.8 0.0 copy-done.2
  183.8 0.7 fusion.11
  184.5 0.0 all-gather.7.cloned.1.call-update
  184.6 0.2 copy.13
  184.8 0.6 compare_reduce_fusion
  185.4 0.6 compare_reduce_fusion.1
  186.1 20.9 %all-gather.2 = f32[16,1,128]{2,1,0:T(1,128)S(1)} all-gather(f32[1,1,128]{2,1,0:T(1,128)S(1)} %fusion.18), channel_id=2, replica_groups=mesh['template'=16,'fsdp'=16,'dp'=2] {'fsdp'}, dimensions={0}, use_global_device_ids=true | all-gather | bytes 8704 | tf_op jit(solution)/shard_map/all_gather | solution.py:46
  206.9 0.0 all-to-all-done
  206.9 2.3 multiply_convert_fusion.3
  209.2 0.0 copy-start.3
  209.2 43.2 %all-gather.7.cloned.1.call-done = bf16[2048,512]{1,0:T(8,128)(2,1)} async-done(((bf16[128,512]{1,0:T(8,128)(2,1)}), bf16[2048,512]{1,0:T(8,128)(2,1)}) %all-gather.7.cloned.1.call-update) | async-done | bytes 2097168 | tf_op jit(solution)/shard_map/all_gather | solution.py:47
  252.4 3.8 %multiply_reduce_fusion = f32[512]{0:T(512)S(1)} fusion(bf16[128,16,512]{2,0,1:T(8,128)(2,1)} %all-to-all-done, bf16[2048,512]{1,0:T(8,128)(2,1)} %all-gather.7.cloned.1.call-done, f32[2048]{0:T(1024)S(1)} %bitcast.65, bf16[1,512,512]{2,1,0:T(8,128)(2,1)S(1)} %copy-done.1), kind=kOutput, calls=%fused_computation.1 | convolution fusion | flops 1080032768 | bytes 4728832 | tf_op jit(solution)/shard_map/th,dh->td/dot_general | solution.py:54
  256.3 1.3 broadcast_select_fusion.2
  257.6 0.1 scatter.9
  257.6 2.9 convert_multiply_fusion
  260.5 0.2 pad_maximum_fusion
  260.7 2.0 copy.14
  262.7 1.9 copy.15
  264.6 46.4 %all_to_all.23 = f32[32,16,1152]{2,1,0:T(8,128)S(1)} all-to-all(f32[32,16,1152]{2,1,0:T(8,128)S(1)} %bitcast.56), channel_id=1, replica_groups=mesh['template'=16,'fsdp'=16,'dp'=2] {'template','dp'}, dimensions={0} | all-to-all | bytes 4718592 | tf_op jit(solution)/shard_map/all_to_all | solution.py:63
  311.0 0.1 reduce_sum.32
  311.1 0.1 broadcast_in_dim.2
  311.2 23.4 %all_to_all.24 = f32[16,16,1152]{2,1,0:T(8,128)S(1)} all-to-all(f32[16,16,1152]{2,1,0:T(8,128)S(1)} %broadcast_in_dim.2), channel_id=1, replica_groups=mesh['template'=16,'fsdp'=16,'dp'=2] {'template'}, dimensions={0} | all-to-all | bytes 2359296 | tf_op jit(solution)/shard_map/all_to_all | solution.py:65
  334.6 0.9 slice_divide_fusion
  335.5 0.8 fusion.12
  (10 shorter events, 0.1 us)
Async XLA Ops:
  7.2 164.9 %all-gather.9.cloned.1.call-start = ((), (), s32[]{:S(2)}) async-start(), calls=%async_computation.4 | async-start | bytes 4526080 | tf_op jit(solution)/shard_map/all_gather | solution.py:30
  14.7 16.0 %copy-start = (bf16[1,128,8192]{2,1,0:T(8,128)(2,1)S(1)}, bf16[1,128,8192]{2,1,0:T(8,128)(2,1)}, u32[]{:S(2)}) copy-start(bf16[1,128,8192]{2,1,0:T(8,128)(2,1)} %param.8) | copy-start | bytes 6291460
  14.7 192.3 %all-to-all-start = ((bf16[128,16,512]{2,0,1:T(8,128)(2,1)}), bf16[128,16,512]{2,0,1:T(8,128)(2,1)}, u32[]{:S(2)}, u32[]{:S(2)}) async-start(bf16[128,16,512]{2,0,1:T(8,128)(2,1)} %copy.12), calls=%async_computation | async-start | bytes 4194304 | tf_op jit(solution)/shard_map/all_to_all | solution.py:45
  30.6 221.8 %all-gather.7.cloned.1.call-start = ((), (), s32[]{:S(2)}) async-start(), calls=%async_computation.3 | async-start | bytes 2228224 | tf_op jit(solution)/shard_map/all_gather | solution.py:47
  30.7 144.8 %collective-permute-start = (bf16[128,8192]{1,0:T(8,128)(2,1)S(1)}, bf16[128,8192]{1,0:T(8,128)(2,1)}, u32[]{:S(2)}, u32[]{:S(2)}) collective-permute-start(bf16[128,8192]{1,0:T(8,128)(2,1)S(1)} %bitcast.58), channel_id=1, source_target_pairs={{0,1},{1,0},{2,3},{3,2},{4,5},{5,4},{6,7},{7,6},{8,9},{9,8},{10,11... | collective-permute-start | bytes 6291464 | tf_op jit(solution)/shard_map/ppermute | solution.py:24
  34.3 141.2 %collective-permute-start.1 = (f32[128,1]{0,1:T(1,128)S(1)}, f32[128,1]{0,1:T(1,128)S(1)}, u32[]{:S(2)}, u32[]{:S(2)}) collective-permute-start(f32[128,1]{0,1:T(1,128)S(1)} %fusion.19), channel_id=1, source_target_pairs={{0,1},{1,0},{2,3},{3,2},{4,5},{5,4},{6,7},{7,6},{8,9},{9,8},{10,11... | collective-permute-start | bytes 1544 | tf_op jit(solution)/shard_map/ppermute | solution.py:25
  177.9 5.9 %copy-start.2 = (bf16[1,128,512]{2,1,0:T(8,128)(2,1)S(1)}, bf16[1,128,512]{2,1,0:T(8,128)(2,1)}, u32[]{:S(2)}) copy-start(bf16[1,128,512]{2,1,0:T(8,128)(2,1)} %param.9) | copy-start | bytes 393220
  177.9 6.6 %copy-start.1 = (bf16[1,512,512]{2,1,0:T(8,128)(2,1)S(1)}, bf16[1,512,512]{2,1,0:T(8,128)(2,1)}, u32[]{:S(2)}) copy-start(bf16[1,512,512]{2,1,0:T(8,128)(2,1)} %param.10) | copy-start | bytes 1572868
  178.0 5.8 %collective-permute-start.2 = (f32[128,256]{1,0:T(8,128)S(1)}, f32[128,256]{1,0:T(8,128)S(1)}, u32[]{:S(2)}, u32[]{:S(2)}) collective-permute-start(f32[128,256]{1,0:T(8,128)S(1)} %fusion.3), channel_id=1, source_target_pairs={{0,1},{1,0},{2,3},{3,2},{4,5},{5,4},{6,7},{7,6},{8,9},{9,8},{10,11... | collective-permute-start | bytes 393224 | tf_op jit(solution)/shard_map/ppermute | solution.py:38
  209.2 47.1 %copy-start.3 = (bf16[1,512]{1,0:T(2,128)(2,1)S(1)}, bf16[1,512]{1,0:T(2,128)(2,1)}, u32[]{:S(2)}) copy-start(bf16[1,512]{1,0:T(2,128)(2,1)} %param.11) | copy-start | bytes 3076
Sparse Core Ops, SparseCore 0:
  10.7 161.4 all-gather.8
  184.7 67.7 all-gather.6

commit v4 on v3

--- a/solution.py
+++ b/solution.py
@@ -44,28 +44,39 @@
 
     local_hidden = lax.all_to_all(token_batch, "fsdp", 1, 0, tiled=True)
     local_ratio = lax.all_gather(ratio, "fsdp", axis=0, tiled=True)
-    local_delta = lax.all_gather(delta, "fsdp", axis=0, tiled=True)
     local_xhat = local_hidden.astype(jnp.float32) * local_ratio
     g_f = g_shard.astype(jnp.float32)
     local_normed = (local_xhat * g_f[None, :]).astype(jnp.bfloat16)
     sq_normed = jnp.square(local_normed.astype(jnp.float32)).astype(jnp.bfloat16)
-    sq_delta = jnp.square(local_delta.astype(jnp.float32)).astype(jnp.bfloat16)
-    fisher = jnp.einsum("td,th->dh", sq_normed, sq_delta, preferred_element_type=jnp.float32)
+    w_f = w_shard.astype(jnp.float32)
+    piece = rows // (n_t * n_dp)
+
+    def reduce_rows(pack):
+        cols = pack.shape[1]
+        pack = pack.reshape(n_dp, n_t, piece, cols).transpose(1, 0, 2, 3).reshape(n_t * n_dp, piece, cols)
+        parts = lax.all_to_all(pack, ("template", "dp"), 0, 0, tiled=True)
+        total = jnp.sum(parts, axis=0, keepdims=True)
+        spread = lax.all_to_all(jnp.broadcast_to(total, (n_t, piece, cols)), "template", 0, 0, tiled=True)
+        return spread.reshape(n_t * piece, cols)
+
+    delta_a = lax.all_gather(delta[:, :half], "fsdp", axis=0, tiled=True)
+    delta_b = lax.all_gather(delta[:, half:], "fsdp", axis=0, tiled=True)
+    sq_a = jnp.square(delta_a.astype(jnp.float32)).astype(jnp.bfloat16)
+    fisher_a = jnp.einsum("td,th->dh", sq_normed, sq_a, preferred_element_type=jnp.float32)
+    full_a = reduce_rows(jnp.concatenate([fisher_a * w_f[:, :half], fisher_a], axis=1))
+    full_a, sq_normed, local_xhat = lax.optimization_barrier((full_a, sq_normed, local_xhat))
+    sq_b = jnp.square(delta_b.astype(jnp.float32)).astype(jnp.bfloat16)
+    fisher_b = jnp.einsum("td,th->dh", sq_normed, sq_b, preferred_element_type=jnp.float32)
+    local_delta = jnp.concatenate([delta_a, delta_b], axis=1)
     back = jnp.einsum("th,dh->td", local_delta, w_shard, preferred_element_type=jnp.float32) * scale
     gain_info = jnp.sum(jnp.square(back * local_xhat), axis=0)
-
     extra = jnp.zeros((rows, 128), jnp.float32)
     extra = extra.at[:, 0].set(gain_info * g_f).at[:, 1].set(gain_info)
-    pack = jnp.concatenate([fisher * w_shard.astype(jnp.float32), fisher, extra], axis=1)
-    cols = pack.shape[1]
-    piece = rows // (n_t * n_dp)
-    pack = pack.reshape(n_dp, n_t, piece, cols).transpose(1, 0, 2, 3).reshape(n_t * n_dp, piece, cols)
-    parts = lax.all_to_all(pack, ("template", "dp"), 0, 0, tiled=True)
-    total = jnp.sum(parts, axis=0, keepdims=True)
-    spread = lax.all_to_all(jnp.broadcast_to(total, (n_t, piece, cols)), "template", 0, 0, tiled=True)
-    full = spread.reshape(n_t * piece, cols)
-    merged = full[:, :heads] / full[:, heads : 2 * heads]
-    merged_gain = full[:, 2 * heads] / full[:, 2 * heads + 1]
+    full_b = reduce_rows(jnp.concatenate([fisher_b * w_f[:, half:], fisher_b, extra], axis=1))
+    merged = jnp.concatenate(
+        [full_a[:, :half] / full_a[:, half:], full_b[:, :half] / full_b[:, half : 2 * half]], axis=1
+    )
+    merged_gain = full_b[:, 2 * half] / full_b[:, 2 * half + 1]
     return merged, merged_gain
 
 

time: 344 us -> 392 us (1.14)
  waiting for transfers between devices: 181 us -> 215 us
  starting transfers between devices: 24.5 us -> 35.3 us
    all_to_all x0 -> x2, waiting for transfers between devices: none -> 22.7 us  [reduce_rows(): lax.all_to_all(jnp.broadcast_to(total, (n_t, piece, cols)), 'template', 0...]
    all_gather x1 -> x2, waiting for transfers between devices: 43.2 us -> 55.2 us  [the longest x1 38.1 us: body(): delta_a = lax.all_gather(delta[:, :half], 'fsdp', axis=0, tiled=True)]
    all_to_all x0 -> x2, starting transfers between devices: none -> 10.7 us  [reduce_rows(): lax.all_to_all(jnp.broadcast_to(total, (n_t, piece, cols)), 'template', 0...]
  transfers between devices with their start and end apart: 6 -> 9, of which waited for: 3 -> 6; matrix products, arithmetic and copies ran while one was open for 5% -> 6% of each run, Pallas kernels for 0% -> 0%
where the time goes in v4:
time: 392 us; the launch traced here: 391 us
  waiting for transfers between devices  215 us (55%)
  blocking collectives  89.3 us (23%)
  starting transfers between devices  35.3 us (9%)
  between operations  14 us (4%)
  other arithmetic  13 us (3%)
  local copies, waits for them, and re-layouts  12.1 us (3%)
  matrix products  11.7 us (3%)
    all_gather x1, waiting for transfers between devices, body(): gathered = lax.all_gather(w_ext, 'fsdp', axis=0, tiled=False)  136 us
    all_to_all x2, blocking collectives, reduce_rows(): parts = lax.all_to_all(pack, ('template', 'dp'), 0, 0, tiled=True)  68.5 us
    all_gather x1, waiting for transfers between devices, body(): delta_a = lax.all_gather(delta[:, :half], 'fsdp', axis=0, tiled=True)  38.1 us
    all_to_all x2, waiting for transfers between devices, reduce_rows(): lax.all_to_all(jnp.broadcast_to(total, (n_t, piece, cols)), 'template', 0...  22.7 us
    all_gather x1, blocking collectives, body(): local_ratio = lax.all_gather(ratio, 'fsdp', axis=0, tiled=True)  20.9 us
    all_gather x1, waiting for transfers between devices, body(): delta_b = lax.all_gather(delta[:, half:], 'fsdp', axis=0, tiled=True)  17.1 us
    all_to_all x1, starting transfers between devices, body(): local_hidden = lax.all_to_all(token_batch, 'fsdp', 1, 0, tiled=True)  15.9 us
    all_to_all x2, starting transfers between devices, reduce_rows(): lax.all_to_all(jnp.broadcast_to(total, (n_t, piece, cols)), 'template', 0...  10.7 us
  transfers between devices with their start and end apart: 9, of which 6 were waited for; matrix products, arithmetic and copies ran while one was open for 6% of the time, Pallas kernels for 0%

profile of v4, /device:TPU:1, one launch (start us, length us, event | category | flops | bytes accessed | tf_op | source)
XLA Modules:
  0.0 390.8 jit_solution(16930532056720308684)
XLA Ops:
  7.2 0.8 fusion.19
  8.0 1.0 dynamic-slice_bitcast_fusion
  9.0 0.7 maximum_bitcast_fusion
  9.7 2.4 copy.20
  12.2 2.5 copy.14
  14.7 15.9 %all-to-all-start = ((bf16[128,16,512]{2,0,1:T(8,128)(2,1)}), bf16[128,16,512]{2,0,1:T(8,128)(2,1)}, u32[]{:S(2)}, u32[]{:S(2)}) async-start(bf16[128,16,512]{2,0,1:T(8,128)(2,1)} %copy.14), calls=%async_computation | async-start | bytes 4194304 | tf_op jit(solution)/shard_map/all_to_all | solution.py:45
  30.7 3.1 collective-permute-start
  33.8 0.5 multiply_reduce_fusion.1
  34.3 2.2 collective-permute-start.1
  36.5 135.6 %all-gather.12.cloned.1.call-done = bf16[16,514,256]{2,1,0:T(8,128)(2,1)} async-done(((bf16[1,514,256]{2,1,0:T(8,128)(2,1)}), bf16[16,514,256]{2,1,0:T(8,128)(2,1)}) %all-gather.12.cloned.1.call-update) | async-done | bytes 4210704 | tf_op jit(solution)/shard_map/all_gather | solution.py:30
  172.1 0.8 convert_bitcast_fusion
  173.0 2.5 slice.78
  175.5 2.4 fusion.3
  178.0 3.3 collective-permute-start.2
  181.2 0.8 fusion.1
  182.1 1.7 collective-permute-done.2
  183.9 0.7 fusion.18
  184.6 0.2 copy.15
  184.8 20.9 %all-gather.2 = f32[16,1,128]{2,1,0:T(1,128)S(1)} all-gather(f32[1,1,128]{2,1,0:T(1,128)S(1)} %fusion.25), channel_id=2, replica_groups=mesh['template'=16,'fsdp'=16,'dp'=2] {'fsdp'}, dimensions={0}, use_global_device_ids=true | all-gather | bytes 8704 | tf_op jit(solution)/shard_map/all_gather | solution.py:46
  205.7 1.2 bitcast_convert_fusion
  206.9 4.2 %bitcast_multiply_fusion = (f32[2048,512]{1,0:T(8,128)}, bf16[2048,512]{1,0:T(8,128)(2,1)S(1)}) fusion(f32[2048]{0:T(1024)S(1)} %bitcast.70, bf16[128,16,512]{2,0,1:T(8,128)(2,1)} %all-to-all-done, f32[512]{0:T(512)S(1)} %bitcast.71), kind=kLoop, calls=%fused_computation | loop fusion | flops 7340032 | bytes 8398848 | tf_op jit(solution)/shard_map/mul | solution.py:47
  211.1 38.1 %all-gather.8.cloned.1.call-done = bf16[2048,256]{1,0:T(8,128)(2,1)} async-done(((bf16[128,256]{1,0:T(8,128)(2,1)}), bf16[2048,256]{1,0:T(8,128)(2,1)}) %all-gather.8.cloned.1.call-update) | async-done | bytes 1048592 | tf_op jit(solution)/shard_map/all_gather | solution.py:62
  249.3 2.1 slice_multiply_fusion.1
  251.4 0.1 pad_maximum_fusion.1
  251.5 0.3 copy.16
  251.8 0.1 copy.17
  251.9 32.3 %all_to_all.33 = f32[32,16,512]{2,1,0:T(8,128)S(1)} all-to-all(f32[32,16,512]{2,1,0:T(8,128)S(1)} %bitcast.64), channel_id=1, replica_groups=mesh['template'=16,'fsdp'=16,'dp'=2] {'template','dp'}, dimensions={0} | all-to-all | bytes 2097152 | tf_op jit(solution)/shard_map/all_to_all | solution.py:57
  284.2 0.1 reduce_sum.39
  284.3 0.9 broadcast_in_dim.4
  285.2 6.1 %all-to-all-start.2 = ((f32[16,16,512]{2,1,0:T(8,128)}), f32[16,16,512]{2,1,0:T(8,128)S(1)}, u32[]{:S(2)}, u32[]{:S(2)}) async-start(f32[16,16,512]{2,1,0:T(8,128)} %broadcast_in_dim.4), calls=%async_computation.2 | async-start | bytes 1048576 | tf_op jit(solution)/shard_map/all_to_all | solution.py:59
  291.2 0.6 compare_reduce_fusion
  291.9 0.7 compare_reduce_fusion.1
  292.6 10.0 %all-to-all-done.2 = f32[16,16,512]{2,1,0:T(8,128)S(1)} async-done(((f32[16,16,512]{2,1,0:T(8,128)}), f32[16,16,512]{2,1,0:T(8,128)S(1)}, u32[]{:S(2)}, u32[]{:S(2)}) %all-to-all-start.2) | async-done | bytes 524320 | tf_op jit(solution)/shard_map/all_to_all | solution.py:59
  302.5 17.1 %all-gather.10.cloned.1.call-done = bf16[2048,256]{1,0:T(8,128)(2,1)} async-done(((bf16[128,256]{1,0:T(8,128)(2,1)}), bf16[2048,256]{1,0:T(8,128)(2,1)}) %all-gather.10.cloned.1.call-update) | async-done | bytes 1048592 | tf_op jit(solution)/shard_map/all_gather | solution.py:63
  319.7 4.2 %multiply_reduce_fusion = f32[512]{0:T(512)S(1)} fusion(f32[2048,512]{1,0:T(8,128)} %get-tuple-element.31, bf16[2048,256]{1,0:T(8,128)(2,1)} %all-gather.10.cloned.1.call-done, bf16[2048,256]{1,0:T(8,128)(2,1)} %all-gather.8.cloned.1.call-done, bf16[1,512,512]{2,1,0:T(8,128)(2,1)S(1)} %copy-done.3), kind=kOutput, calls=%fused_computation.1 | convolution fusion | flops 1082129920 | bytes 6817792 | tf_op jit(solution)/shard_map/th,dh->td/dot_general | solution.py:71
  323.9 1.3 broadcast_select_fusion.2
  325.2 0.1 scatter.9
  325.3 2.1 slice_multiply_fusion
  327.4 0.1 pad_maximum_fusion
  327.6 0.4 copy.18
  328.0 0.1 copy.19
  328.1 36.1 %all_to_all.34 = f32[32,16,640]{2,1,0:T(8,128)S(1)} all-to-all(f32[32,16,640]{2,1,0:T(8,128)S(1)} %bitcast.60), channel_id=1, replica_groups=mesh['template'=16,'fsdp'=16,'dp'=2] {'template','dp'}, dimensions={0} | all-to-all | bytes 2621440 | tf_op jit(solution)/shard_map/all_to_all | solution.py:57
  364.2 0.1 reduce_sum.42
  364.3 0.9 broadcast_in_dim.5
  365.2 4.6 %all-to-all-start.4 = ((f32[16,16,640]{2,1,0:T(8,128)}), f32[16,16,640]{2,1,0:T(8,128)S(1)}, u32[]{:S(2)}, u32[]{:S(2)}) async-start(f32[16,16,640]{2,1,0:T(8,128)} %broadcast_in_dim.5), calls=%async_computation.4 | async-start | bytes 1310720 | tf_op jit(solution)/shard_map/all_to_all | solution.py:59
  369.8 12.7 %all-to-all-done.4 = f32[16,16,640]{2,1,0:T(8,128)S(1)} async-done(((f32[16,16,640]{2,1,0:T(8,128)}), f32[16,16,640]{2,1,0:T(8,128)S(1)}, u32[]{:S(2)}, u32[]{:S(2)}) %all-to-all-start.4) | async-done | bytes 655392 | tf_op jit(solution)/shard_map/all_to_all | solution.py:59
  382.6 0.8 fusion.16
  383.4 0.9 pad_maximum_fusion.2
  (31 shorter events, 0.4 us)
Async XLA Ops:
  7.2 164.9 %all-gather.12.cloned.1.call-start = ((), (), s32[]{:S(2)}) async-start(), calls=%async_computation.7 | async-start | bytes 4526080 | tf_op jit(solution)/shard_map/all_gather | solution.py:30
  14.7 16.0 %copy-start = (bf16[1,128,8192]{2,1,0:T(8,128)(2,1)S(1)}, bf16[1,128,8192]{2,1,0:T(8,128)(2,1)}, u32[]{:S(2)}) copy-start(bf16[1,128,8192]{2,1,0:T(8,128)(2,1)} %param.8) | copy-start | bytes 6291460
  14.7 192.2 %all-to-all-start = ((bf16[128,16,512]{2,0,1:T(8,128)(2,1)}), bf16[128,16,512]{2,0,1:T(8,128)(2,1)}, u32[]{:S(2)}, u32[]{:S(2)}) async-start(bf16[128,16,512]{2,0,1:T(8,128)(2,1)} %copy.14), calls=%async_computation | async-start | bytes 4194304 | tf_op jit(solution)/shard_map/all_to_all | solution.py:45
  30.6 218.6 %all-gather.8.cloned.1.call-start = ((), (), s32[]{:S(2)}) async-start(), calls=%async_computation.5 | async-start | bytes 1114112 | tf_op jit(solution)/shard_map/all_gather | solution.py:62
  30.7 144.8 %collective-permute-start = (bf16[128,8192]{1,0:T(8,128)(2,1)S(1)}, bf16[128,8192]{1,0:T(8,128)(2,1)}, u32[]{:S(2)}, u32[]{:S(2)}) collective-permute-start(bf16[128,8192]{1,0:T(8,128)(2,1)S(1)} %bitcast.57), channel_id=1, source_target_pairs={{0,1},{1,0},{2,3},{3,2},{4,5},{5,4},{6,7},{7,6},{8,9},{9,8},{10,11... | collective-permute-start | bytes 6291464 | tf_op jit(solution)/shard_map/ppermute | solution.py:24
  34.3 141.2 %collective-permute-start.1 = (f32[128,1]{0,1:T(1,128)S(1)}, f32[128,1]{0,1:T(1,128)S(1)}, u32[]{:S(2)}, u32[]{:S(2)}) collective-permute-start(f32[128,1]{0,1:T(1,128)S(1)} %fusion.24), channel_id=1, source_target_pairs={{0,1},{1,0},{2,3},{3,2},{4,5},{5,4},{6,7},{7,6},{8,9},{9,8},{10,11... | collective-permute-start | bytes 1544 | tf_op jit(solution)/shard_map/ppermute | solution.py:25
  177.9 5.9 %copy-start.4 = (bf16[1,128,512]{2,1,0:T(8,128)(2,1)S(1)}, bf16[1,128,512]{2,1,0:T(8,128)(2,1)}, u32[]{:S(2)}) copy-start(bf16[1,128,512]{2,1,0:T(8,128)(2,1)} %param.9) | copy-start | bytes 393220
  177.9 6.7 %copy-start.3 = (bf16[1,512,512]{2,1,0:T(8,128)(2,1)S(1)}, bf16[1,512,512]{2,1,0:T(8,128)(2,1)}, u32[]{:S(2)}) copy-start(bf16[1,512,512]{2,1,0:T(8,128)(2,1)} %param.10) | copy-start | bytes 1572868
  178.0 5.8 %collective-permute-start.2 = (f32[128,256]{1,0:T(8,128)S(1)}, f32[128,256]{1,0:T(8,128)S(1)}, u32[]{:S(2)}, u32[]{:S(2)}) collective-permute-start(f32[128,256]{1,0:T(8,128)S(1)} %fusion.3), channel_id=1, source_target_pairs={{0,1},{1,0},{2,3},{3,2},{4,5},{5,4},{6,7},{7,6},{8,9},{9,8},{10,11... | collective-permute-start | bytes 393224 | tf_op jit(solution)/shard_map/ppermute | solution.py:38
  184.6 135.1 %all-gather.10.cloned.1.call-start = ((), (), s32[]{:S(2)}) async-start(), calls=%async_computation.6 | async-start | bytes 1114112 | tf_op jit(solution)/shard_map/all_gather | solution.py:63
  211.1 40.2 %copy-start.1 = (bf16[2048,512]{1,0:T(8,128)(2,1)}, bf16[2048,512]{1,0:T(8,128)(2,1)S(1)}, u32[]{:S(2)}) copy-start(bf16[2048,512]{1,0:T(8,128)(2,1)S(1)} %get-tuple-element.30) | copy-start | bytes 6291460
  285.2 17.4 %all-to-all-start.2 = ((f32[16,16,512]{2,1,0:T(8,128)}), f32[16,16,512]{2,1,0:T(8,128)S(1)}, u32[]{:S(2)}, u32[]{:S(2)}) async-start(f32[16,16,512]{2,1,0:T(8,128)} %broadcast_in_dim.4), calls=%async_computation.2 | async-start | bytes 1048576 | tf_op jit(solution)/shard_map/all_to_all | solution.py:59
  302.5 21.3 %copy-start.5 = (bf16[1,512]{1,0:T(2,128)(2,1)S(1)}, bf16[1,512]{1,0:T(2,128)(2,1)}, u32[]{:S(2)}) copy-start(bf16[1,512]{1,0:T(2,128)(2,1)} %param.11) | copy-start | bytes 3076
  302.5 22.8 %copy-start.2 = (bf16[2048,512]{1,0:T(8,128)(2,1)S(1)}, bf16[2048,512]{1,0:T(8,128)(2,1)}, u32[]{:S(2)}) copy-start(bf16[2048,512]{1,0:T(8,128)(2,1)} %copy-done.1) | copy-start | bytes 6291460
  365.2 17.4 %all-to-all-start.4 = ((f32[16,16,640]{2,1,0:T(8,128)}), f32[16,16,640]{2,1,0:T(8,128)S(1)}, u32[]{:S(2)}, u32[]{:S(2)}) async-start(f32[16,16,640]{2,1,0:T(8,128)} %broadcast_in_dim.5), calls=%async_computation.4 | async-start | bytes 1310720 | tf_op jit(solution)/shard_map/all_to_all | solution.py:59
Sparse Core Ops, SparseCore 0:
  10.7 161.4 all-gather.11
  184.7 64.5 all-gather.7
  251.3 68.2 all-gather.9

commit v5 on v3

--- a/solution.py
+++ b/solution.py
@@ -42,7 +42,8 @@
     values = jnp.concatenate([first, second], axis=1) * scale
     delta = (values - goal.astype(jnp.float32)).astype(jnp.bfloat16)
 
-    local_hidden = lax.all_to_all(token_batch, "fsdp", 1, 0, tiled=True)
+    late_batch, _ = lax.optimization_barrier((token_batch, delta))
+    local_hidden = lax.all_to_all(late_batch, "fsdp", 1, 0, tiled=True)
     local_ratio = lax.all_gather(ratio, "fsdp", axis=0, tiled=True)
     local_delta = lax.all_gather(delta, "fsdp", axis=0, tiled=True)
     local_xhat = local_hidden.astype(jnp.float32) * local_ratio

time: 344 us -> 321 us (0.933)
  waiting for transfers between devices: 181 us -> 72.3 us
  blocking collectives: 90.7 us -> 189 us
  starting transfers between devices: 24.5 us -> 15.1 us
    all_gather x1, blocking collectives: 20.9 us -> 121 us  [body(): local_ratio = lax.all_gather(ratio, 'fsdp', axis=0, tiled=True)]
    all_gather x1, waiting for transfers between devices: 136 us -> 68.9 us  [body(): gathered = lax.all_gather(w_ext, 'fsdp', axis=0, tiled=False)]
    all_gather x1, waiting for transfers between devices: 43.2 us -> 0.71 us  [body(): local_delta = lax.all_gather(delta, 'fsdp', axis=0, tiled=True)]
    all_to_all x1, starting transfers between devices: 15.9 us -> 6.16 us  [body(): local_hidden = lax.all_to_all(late_batch, 'fsdp', 1, 0, tiled=True)]
  transfers between devices with their start and end apart: 6 -> 6, of which waited for: 3 -> 3; matrix products, arithmetic and copies ran while one was open for 5% -> 2% of each run, Pallas kernels for 0% -> 0%
where the time goes in v5:
time: 321 us
  blocking collectives  189 us (59%)
  waiting for transfers between devices  72.3 us (23%)
  starting transfers between devices  15.1 us (5%)
  between operations  14.3 us (4%)
  local copies, waits for them, and re-layouts  11.5 us (4%)
  other arithmetic  10.4 us (3%)
  matrix products  7.94 us (2%)
    all_gather x1, blocking collectives, body(): local_ratio = lax.all_gather(ratio, 'fsdp', axis=0, tiled=True)  121 us
    all_gather x1, waiting for transfers between devices, body(): gathered = lax.all_gather(w_ext, 'fsdp', axis=0, tiled=False)  68.9 us
    all_to_all x1, blocking collectives, body(): parts = lax.all_to_all(pack, ('template', 'dp'), 0, 0, tiled=True)  44.8 us
    all_to_all x1, blocking collectives, body(): lax.all_to_all(jnp.broadcast_to(total, (n_t, piece, cols)), 'template', 0...  23.4 us
  transfers between devices with their start and end apart: 6, of which 3 were waited for; matrix products, arithmetic and copies ran while one was open for 2% of the time, Pallas kernels for 0%

profile of v5, /device:TPU:1, one launch (start us, length us, event | category | flops | bytes accessed | tf_op | source)
XLA Modules:
  0.0 320.8 jit_solution(162053636718987232)
XLA Ops:
  7.2 0.0 all-gather.9.cloned.1.call-start
  7.2 0.8 fusion.13
  8.0 1.0 dynamic-slice_bitcast_fusion
  9.0 0.7 maximum_bitcast_fusion
  9.7 0.0 all-gather.9.cloned.1.call-update
  9.7 4.0 %collective-permute-start = (bf16[128,8192]{1,0:T(8,128)(2,1)}, bf16[128,8192]{1,0:T(8,128)(2,1)S(1)}, u32[]{:S(2)}, u32[]{:S(2)}) collective-permute-start(bf16[128,8192]{1,0:T(8,128)(2,1)} %bitcast.58), channel_id=1, source_target_pairs={{0,1},{1,0},{2,3},{3,2},{4,5},{5,4},{6,7},{7,6},{8,9},{9,8},{10,11... | collective-permute-start | bytes 6291464 | tf_op jit(solution)/shard_map/ppermute | solution.py:24
  13.7 2.1 multiply_reduce_fusion.1
  15.8 1.9 collective-permute-start.1
  17.7 68.9 %all-gather.9.cloned.1.call-done = bf16[16,514,256]{2,1,0:T(8,128)(2,1)} async-done(((bf16[1,514,256]{2,1,0:T(8,128)(2,1)}), bf16[16,514,256]{2,1,0:T(8,128)(2,1)}) %all-gather.9.cloned.1.call-update) | async-done | bytes 4210704 | tf_op jit(solution)/shard_map/all_gather | solution.py:30
  86.7 0.8 convert_bitcast_fusion
  87.5 2.5 slice.54
  90.0 0.0 collective-permute-done.1
  90.0 0.0 collective-permute-done
  90.0 0.0 copy-start.5
  90.0 1.3 copy-done.5
  91.4 2.6 fusion.3
  94.0 0.0 copy-start.2
  94.0 3.0 collective-permute-start.2
  97.0 0.0 copy-done
  97.0 0.9 fusion.1
  97.9 2.0 collective-permute-done.2
  99.9 0.7 fusion.11
  100.6 1.5 copy.19
  102.1 6.2 %all-to-all-start = ((bf16[128,16,512]{2,0,1:T(8,128)(2,1)}), bf16[128,16,512]{2,0,1:T(8,128)(2,1)S(1)}, u32[]{:S(2)}, u32[]{:S(2)}) async-start(bf16[128,16,512]{2,0,1:T(8,128)(2,1)} %bitcast.60), calls=%async_computation | async-start | bytes 4194304 | tf_op jit(solution)/shard_map/all_to_all | solution.py:46
  108.3 0.0 all-gather.7.cloned.1.call-start
  108.3 0.7 all-gather.7.cloned.1.call-update
  109.0 0.2 copy.13
  109.3 0.6 compare_reduce_fusion
  109.9 0.7 compare_reduce_fusion.1
  110.6 121.1 %all-gather.3 = f32[16,1,128]{2,1,0:T(1,128)S(1)} all-gather(f32[1,1,128]{2,1,0:T(1,128)S(1)} %fusion.18), channel_id=3, replica_groups=mesh['template'=16,'fsdp'=16,'dp'=2] {'fsdp'}, dimensions={0}, use_global_device_ids=true | all-gather | bytes 8704 | tf_op jit(solution)/shard_map/all_gather | solution.py:47
  231.6 0.7 all-gather.7.cloned.1.call-done
  232.4 0.0 all-to-all-done
  232.4 3.2 multiply_reduce_fusion
  235.6 1.3 broadcast_select_fusion.2
  236.9 0.1 scatter.9
  236.9 0.0 copy-start.4
  236.9 0.7 multiply_convert_fusion.1
  237.6 0.9 copy-done.4
  238.5 1.3 convert_multiply_fusion
  239.8 0.2 pad_maximum_fusion
  240.0 2.0 copy.14
  242.0 1.9 copy.15
  243.9 44.8 %all_to_all.23 = f32[32,16,1152]{2,1,0:T(8,128)S(1)} all-to-all(f32[32,16,1152]{2,1,0:T(8,128)S(1)} %bitcast.57), channel_id=1, replica_groups=mesh['template'=16,'fsdp'=16,'dp'=2] {'template','dp'}, dimensions={0} | all-to-all | bytes 4718592 | tf_op jit(solution)/shard_map/all_to_all | solution.py:64
  288.7 0.1 reduce_sum.32
  288.8 0.1 broadcast_in_dim.2
  288.9 23.4 %all_to_all.24 = f32[16,16,1152]{2,1,0:T(8,128)S(1)} all-to-all(f32[16,16,1152]{2,1,0:T(8,128)S(1)} %broadcast_in_dim.2), channel_id=1, replica_groups=mesh['template'=16,'fsdp'=16,'dp'=2] {'template'}, dimensions={0} | all-to-all | bytes 2359296 | tf_op jit(solution)/shard_map/all_to_all | solution.py:66
  312.3 0.9 slice_divide_fusion
  313.2 0.8 fusion.12
  (13 shorter events, 0.1 us)
Async XLA Ops:
  7.2 79.5 %all-gather.9.cloned.1.call-start = ((), (), s32[]{:S(2)}) async-start(), calls=%async_computation.4 | async-start | bytes 4526080 | tf_op jit(solution)/shard_map/all_gather | solution.py:30
  9.7 80.3 %collective-permute-start = (bf16[128,8192]{1,0:T(8,128)(2,1)}, bf16[128,8192]{1,0:T(8,128)(2,1)S(1)}, u32[]{:S(2)}, u32[]{:S(2)}) collective-permute-start(bf16[128,8192]{1,0:T(8,128)(2,1)} %bitcast.58), channel_id=1, source_target_pairs={{0,1},{1,0},{2,3},{3,2},{4,5},{5,4},{6,7},{7,6},{8,9},{9,8},{10,11... | collective-permute-start | bytes 6291464 | tf_op jit(solution)/shard_map/ppermute | solution.py:24
  15.8 74.2 %collective-permute-start.1 = (f32[128,1]{0,1:T(1,128)S(1)}, f32[128,1]{0,1:T(1,128)S(1)}, u32[]{:S(2)}, u32[]{:S(2)}) collective-permute-start(f32[128,1]{0,1:T(1,128)S(1)} %fusion.19), channel_id=1, source_target_pairs={{0,1},{1,0},{2,3},{3,2},{4,5},{5,4},{6,7},{7,6},{8,9},{9,8},{10,11... | collective-permute-start | bytes 1544 | tf_op jit(solution)/shard_map/ppermute | solution.py:25
  90.0 1.3 copy-start.5
  91.4 5.6 %copy-start = (bf16[1,128,8192]{2,1,0:T(8,128)(2,1)S(1)}, bf16[1,128,8192]{2,1,0:T(8,128)(2,1)}, u32[]{:S(2)}) copy-start(bf16[1,128,8192]{2,1,0:T(8,128)(2,1)} %param.8) | copy-start | bytes 6291460
  94.0 5.9 %copy-start.2 = (bf16[1,128,512]{2,1,0:T(8,128)(2,1)S(1)}, bf16[1,128,512]{2,1,0:T(8,128)(2,1)}, u32[]{:S(2)}) copy-start(bf16[1,128,512]{2,1,0:T(8,128)(2,1)} %param.9) | copy-start | bytes 393220
  94.0 5.8 %collective-permute-start.2 = (f32[128,256]{1,0:T(8,128)S(1)}, f32[128,256]{1,0:T(8,128)S(1)}, u32[]{:S(2)}, u32[]{:S(2)}) collective-permute-start(f32[128,256]{1,0:T(8,128)S(1)} %fusion.3), channel_id=1, source_target_pairs={{0,1},{1,0},{2,3},{3,2},{4,5},{5,4},{6,7},{7,6},{8,9},{9,8},{10,11... | collective-permute-start | bytes 393224 | tf_op jit(solution)/shard_map/ppermute | solution.py:38
  102.1 6.9 %copy-start.1 = (bf16[1,512,512]{2,1,0:T(8,128)(2,1)S(1)}, bf16[1,512,512]{2,1,0:T(8,128)(2,1)}, u32[]{:S(2)}) copy-start(bf16[1,512,512]{2,1,0:T(8,128)(2,1)} %param.10) | copy-start | bytes 1572868
  102.1 130.3 %all-to-all-start = ((bf16[128,16,512]{2,0,1:T(8,128)(2,1)}), bf16[128,16,512]{2,0,1:T(8,128)(2,1)S(1)}, u32[]{:S(2)}, u32[]{:S(2)}) async-start(bf16[128,16,512]{2,0,1:T(8,128)(2,1)} %bitcast.60), calls=%async_computation | async-start | bytes 4194304 | tf_op jit(solution)/shard_map/all_to_all | solution.py:46
  108.3 124.1 %all-gather.7.cloned.1.call-start = ((), (), s32[]{:S(2)}) async-start(), calls=%async_computation.3 | async-start | bytes 2228224 | tf_op jit(solution)/shard_map/all_gather | solution.py:48
  232.4 3.2 %copy-start.3 = (bf16[1,512]{1,0:T(2,128)(2,1)S(1)}, bf16[1,512]{1,0:T(2,128)(2,1)}, u32[]{:S(2)}) copy-start(bf16[1,512]{1,0:T(2,128)(2,1)} %param.11) | copy-start | bytes 3076
  236.9 1.6 copy-start.4
Sparse Core Ops, SparseCore 0:
  10.7 75.9 all-gather.8
  111.8 120.5 all-gather.6

commit v6 on v5

--- a/solution.py
+++ b/solution.py
@@ -42,7 +42,7 @@
     values = jnp.concatenate([first, second], axis=1) * scale
     delta = (values - goal.astype(jnp.float32)).astype(jnp.bfloat16)
 
-    late_batch, _ = lax.optimization_barrier((token_batch, delta))
+    late_batch, _, _ = lax.optimization_barrier((token_batch, mine_half, other_hidden))
     local_hidden = lax.all_to_all(late_batch, "fsdp", 1, 0, tiled=True)
     local_ratio = lax.all_gather(ratio, "fsdp", axis=0, tiled=True)
     local_delta = lax.all_gather(delta, "fsdp", axis=0, tiled=True)

time: 321 us -> 314 us (0.978)
  blocking collectives: 189 us -> 172 us
  waiting for transfers between devices: 72.3 us -> 80.2 us
    all_gather x1, blocking collectives: 121 us -> 105 us  [body(): local_ratio = lax.all_gather(ratio, 'fsdp', axis=0, tiled=True)]
    all_gather x1, waiting for transfers between devices: 0.71 us -> 5.54 us  [body(): local_delta = lax.all_gather(delta, 'fsdp', axis=0, tiled=True)]
  transfers between devices with their start and end apart: 6 -> 6, of which waited for: 3 -> 4; matrix products, arithmetic and copies ran while one was open for 2% -> 4% of each run, Pallas kernels for 0% -> 0%
where the time goes in v6:
time: 314 us
  blocking collectives  172 us (55%)
  waiting for transfers between devices  80.2 us (26%)
  starting transfers between devices  16.3 us (5%)
  between operations  14.3 us (5%)
  local copies, waits for them, and re-layouts  11.9 us (4%)
  other arithmetic  10.4 us (3%)
  matrix products  8.9 us (3%)
    all_gather x1, blocking collectives, body(): local_ratio = lax.all_gather(ratio, 'fsdp', axis=0, tiled=True)  105 us
    all_gather x1, waiting for transfers between devices, body(): gathered = lax.all_gather(w_ext, 'fsdp', axis=0, tiled=False)  70.9 us
    all_to_all x1, blocking collectives, body(): parts = lax.all_to_all(pack, ('template', 'dp'), 0, 0, tiled=True)  43.2 us
    all_to_all x1, blocking collectives, body(): lax.all_to_all(jnp.broadcast_to(total, (n_t, piece, cols)), 'template', 0...  23.4 us
  transfers between devices with their start and end apart: 6, of which 4 were waited for; matrix products, arithmetic and copies ran while one was open for 4% of the time, Pallas kernels for 0%

profile of v6, /device:TPU:1, one launch (start us, length us, event | category | flops | bytes accessed | tf_op | source)
XLA Modules:
  0.0 313.6 jit_solution(10359301670653984660)
XLA Ops:
  7.2 0.0 all-gather.9.cloned.1.call-start
  7.2 0.8 fusion.13
  8.0 1.0 dynamic-slice_bitcast_fusion
  9.0 0.7 maximum_bitcast_fusion
  9.7 0.0 all-gather.9.cloned.1.call-update
  9.7 4.0 %collective-permute-start = (bf16[128,8192]{1,0:T(8,128)(2,1)}, bf16[128,8192]{1,0:T(8,128)(2,1)S(1)}, u32[]{:S(2)}, u32[]{:S(2)}) collective-permute-start(bf16[128,8192]{1,0:T(8,128)(2,1)} %bitcast.58), channel_id=1, source_target_pairs={{0,1},{1,0},{2,3},{3,2},{4,5},{5,4},{6,7},{7,6},{8,9},{9,8},{10,11... | collective-permute-start | bytes 6291464 | tf_op jit(solution)/shard_map/ppermute | solution.py:24
  13.7 2.1 multiply_reduce_fusion.1
  15.8 70.9 %all-gather.9.cloned.1.call-done = bf16[16,514,256]{2,1,0:T(8,128)(2,1)} async-done(((bf16[1,514,256]{2,1,0:T(8,128)(2,1)}), bf16[16,514,256]{2,1,0:T(8,128)(2,1)}) %all-gather.9.cloned.1.call-update) | async-done | bytes 4210704 | tf_op jit(solution)/shard_map/all_gather | solution.py:30
  86.7 0.8 convert_bitcast_fusion
  87.5 0.0 copy-start
  87.6 2.6 slice.54
  90.2 0.2 copy-done
  90.4 0.8 fusion.1
  91.2 0.9 copy-done.1
  92.1 0.0 collective-permute-done
  92.1 1.7 copy.19
  93.8 0.3 copy-done.6
  94.1 6.0 %all-to-all-start = ((bf16[128,16,512]{2,0,1:T(8,128)(2,1)}), bf16[128,16,512]{2,0,1:T(8,128)(2,1)S(1)}, u32[]{:S(2)}, u32[]{:S(2)}) async-start(bf16[128,16,512]{2,0,1:T(8,128)(2,1)} %bitcast.60), calls=%async_computation | async-start | bytes 4194304 | tf_op jit(solution)/shard_map/all_to_all | solution.py:46
  100.1 0.0 all-gather.7.cloned.1.call-start
  100.2 3.1 collective-permute-start.1
  103.3 1.2 collective-permute-done.1
  104.5 3.6 %fusion.3 = f32[128,256]{1,0:T(8,128)S(1)} fusion(bf16[8192,256]{1,0:T(8,128)(2,1)} %bitcast.64, bf16[128,8192]{1,0:T(8,128)(2,1)} %copy-done.6, f32[8192]{0:T(1024)S(1)} %bitcast.68, f32[128]{0:T(128)S(1)} %bitcast.71), kind=kOutput, calls=%fused_computation.11 | convolution fusion | flops 541065216 | bytes 6455808 | tf_op jit(solution)/shard_map/dot_general | solution.py:37
  108.1 3.1 collective-permute-start.2
  111.2 2.6 collective-permute-done.2
  113.9 0.7 fusion.11
  114.6 0.0 all-gather.7.cloned.1.call-update
  114.6 0.0 copy-done.2
  114.6 0.2 copy.13
  114.8 0.6 compare_reduce_fusion.1
  115.5 0.6 compare_reduce_fusion
  116.1 105.2 %all-gather.3 = f32[16,1,128]{2,1,0:T(1,128)S(1)} all-gather(f32[1,1,128]{2,1,0:T(1,128)S(1)} %fusion.18), channel_id=3, replica_groups=mesh['template'=16,'fsdp'=16,'dp'=2] {'fsdp'}, dimensions={0}, use_global_device_ids=true | all-gather | bytes 8704 | tf_op jit(solution)/shard_map/all_gather | solution.py:47
  221.3 5.5 %all-gather.7.cloned.1.call-done = bf16[2048,512]{1,0:T(8,128)(2,1)} async-done(((bf16[128,512]{1,0:T(8,128)(2,1)}), bf16[2048,512]{1,0:T(8,128)(2,1)}) %all-gather.7.cloned.1.call-update) | async-done | bytes 2097168 | tf_op jit(solution)/shard_map/all_gather | solution.py:48
  226.8 0.0 all-to-all-done
  226.8 3.2 %multiply_reduce_fusion = f32[512]{0:T(512)S(1)} fusion(bf16[128,16,512]{2,0,1:T(8,128)(2,1)S(1)} %all-to-all-done, bf16[2048,512]{1,0:T(8,128)(2,1)} %all-gather.7.cloned.1.call-done, f32[2048]{0:T(1024)S(1)} %bitcast.65, bf16[1,512,512]{2,1,0:T(8,128)(2,1)S(1)} %copy-done.2), kind=kOutput, calls=%fused_computation.1 | convolution fusion | flops 1080032768 | bytes 4728832 | tf_op jit(solution)/shard_map/th,dh->td/dot_general | solution.py:55
  230.0 1.3 broadcast_select_fusion.2
  231.3 0.1 scatter.9
  231.4 0.7 multiply_convert_fusion.2
  232.1 0.9 copy-done.5
  233.0 1.3 convert_multiply_fusion
  234.3 0.2 pad_maximum_fusion
  234.5 2.0 copy.14
  236.5 1.9 copy.15
  238.4 43.2 %all_to_all.23 = f32[32,16,1152]{2,1,0:T(8,128)S(1)} all-to-all(f32[32,16,1152]{2,1,0:T(8,128)S(1)} %bitcast.57), channel_id=1, replica_groups=mesh['template'=16,'fsdp'=16,'dp'=2] {'template','dp'}, dimensions={0} | all-to-all | bytes 4718592 | tf_op jit(solution)/shard_map/all_to_all | solution.py:64
  281.6 0.1 reduce_sum.32
  281.7 0.1 broadcast_in_dim.2
  281.8 23.4 %all_to_all.24 = f32[16,16,1152]{2,1,0:T(8,128)S(1)} all-to-all(f32[16,16,1152]{2,1,0:T(8,128)S(1)} %broadcast_in_dim.2), channel_id=1, replica_groups=mesh['template'=16,'fsdp'=16,'dp'=2] {'template'}, dimensions={0} | all-to-all | bytes 2359296 | tf_op jit(solution)/shard_map/all_to_all | solution.py:66
  305.2 0.8 fusion.12
  305.9 0.9 slice_divide_fusion
  (15 shorter events, 0.1 us)
Async XLA Ops:
  7.2 79.5 %all-gather.9.cloned.1.call-start = ((), (), s32[]{:S(2)}) async-start(), calls=%async_computation.4 | async-start | bytes 4526080 | tf_op jit(solution)/shard_map/all_gather | solution.py:30
  9.7 82.4 %collective-permute-start = (bf16[128,8192]{1,0:T(8,128)(2,1)}, bf16[128,8192]{1,0:T(8,128)(2,1)S(1)}, u32[]{:S(2)}, u32[]{:S(2)}) collective-permute-start(bf16[128,8192]{1,0:T(8,128)(2,1)} %bitcast.58), channel_id=1, source_target_pairs={{0,1},{1,0},{2,3},{3,2},{4,5},{5,4},{6,7},{7,6},{8,9},{9,8},{10,11... | collective-permute-start | bytes 6291464 | tf_op jit(solution)/shard_map/ppermute | solution.py:24
  87.5 2.9 copy-start
  90.2 1.9 copy-start.1
  92.1 2.0 copy-start.6
  94.1 132.7 %all-to-all-start = ((bf16[128,16,512]{2,0,1:T(8,128)(2,1)}), bf16[128,16,512]{2,0,1:T(8,128)(2,1)S(1)}, u32[]{:S(2)}, u32[]{:S(2)}) async-start(bf16[128,16,512]{2,0,1:T(8,128)(2,1)} %bitcast.60), calls=%async_computation | async-start | bytes 4194304 | tf_op jit(solution)/shard_map/all_to_all | solution.py:46
  100.1 126.7 %all-gather.7.cloned.1.call-start = ((), (), s32[]{:S(2)}) async-start(), calls=%async_computation.3 | async-start | bytes 2228224 | tf_op jit(solution)/shard_map/all_gather | solution.py:48
  100.2 4.3 %collective-permute-start.1 = (f32[128,1]{0,1:T(1,128)S(1)}, f32[128,1]{0,1:T(1,128)S(1)}, u32[]{:S(2)}, u32[]{:S(2)}) collective-permute-start(f32[128,1]{0,1:T(1,128)S(1)} %fusion.19), channel_id=1, source_target_pairs={{0,1},{1,0},{2,3},{3,2},{4,5},{5,4},{6,7},{7,6},{8,9},{9,8},{10,11... | collective-permute-start | bytes 1544 | tf_op jit(solution)/shard_map/ppermute | solution.py:25
  104.5 9.4 %copy-start.3 = (bf16[1,128,512]{2,1,0:T(8,128)(2,1)S(1)}, bf16[1,128,512]{2,1,0:T(8,128)(2,1)}, u32[]{:S(2)}) copy-start(bf16[1,128,512]{2,1,0:T(8,128)(2,1)} %param.9) | copy-start | bytes 393220
  104.5 10.1 %copy-start.2 = (bf16[1,512,512]{2,1,0:T(8,128)(2,1)S(1)}, bf16[1,512,512]{2,1,0:T(8,128)(2,1)}, u32[]{:S(2)}) copy-start(bf16[1,512,512]{2,1,0:T(8,128)(2,1)} %param.10) | copy-start | bytes 1572868
  108.1 5.7 %collective-permute-start.2 = (f32[128,256]{1,0:T(8,128)S(1)}, f32[128,256]{1,0:T(8,128)S(1)}, u32[]{:S(2)}, u32[]{:S(2)}) collective-permute-start(f32[128,256]{1,0:T(8,128)S(1)} %fusion.3), channel_id=1, source_target_pairs={{0,1},{1,0},{2,3},{3,2},{4,5},{5,4},{6,7},{7,6},{8,9},{9,8},{10,11... | collective-permute-start | bytes 393224 | tf_op jit(solution)/shard_map/ppermute | solution.py:38
  226.8 3.2 %copy-start.4 = (bf16[1,512]{1,0:T(2,128)(2,1)S(1)}, bf16[1,512]{1,0:T(2,128)(2,1)}, u32[]{:S(2)}) copy-start(bf16[1,512]{1,0:T(2,128)(2,1)} %param.11) | copy-start | bytes 3076
  231.4 1.6 copy-start.5
Sparse Core Ops, SparseCore 0:
  10.7 75.9 all-gather.8
  114.7 112.0 all-gather.6

commit v7 on v6

--- a/solution.py
+++ b/solution.py
@@ -22,7 +22,8 @@
     ratio = lax.rsqrt(jnp.mean(jnp.square(hidden_f), axis=1, keepdims=True) + 1e-05)
     swap = [(i, (i + 1) % n_dp) for i in range(n_dp)]
     other_hidden = lax.ppermute(token_batch, "dp", swap)
-    other_ratio = lax.ppermute(ratio, "dp", swap)
+    other_f = other_hidden.astype(jnp.float32)
+    other_ratio = lax.rsqrt(jnp.mean(jnp.square(other_f), axis=1, keepdims=True) + 1e-05)
     half = heads // n_dp
     dp_at = lax.axis_index("dp")
     w_cols = lax.dynamic_slice_in_dim(w_shard, dp_at * half, half, 1)
@@ -32,7 +33,7 @@
     g_full = gathered[:, rows:, :].reshape(-1).astype(jnp.float32)
     xhat = hidden_f * ratio
     normed = (xhat * g_full[None, :]).astype(jnp.bfloat16)
-    other_normed = (other_hidden.astype(jnp.float32) * other_ratio * g_full[None, :]).astype(jnp.bfloat16)
+    other_normed = (other_f * other_ratio * g_full[None, :]).astype(jnp.bfloat16)
     mine_half = jnp.dot(normed, w_half, preferred_element_type=jnp.float32)
     theirs_half = jnp.dot(other_normed, w_half, preferred_element_type=jnp.float32)
     from_other = lax.ppermute(theirs_half, "dp", swap)
@@ -42,7 +43,7 @@
     values = jnp.concatenate([first, second], axis=1) * scale
     delta = (values - goal.astype(jnp.float32)).astype(jnp.bfloat16)
 
-    late_batch, _, _ = lax.optimization_barrier((token_batch, mine_half, other_hidden))
+    late_batch, _, _ = lax.optimization_barrier((token_batch, mine_half, other_normed))
     local_hidden = lax.all_to_all(late_batch, "fsdp", 1, 0, tiled=True)
     local_ratio = lax.all_gather(ratio, "fsdp", axis=0, tiled=True)
     local_delta = lax.all_gather(delta, "fsdp", axis=0, tiled=True)
@@ -60,8 +61,8 @@
     pack = jnp.concatenate([fisher * w_shard.astype(jnp.float32), fisher, extra], axis=1)
     cols = pack.shape[1]
     piece = rows // (n_t * n_dp)
-    pack = pack.reshape(n_dp, n_t, piece, cols).transpose(1, 0, 2, 3).reshape(n_t * n_dp, piece, cols)
-    parts = lax.all_to_all(pack, ("template", "dp"), 0, 0, tiled=True)
+    pack = pack.reshape(n_t * n_dp, piece, cols)
+    parts = lax.all_to_all(pack, ("dp", "template"), 0, 0, tiled=True)
     total = jnp.sum(parts, axis=0, keepdims=True)
     spread = lax.all_to_all(jnp.broadcast_to(total, (n_t, piece, cols)), "template", 0, 0, tiled=True)
     full = spread.reshape(n_t * piece, cols)

time: 314 us -> 314 us (level)
  waiting for transfers between devices: 80.2 us -> 74.1 us
  blocking collectives: 172 us -> 177 us
    all_gather x1, waiting for transfers between devices: 70.9 us -> 30.5 us  [body(): gathered = lax.all_gather(w_ext, 'fsdp', axis=0, tiled=False)]
    ppermute x1, waiting for transfers between devices: 0.01 us -> 38.5 us  [body(): other_hidden = lax.ppermute(token_batch, 'dp', swap)]
    all_gather x1, blocking collectives: 105 us -> 112 us  [body(): local_ratio = lax.all_gather(ratio, 'fsdp', axis=0, tiled=True)]
    all_gather x1, waiting for transfers between devices: 5.54 us -> 2.37 us  [body(): local_delta = lax.all_gather(delta, 'fsdp', axis=0, tiled=True)]
  transfers between devices with their start and end apart: 6 -> 5, of which waited for: 4 -> 4; matrix products, arithmetic and copies ran while one was open for 4% -> 2% of each run, Pallas kernels for 0% -> 0%
where the time goes in v7:
time: 314 us; the launch traced here: 313 us
  blocking collectives  177 us (56%)
  waiting for transfers between devices  74.1 us (24%)
  between operations  14.2 us (5%)
  starting transfers between devices  13.2 us (4%)
  other arithmetic  13 us (4%)
  local copies, waits for them, and re-layouts  11.2 us (4%)
  matrix products  10.4 us (3%)
    all_gather x1, blocking collectives, body(): local_ratio = lax.all_gather(ratio, 'fsdp', axis=0, tiled=True)  112 us
    all_to_all x1, blocking collectives, body(): parts = lax.all_to_all(pack, ('dp', 'template'), 0, 0, tiled=True)  43.3 us
    ppermute x1, waiting for transfers between devices, body(): other_hidden = lax.ppermute(token_batch, 'dp', swap)  38.5 us
    all_gather x1, waiting for transfers between devices, body(): gathered = lax.all_gather(w_ext, 'fsdp', axis=0, tiled=False)  30.5 us
    all_to_all x1, blocking collectives, body(): lax.all_to_all(jnp.broadcast_to(total, (n_t, piece, cols)), 'template', 0...  22.2 us
  transfers between devices with their start and end apart: 5, of which 4 were waited for; matrix products, arithmetic and copies ran while one was open for 2% of the time, Pallas kernels for 0%

profile of v7, /device:TPU:1, one launch (start us, length us, event | category | flops | bytes accessed | tf_op | source)
XLA Modules:
  0.0 313.3 jit_solution(14249763848364139519)
XLA Ops:
  7.2 0.0 all-gather.9.cloned.1.call-start
  7.2 0.8 fusion.14
  8.0 1.0 dynamic-slice_bitcast_fusion
  9.0 0.7 maximum_bitcast_fusion
  9.7 0.0 all-gather.9.cloned.1.call-update
  9.7 4.0 %collective-permute-start = (bf16[128,8192]{1,0:T(8,128)(2,1)}, bf16[128,8192]{1,0:T(8,128)(2,1)S(1)}, u32[]{:S(2)}, u32[]{:S(2)}) collective-permute-start(bf16[128,8192]{1,0:T(8,128)(2,1)} %bitcast.54), channel_id=1, source_target_pairs={{0,1},{1,0},{2,3},{3,2},{4,5},{5,4},{6,7},{7,6},{8,9},{9,8},{10,11... | collective-permute-start | bytes 6291464 | tf_op jit(solution)/shard_map/ppermute | solution.py:24
  13.7 2.1 multiply_reduce_fusion.1
  15.8 38.5 %collective-permute-done = bf16[128,8192]{1,0:T(8,128)(2,1)S(1)} collective-permute-done((bf16[128,8192]{1,0:T(8,128)(2,1)}, bf16[128,8192]{1,0:T(8,128)(2,1)S(1)}, u32[]{:S(2)}, u32[]{:S(2)}) %collective-permute-start) | collective-permute-done | bytes 2097184 | tf_op jit(solution)/shard_map/ppermute | solution.py:24
  54.3 1.3 copy-done.2
  55.6 0.5 fusion
  56.1 30.5 %all-gather.9.cloned.1.call-done = bf16[16,514,256]{2,1,0:T(8,128)(2,1)} async-done(((bf16[1,514,256]{2,1,0:T(8,128)(2,1)}), bf16[16,514,256]{2,1,0:T(8,128)(2,1)}) %all-gather.9.cloned.1.call-update) | async-done | bytes 4210704 | tf_op jit(solution)/shard_map/all_gather | solution.py:31
  86.7 0.8 convert_bitcast_fusion
  87.5 0.0 copy-start.1
  87.6 2.6 slice.54
  90.2 0.2 copy-done.1
  90.4 0.8 fusion.4
  91.2 1.0 copy-done
  92.2 1.1 copy-done.3
  93.3 0.6 fusion.2
  93.9 1.6 copy.17
  95.4 6.1 %all-to-all-start = ((bf16[128,16,512]{2,0,1:T(8,128)(2,1)}), bf16[128,16,512]{2,0,1:T(8,128)(2,1)}, u32[]{:S(2)}, u32[]{:S(2)}) async-start(bf16[128,16,512]{2,0,1:T(8,128)(2,1)} %bitcast.56), calls=%async_computation | async-start | bytes 4194304 | tf_op jit(solution)/shard_map/all_to_all | solution.py:47
  101.5 0.0 copy-start.5
  101.5 0.0 copy-start.4
  101.6 0.0 all-gather.7.cloned.1.call-start
  101.6 3.0 fusion.15
  104.6 3.1 collective-permute-start.1
  107.7 2.6 collective-permute-done.1
  110.3 0.7 fusion.11
  111.0 0.0 all-gather.7.cloned.1.call-update
  111.0 0.2 copy.12
  111.3 0.6 compare_reduce_fusion.1
  111.9 0.6 compare_reduce_fusion
  112.5 111.6 %all-gather.3 = f32[16,1,128]{2,1,0:T(1,128)S(1)} all-gather(f32[1,1,128]{2,1,0:T(1,128)S(1)} %get-tuple-element.34), channel_id=3, replica_groups=mesh['template'=16,'fsdp'=16,'dp'=2] {'fsdp'}, dimensions={0}, use_global_device_ids=true | all-gather | bytes 8704 | tf_op jit(solution)/shard_map/all_gather | solution.py:48
  224.1 2.4 all-gather.7.cloned.1.call-done
  226.5 0.0 all-to-all-done
  226.5 3.8 %multiply_reduce_fusion = f32[512]{0:T(512)S(1)} fusion(bf16[128,16,512]{2,0,1:T(8,128)(2,1)} %all-to-all-done, bf16[2048,512]{1,0:T(8,128)(2,1)} %all-gather.7.cloned.1.call-done, f32[2048]{0:T(1024)S(1)} %bitcast.61, bf16[1,512,512]{2,1,0:T(8,128)(2,1)S(1)} %copy-done.4), kind=kOutput, calls=%fused_computation.6 | convolution fusion | flops 1080032768 | bytes 4728832 | tf_op jit(solution)/shard_map/th,dh->td/dot_general | solution.py:56
  230.4 1.3 broadcast_select_fusion.2
  231.7 0.1 scatter.9
  231.7 2.3 multiply_convert_fusion.1
  234.0 2.9 convert_multiply_fusion.2
  236.9 0.2 pad_maximum_fusion
  237.1 2.0 copy.13
  239.1 43.3 %all_to_all.23 = f32[32,16,1152]{2,1,0:T(8,128)S(1)} all-to-all(f32[32,16,1152]{2,1,0:T(8,128)} %bitcast.53), channel_id=1, replica_groups=mesh['template'=16,'fsdp'=16,'dp'=2] {'dp','template'}, dimensions={0} | all-to-all | bytes 4718592 | tf_op jit(solution)/shard_map/all_to_all | solution.py:65
  282.4 0.1 reduce_sum.42
  282.5 0.1 broadcast_in_dim.2
  282.6 22.2 %all_to_all.24 = f32[16,16,1152]{2,1,0:T(8,128)S(1)} all-to-all(f32[16,16,1152]{2,1,0:T(8,128)S(1)} %broadcast_in_dim.2), channel_id=1, replica_groups=mesh['template'=16,'fsdp'=16,'dp'=2] {'template'}, dimensions={0} | all-to-all | bytes 2359296 | tf_op jit(solution)/shard_map/all_to_all | solution.py:67
  304.8 0.8 fusion.12
  305.6 0.9 slice_divide_fusion
  (13 shorter events, 0.1 us)
Async XLA Ops:
  7.2 79.5 %all-gather.9.cloned.1.call-start = ((), (), s32[]{:S(2)}) async-start(), calls=%async_computation.4 | async-start | bytes 4526080 | tf_op jit(solution)/shard_map/all_gather | solution.py:31
  9.7 44.6 %collective-permute-start = (bf16[128,8192]{1,0:T(8,128)(2,1)}, bf16[128,8192]{1,0:T(8,128)(2,1)S(1)}, u32[]{:S(2)}, u32[]{:S(2)}) collective-permute-start(bf16[128,8192]{1,0:T(8,128)(2,1)} %bitcast.54), channel_id=1, source_target_pairs={{0,1},{1,0},{2,3},{3,2},{4,5},{5,4},{6,7},{7,6},{8,9},{9,8},{10,11... | collective-permute-start | bytes 6291464 | tf_op jit(solution)/shard_map/ppermute | solution.py:24
  54.3 1.3 copy-start.2
  87.5 2.9 copy-start.1
  90.2 2.0 copy-start
  90.4 2.9 copy-start.3
  95.4 131.1 %all-to-all-start = ((bf16[128,16,512]{2,0,1:T(8,128)(2,1)}), bf16[128,16,512]{2,0,1:T(8,128)(2,1)}, u32[]{:S(2)}, u32[]{:S(2)}) async-start(bf16[128,16,512]{2,0,1:T(8,128)(2,1)} %bitcast.56), calls=%async_computation | async-start | bytes 4194304 | tf_op jit(solution)/shard_map/all_to_all | solution.py:47
  101.5 8.8 %copy-start.5 = (bf16[1,128,512]{2,1,0:T(8,128)(2,1)S(1)}, bf16[1,128,512]{2,1,0:T(8,128)(2,1)}, u32[]{:S(2)}) copy-start(bf16[1,128,512]{2,1,0:T(8,128)(2,1)} %param.9) | copy-start | bytes 393220
  101.5 9.5 %copy-start.4 = (bf16[1,512,512]{2,1,0:T(8,128)(2,1)S(1)}, bf16[1,512,512]{2,1,0:T(8,128)(2,1)}, u32[]{:S(2)}) copy-start(bf16[1,512,512]{2,1,0:T(8,128)(2,1)} %param.10) | copy-start | bytes 1572868
  101.6 125.0 %all-gather.7.cloned.1.call-start = ((), (), s32[]{:S(2)}) async-start(), calls=%async_computation.3 | async-start | bytes 2228224 | tf_op jit(solution)/shard_map/all_gather | solution.py:49
  104.6 5.7 %collective-permute-start.1 = (f32[128,256]{1,0:T(8,128)S(1)}, f32[128,256]{1,0:T(8,128)S(1)}, u32[]{:S(2)}, u32[]{:S(2)}) collective-permute-start(f32[128,256]{1,0:T(8,128)S(1)} %fusion.15), channel_id=1, source_target_pairs={{0,1},{1,0},{2,3},{3,2},{4,5},{5,4},{6,7},{7,6},{8,9},{9,8},{10,11... | collective-permute-start | bytes 393224 | tf_op jit(solution)/shard_map/ppermute | solution.py:39
  226.5 3.8 %copy-start.6 = (bf16[1,512]{1,0:T(2,128)(2,1)S(1)}, bf16[1,512]{1,0:T(2,128)(2,1)}, u32[]{:S(2)}) copy-start(bf16[1,512]{1,0:T(2,128)(2,1)} %param.11) | copy-start | bytes 3076
Sparse Core Ops, SparseCore 0:
  10.7 75.9 all-gather.8
  111.2 115.3 all-gather.6

commit v8 on v7

--- a/solution.py
+++ b/solution.py
@@ -63,11 +63,13 @@
     piece = rows // (n_t * n_dp)
     pack = pack.reshape(n_t * n_dp, piece, cols)
     parts = lax.all_to_all(pack, ("dp", "template"), 0, 0, tiled=True)
-    total = jnp.sum(parts, axis=0, keepdims=True)
-    spread = lax.all_to_all(jnp.broadcast_to(total, (n_t, piece, cols)), "template", 0, 0, tiled=True)
-    full = spread.reshape(n_t * piece, cols)
-    merged = full[:, :heads] / full[:, heads : 2 * heads]
-    merged_gain = full[:, 2 * heads] / full[:, 2 * heads + 1]
+    total = jnp.sum(parts, axis=0)
+    ratio_block = jnp.zeros((piece, 128), jnp.float32).at[:, 0].set(total[:, 2 * heads] / total[:, 2 * heads + 1])
+    done = jnp.concatenate([total[:, :heads] / total[:, heads : 2 * heads], ratio_block], axis=1)
+    spread = lax.all_to_all(jnp.broadcast_to(done[None], (n_t,) + done.shape), "template", 0, 0, tiled=True)
+    full = spread.reshape(n_t * piece, done.shape[1])
+    merged = full[:, :heads]
+    merged_gain = full[:, heads]
     return merged, merged_gain
 
 

time: 314 us -> 309 us (0.984)
  blocking collectives: 177 us -> 171 us
    all_to_all x1, blocking collectives: 22.2 us -> 16.6 us  [body(): lax.all_to_all(jnp.broadcast_to(done[None], (n_t,) + done.shape), 'templa...]
  transfers between devices with their start and end apart: 5 -> 5, of which waited for: 4 -> 4; matrix products, arithmetic and copies ran while one was open for 2% -> 3% of each run, Pallas kernels for 0% -> 0%
where the time goes in v8:
time: 309 us; the launch traced here: 308 us
  blocking collectives  171 us (55%)
  waiting for transfers between devices  74.3 us (24%)
  between operations  14.3 us (5%)
  starting transfers between devices  13.2 us (4%)
  local copies, waits for them, and re-layouts  12.8 us (4%)
  other arithmetic  12 us (4%)
  matrix products  10.4 us (3%)
    all_gather x1, blocking collectives, body(): local_ratio = lax.all_gather(ratio, 'fsdp', axis=0, tiled=True)  111 us
    all_to_all x1, blocking collectives, body(): parts = lax.all_to_all(pack, ('dp', 'template'), 0, 0, tiled=True)  43.2 us
    ppermute x1, waiting for transfers between devices, body(): other_hidden = lax.ppermute(token_batch, 'dp', swap)  38.5 us
    all_gather x1, waiting for transfers between devices, body(): gathered = lax.all_gather(w_ext, 'fsdp', axis=0, tiled=False)  30.5 us
    all_to_all x1, blocking collectives, body(): lax.all_to_all(jnp.broadcast_to(done[None], (n_t,) + done.shape), 'templa...  16.6 us
  transfers between devices with their start and end apart: 5, of which 4 were waited for; matrix products, arithmetic and copies ran while one was open for 3% of the time, Pallas kernels for 0%

profile of v8, /device:TPU:1, one launch (start us, length us, event | category | flops | bytes accessed | tf_op | source)
XLA Modules:
  0.0 308.2 jit_solution(9560702299736126559)
XLA Ops:
  7.2 0.0 all-gather.9.cloned.1.call-start
  7.2 0.8 fusion.14
  8.0 1.0 dynamic-slice_bitcast_fusion
  9.0 0.7 maximum_bitcast_fusion
  9.7 0.0 all-gather.9.cloned.1.call-update
  9.7 4.0 %collective-permute-start = (bf16[128,8192]{1,0:T(8,128)(2,1)}, bf16[128,8192]{1,0:T(8,128)(2,1)S(1)}, u32[]{:S(2)}, u32[]{:S(2)}) collective-permute-start(bf16[128,8192]{1,0:T(8,128)(2,1)} %bitcast.54), channel_id=1, source_target_pairs={{0,1},{1,0},{2,3},{3,2},{4,5},{5,4},{6,7},{7,6},{8,9},{9,8},{10,11... | collective-permute-start | bytes 6291464 | tf_op jit(solution)/shard_map/ppermute | solution.py:24
  13.7 2.1 multiply_reduce_fusion.1
  15.8 38.5 %collective-permute-done = bf16[128,8192]{1,0:T(8,128)(2,1)S(1)} collective-permute-done((bf16[128,8192]{1,0:T(8,128)(2,1)}, bf16[128,8192]{1,0:T(8,128)(2,1)S(1)}, u32[]{:S(2)}, u32[]{:S(2)}) %collective-permute-start) | collective-permute-done | bytes 2097184 | tf_op jit(solution)/shard_map/ppermute | solution.py:24
  54.3 1.3 copy-done.2
  55.6 0.5 fusion
  56.1 30.5 %all-gather.9.cloned.1.call-done = bf16[16,514,256]{2,1,0:T(8,128)(2,1)} async-done(((bf16[1,514,256]{2,1,0:T(8,128)(2,1)}), bf16[16,514,256]{2,1,0:T(8,128)(2,1)}) %all-gather.9.cloned.1.call-update) | async-done | bytes 4210704 | tf_op jit(solution)/shard_map/all_gather | solution.py:31
  86.7 0.8 convert_bitcast_fusion
  87.5 0.0 copy-start.1
  87.6 2.6 slice.76
  90.2 0.0 copy-start
  90.2 0.2 copy-done.1
  90.4 0.8 fusion.4
  91.2 2.2 copy-done.3
  93.3 0.6 fusion.2
  93.9 1.6 copy.17
  95.5 6.1 %all-to-all-start = ((bf16[128,16,512]{2,0,1:T(8,128)(2,1)}), bf16[128,16,512]{2,0,1:T(8,128)(2,1)}, u32[]{:S(2)}, u32[]{:S(2)}) async-start(bf16[128,16,512]{2,0,1:T(8,128)(2,1)} %bitcast.56), calls=%async_computation | async-start | bytes 4194304 | tf_op jit(solution)/shard_map/all_to_all | solution.py:47
  101.6 0.0 copy-start.5
  101.6 0.0 copy-start.4
  101.6 0.0 all-gather.7.cloned.1.call-start
  101.7 3.0 fusion.15
  104.6 3.1 %collective-permute-start.1 = (f32[128,256]{1,0:T(8,128)S(1)}, f32[128,256]{1,0:T(8,128)S(1)}, u32[]{:S(2)}, u32[]{:S(2)}) collective-permute-start(f32[128,256]{1,0:T(8,128)S(1)} %fusion.15), channel_id=1, source_target_pairs={{0,1},{1,0},{2,3},{3,2},{4,5},{5,4},{6,7},{7,6},{8,9},{9,8},{10,11... | collective-permute-start | bytes 393224 | tf_op jit(solution)/shard_map/ppermute | solution.py:39
  107.8 2.6 collective-permute-done.1
  110.4 0.7 fusion.11
  111.1 0.0 all-gather.7.cloned.1.call-update
  111.1 0.2 copy.12
  111.3 0.6 compare_reduce_fusion.1
  112.0 0.6 compare_reduce_fusion
  112.6 111.4 %all-gather.3 = f32[16,1,128]{2,1,0:T(1,128)S(1)} all-gather(f32[1,1,128]{2,1,0:T(1,128)S(1)} %get-tuple-element.46), channel_id=3, replica_groups=mesh['template'=16,'fsdp'=16,'dp'=2] {'fsdp'}, dimensions={0}, use_global_device_ids=true | all-gather | bytes 8704 | tf_op jit(solution)/shard_map/all_gather | solution.py:48
  224.0 2.6 all-gather.7.cloned.1.call-done
  226.6 0.0 all-to-all-done
  226.6 3.8 %multiply_reduce_fusion = f32[512]{0:T(512)S(1)} fusion(bf16[128,16,512]{2,0,1:T(8,128)(2,1)} %all-to-all-done, bf16[2048,512]{1,0:T(8,128)(2,1)} %all-gather.7.cloned.1.call-done, f32[2048]{0:T(1024)S(1)} %bitcast.61, bf16[1,512,512]{2,1,0:T(8,128)(2,1)S(1)} %copy-done.4), kind=kOutput, calls=%fused_computation.6 | convolution fusion | flops 1080032768 | bytes 4728832 | tf_op jit(solution)/shard_map/th,dh->td/dot_general | solution.py:56
  230.5 1.2 broadcast_select_fusion.2
  231.7 0.1 scatter.11
  231.8 2.3 multiply_convert_fusion.1
  234.1 2.9 convert_multiply_fusion.2
  237.0 0.2 pad_maximum_fusion
  237.2 2.0 copy.13
  239.2 43.2 %all_to_all.23 = f32[32,16,1152]{2,1,0:T(8,128)S(1)} all-to-all(f32[32,16,1152]{2,1,0:T(8,128)} %bitcast.53), channel_id=1, replica_groups=mesh['template'=16,'fsdp'=16,'dp'=2] {'dp','template'}, dimensions={0} | all-to-all | bytes 4718592 | tf_op jit(solution)/shard_map/all_to_all | solution.py:65
  282.4 0.1 reduce_sum.42
  282.5 0.6 fusion.12
  283.2 16.6 %all_to_all.24 = f32[16,16,640]{2,1,0:T(8,128)S(1)} all-to-all(f32[16,16,640]{2,1,0:T(8,128)S(1)} %broadcast_in_dim.2), channel_id=1, replica_groups=mesh['template'=16,'fsdp'=16,'dp'=2] {'template'}, dimensions={0} | all-to-all | bytes 1310720 | tf_op jit(solution)/shard_map/all_to_all | solution.py:69
  299.8 0.7 slice_reduce_fusion
  300.5 0.9 slice.81
  (16 shorter events, 0.2 us)
Async XLA Ops:
  7.2 79.5 %all-gather.9.cloned.1.call-start = ((), (), s32[]{:S(2)}) async-start(), calls=%async_computation.4 | async-start | bytes 4526080 | tf_op jit(solution)/shard_map/all_gather | solution.py:31
  9.7 44.6 %collective-permute-start = (bf16[128,8192]{1,0:T(8,128)(2,1)}, bf16[128,8192]{1,0:T(8,128)(2,1)S(1)}, u32[]{:S(2)}, u32[]{:S(2)}) collective-permute-start(bf16[128,8192]{1,0:T(8,128)(2,1)} %bitcast.54), channel_id=1, source_target_pairs={{0,1},{1,0},{2,3},{3,2},{4,5},{5,4},{6,7},{7,6},{8,9},{9,8},{10,11... | collective-permute-start | bytes 6291464 | tf_op jit(solution)/shard_map/ppermute | solution.py:24
  54.3 1.3 copy-start.2
  87.5 2.9 copy-start.1
  90.2 3.8 %copy-start = (bf16[16,512,256]{2,1,0:T(8,128)(2,1)}, bf16[16,512,256]{2,1,0:T(8,128)(2,1)S(1)}, u32[]{:S(2)}) copy-start(bf16[16,512,256]{2,1,0:T(8,128)(2,1)S(1)} %slice.76) | copy-start | bytes 12582916
  90.2 3.2 %copy-start.3 = (bf16[128,8192]{1,0:T(8,128)(2,1)S(1)}, bf16[128,8192]{1,0:T(8,128)(2,1)}, u32[]{:S(2)}) copy-start(bf16[128,8192]{1,0:T(8,128)(2,1)} %copy-done.2) | copy-start | bytes 6291460
  95.5 131.1 %all-to-all-start = ((bf16[128,16,512]{2,0,1:T(8,128)(2,1)}), bf16[128,16,512]{2,0,1:T(8,128)(2,1)}, u32[]{:S(2)}, u32[]{:S(2)}) async-start(bf16[128,16,512]{2,0,1:T(8,128)(2,1)} %bitcast.56), calls=%async_computation | async-start | bytes 4194304 | tf_op jit(solution)/shard_map/all_to_all | solution.py:47
  101.6 8.8 %copy-start.5 = (bf16[1,128,512]{2,1,0:T(8,128)(2,1)S(1)}, bf16[1,128,512]{2,1,0:T(8,128)(2,1)}, u32[]{:S(2)}) copy-start(bf16[1,128,512]{2,1,0:T(8,128)(2,1)} %param.11) | copy-start | bytes 393220
  101.6 9.5 %copy-start.4 = (bf16[1,512,512]{2,1,0:T(8,128)(2,1)S(1)}, bf16[1,512,512]{2,1,0:T(8,128)(2,1)}, u32[]{:S(2)}) copy-start(bf16[1,512,512]{2,1,0:T(8,128)(2,1)} %param.12) | copy-start | bytes 1572868
  101.6 125.0 %all-gather.7.cloned.1.call-start = ((), (), s32[]{:S(2)}) async-start(), calls=%async_computation.3 | async-start | bytes 2228224 | tf_op jit(solution)/shard_map/all_gather | solution.py:49
  104.6 5.7 %collective-permute-start.1 = (f32[128,256]{1,0:T(8,128)S(1)}, f32[128,256]{1,0:T(8,128)S(1)}, u32[]{:S(2)}, u32[]{:S(2)}) collective-permute-start(f32[128,256]{1,0:T(8,128)S(1)} %fusion.15), channel_id=1, source_target_pairs={{0,1},{1,0},{2,3},{3,2},{4,5},{5,4},{6,7},{7,6},{8,9},{9,8},{10,11... | collective-permute-start | bytes 393224 | tf_op jit(solution)/shard_map/ppermute | solution.py:39
  226.6 3.8 %copy-start.6 = (bf16[1,512]{1,0:T(2,128)(2,1)S(1)}, bf16[1,512]{1,0:T(2,128)(2,1)}, u32[]{:S(2)}) copy-start(bf16[1,512]{1,0:T(2,128)(2,1)} %param.13) | copy-start | bytes 3076
Sparse Core Ops, SparseCore 0:
  10.7 75.9 all-gather.8
  111.2 115.3 all-gather.6

commit v9 on v8

--- a/solution.py
+++ b/solution.py
@@ -44,7 +44,15 @@
     delta = (values - goal.astype(jnp.float32)).astype(jnp.bfloat16)
 
     late_batch, _, _ = lax.optimization_barrier((token_batch, mine_half, other_normed))
-    local_hidden = lax.all_to_all(late_batch, "fsdp", 1, 0, tiled=True)
+    n_f = lax.axis_size("fsdp")
+    early_rows = rows // 4
+    by_dest = token_batch.reshape(token_batch.shape[0], n_f, rows)
+    early_hidden = lax.all_to_all(by_dest[:, :, :early_rows], "fsdp", 1, 0, tiled=True)
+    late_dest = late_batch.reshape(token_batch.shape[0], n_f, rows)
+    late_hidden = lax.all_to_all(late_dest[:, :, early_rows:], "fsdp", 1, 0, tiled=True)
+    local_hidden = jnp.concatenate(
+        [early_hidden.reshape(-1, early_rows), late_hidden.reshape(-1, rows - early_rows)], axis=1
+    )
     local_ratio = lax.all_gather(ratio, "fsdp", axis=0, tiled=True)
     local_delta = lax.all_gather(delta, "fsdp", axis=0, tiled=True)
     local_xhat = local_hidden.astype(jnp.float32) * local_ratio

time: 309 us -> 315 us (1.019)
  blocking collectives: 171 us -> 145 us
  starting transfers between devices: 13.2 us -> 28.9 us
  waiting for transfers between devices: 74.3 us -> 88.4 us
    all_gather x1, blocking collectives: 111 us -> 84.5 us  [body(): local_ratio = lax.all_gather(ratio, 'fsdp', axis=0, tiled=True)]
    all_gather x1, waiting for transfers between devices: 30.5 us -> 51.1 us  [body(): gathered = lax.all_gather(w_ext, 'fsdp', axis=0, tiled=False)]
    ppermute x1, waiting for transfers between devices: 38.5 us -> 21.7 us  [body(): other_hidden = lax.ppermute(token_batch, 'dp', swap)]
    all_to_all x1 -> x2, starting transfers between devices: 6.08 us -> 22.3 us  [the longest x1 14.9 us: body(): lax.all_to_all(by_dest[:, :, :early_rows], 'fsdp', 1, 0, tiled=True)]
    all_gather x1, waiting for transfers between devices: 2.62 us -> 12.5 us  [body(): local_delta = lax.all_gather(delta, 'fsdp', axis=0, tiled=True)]
    convert_element_type x1, other arithmetic: 0.58 us -> 4.09 us  [body(): (other_f * other_ratio * g_full[None, :]).astype(jnp.bfloat16)]
  transfers between devices with their start and end apart: 5 -> 6, of which waited for: 4 -> 4; matrix products, arithmetic and copies ran while one was open for 3% -> 7% of each run, Pallas kernels for 0% -> 0%
where the time goes in v9:
time: 315 us; the launch traced here: 314 us
  blocking collectives  145 us (46%)
  waiting for transfers between devices  88.4 us (28%)
  starting transfers between devices  28.9 us (9%)
  between operations  14.3 us (5%)
  local copies, waits for them, and re-layouts  13.5 us (4%)
  other arithmetic  13.2 us (4%)
  matrix products  11.2 us (4%)
    all_gather x1, blocking collectives, body(): local_ratio = lax.all_gather(ratio, 'fsdp', axis=0, tiled=True)  84.5 us
    all_gather x1, waiting for transfers between devices, body(): gathered = lax.all_gather(w_ext, 'fsdp', axis=0, tiled=False)  51.1 us
    all_to_all x1, blocking collectives, body(): parts = lax.all_to_all(pack, ('dp', 'template'), 0, 0, tiled=True)  43.7 us
    ppermute x1, waiting for transfers between devices, body(): other_hidden = lax.ppermute(token_batch, 'dp', swap)  21.7 us
    all_to_all x1, blocking collectives, body(): lax.all_to_all(jnp.broadcast_to(done[None], (n_t,) + done.shape), 'templa...  16.6 us
    all_to_all x1, starting transfers between devices, body(): lax.all_to_all(by_dest[:, :, :early_rows], 'fsdp', 1, 0, tiled=True)  14.9 us
    all_gather x1, waiting for transfers between devices, body(): local_delta = lax.all_gather(delta, 'fsdp', axis=0, tiled=True)  12.5 us
    all_to_all x1, starting transfers between devices, body(): lax.all_to_all(late_dest[:, :, early_rows:], 'fsdp', 1, 0, tiled=True)  7.41 us
  transfers between devices with their start and end apart: 6, of which 4 were waited for; matrix products, arithmetic and copies ran while one was open for 7% of the time, Pallas kernels for 0%

profile of v9, /device:TPU:1, one launch (start us, length us, event | category | flops | bytes accessed | tf_op | source)
XLA Modules:
  0.0 314.3 jit_solution(2931508510242102842)
XLA Ops:
  7.2 0.0 all-gather.9.cloned.1.call-start
  7.2 0.8 fusion.17
  8.0 1.0 dynamic-slice_bitcast_fusion
  9.0 0.0 copy-start
  9.0 0.7 maximum_bitcast_fusion
  9.7 0.0 all-gather.9.cloned.1.call-update
  9.7 4.0 %collective-permute-start = (bf16[128,8192]{1,0:T(8,128)(2,1)}, bf16[128,8192]{1,0:T(8,128)(2,1)}, u32[]{:S(2)}, u32[]{:S(2)}) collective-permute-start(bf16[128,8192]{1,0:T(8,128)(2,1)} %bitcast.51), channel_id=1, source_target_pairs={{0,1},{1,0},{2,3},{3,2},{4,5},{5,4},{6,7},{7,6},{8,9},{9,8},{10,11... | collective-permute-start | bytes 6291464 | tf_op jit(solution)/shard_map/ppermute | solution.py:24
  13.7 2.4 copy.19
  16.1 0.1 slice.83
  16.3 0.9 copy.17
  17.2 14.9 %all-to-all-start = ((bf16[128,16,128]{2,0,1:T(8,128)(2,1)}), bf16[128,16,128]{2,0,1:T(8,128)(2,1)S(1)}, u32[]{:S(2)}, u32[]{:S(2)}) async-start(bf16[128,16,128]{2,0,1:T(8,128)(2,1)} %copy.17), calls=%async_computation | async-start | bytes 1048576 | tf_op jit(solution)/shard_map/all_to_all | solution.py:50
  32.1 0.5 multiply_reduce_fusion.1
  32.6 21.7 %collective-permute-done = bf16[128,8192]{1,0:T(8,128)(2,1)} collective-permute-done((bf16[128,8192]{1,0:T(8,128)(2,1)}, bf16[128,8192]{1,0:T(8,128)(2,1)}, u32[]{:S(2)}, u32[]{:S(2)}) %collective-permute-start) | collective-permute-done | bytes 2097184 | tf_op jit(solution)/shard_map/ppermute | solution.py:24
  54.4 2.1 fusion
  56.4 51.1 %all-gather.9.cloned.1.call-done = bf16[16,514,256]{2,1,0:T(8,128)(2,1)} async-done(((bf16[1,514,256]{2,1,0:T(8,128)(2,1)}), bf16[16,514,256]{2,1,0:T(8,128)(2,1)}) %all-gather.9.cloned.1.call-update) | async-done | bytes 4210704 | tf_op jit(solution)/shard_map/all_gather | solution.py:31
  107.5 0.8 convert_bitcast_fusion
  108.4 2.5 slice.85
  110.9 0.9 fusion.4
  111.7 4.1 %fusion.2 = bf16[128,8192]{1,0:T(8,128)(2,1)} fusion(bf16[128,8192]{1,0:T(8,128)(2,1)} %collective-permute-done, f32[8192]{0:T(1024)S(1)} %bitcast.64, f32[128]{0:T(128)S(1)} %add_rsqrt_fusion), kind=kLoop, calls=%fused_computation.4 | loop fusion | flops 4194304 | bytes 4227584 | tf_op jit(solution)/shard_map/convert_element_type | solution.py:36
  115.8 0.8 copy.21
  116.7 0.2 slice.86
  116.9 1.6 copy.18
  118.5 7.4 %all-to-all-start.1 = ((bf16[128,16,384]{2,0,1:T(8,128)(2,1)}), bf16[128,16,384]{2,0,1:T(8,128)(2,1)}, u32[]{:S(2)}, u32[]{:S(2)}) async-start(bf16[128,16,384]{2,0,1:T(8,128)(2,1)} %copy.18), calls=%async_computation.1 | async-start | bytes 3145728 | tf_op jit(solution)/shard_map/all_to_all | solution.py:52
  125.9 0.0 copy-start.4
  125.9 0.0 copy-start.3
  125.9 0.0 all-gather.7.cloned.1.call-start
  126.0 3.0 fusion.18
  128.9 2.6 collective-permute-start.1
  131.5 3.1 collective-permute-done.1
  134.7 0.7 fusion.13
  135.4 0.0 all-gather.7.cloned.1.call-update
  135.4 0.2 copy.15
  135.6 0.6 compare_reduce_fusion
  136.3 0.6 compare_reduce_fusion.1
  136.9 84.5 %all-gather.3 = f32[16,1,128]{2,1,0:T(1,128)S(1)} all-gather(f32[1,1,128]{2,1,0:T(1,128)S(1)} %get-tuple-element.46), channel_id=3, replica_groups=mesh['template'=16,'fsdp'=16,'dp'=2] {'fsdp'}, dimensions={0}, use_global_device_ids=true | all-gather | bytes 8704 | tf_op jit(solution)/shard_map/all_gather | solution.py:56
  221.4 12.5 %all-gather.7.cloned.1.call-done = bf16[2048,512]{1,0:T(8,128)(2,1)} async-done(((bf16[128,512]{1,0:T(8,128)(2,1)}), bf16[2048,512]{1,0:T(8,128)(2,1)}) %all-gather.7.cloned.1.call-update) | async-done | bytes 2097168 | tf_op jit(solution)/shard_map/all_gather | solution.py:57
  233.9 3.6 %multiply_reduce_fusion = f32[512]{0:T(512)S(1)} fusion(bf16[2048,512]{1,0:T(8,128)(2,1)} %all-gather.7.cloned.1.call-done, f32[2048]{0:T(1024)S(1)} %bitcast.65, bf16[2048,384]{1,0:T(8,128)(2,1)} %bitcast.10, bf16[2048,128]{1,0:T(8,128)(2,1)S(1)} %bitcast.61, bf16[1,512,512]{2,1,0:T(8,128)(2,1)S(1)} %copy-done.3), kind=kOutput, calls=%fused_computation.5 | convolution fusion | flops 1083178496 | bytes 4728832 | tf_op jit(solution)/shard_map/th,dh->td/dot_general | solution.py:64
  237.6 1.2 broadcast_select_fusion.2
  238.8 0.1 scatter.11
  238.9 3.7 %convert_multiply_fusion.3 = (f32[512,512]{0,1:T(8,128)S(1)}, f32[512,512]{0,1:T(8,128)S(1)}) fusion(bf16[1,512,512]{1,2,0:T(8,128)(2,1)S(1)} %copy.15, bf16[2048,512]{1,0:T(8,128)(2,1)} %all-gather.7.cloned.1.call-done, f32[2048]{0:T(1024)S(1)} %bitcast.66, f32[512]{0:T(512)S(1)} %bitcast.67, bf16[2048,384]{1,0:T(8,128)(2,1)} %bitcast.10, ...), kind=kOutput, calls=%fused_computation.21 | convolution fusion | flops 1087897600 | bytes 6825984 | tf_op jit(solution)/shard_map/td,th->dh/dot_general | solution.py:63
  242.6 0.2 pad_maximum_fusion
  242.8 2.0 copy.16
  244.8 43.7 %all_to_all.40 = f32[32,16,1152]{2,1,0:T(8,128)S(1)} all-to-all(f32[32,16,1152]{2,1,0:T(8,128)} %bitcast.56), channel_id=1, replica_groups=mesh['template'=16,'fsdp'=16,'dp'=2] {'dp','template'}, dimensions={0} | all-to-all | bytes 4718592 | tf_op jit(solution)/shard_map/all_to_all | solution.py:73
  288.5 0.1 reduce_sum.42
  288.6 0.6 fusion.14
  289.3 16.6 %all_to_all.41 = f32[16,16,640]{2,1,0:T(8,128)S(1)} all-to-all(f32[16,16,640]{2,1,0:T(8,128)S(1)} %broadcast_in_dim.2), channel_id=1, replica_groups=mesh['template'=16,'fsdp'=16,'dp'=2] {'template'}, dimensions={0} | all-to-all | bytes 1310720 | tf_op jit(solution)/shard_map/all_to_all | solution.py:77
  306.0 0.9 slice.91
  306.8 0.7 slice_reduce_fusion
  (20 shorter events, 0.2 us)
Async XLA Ops:
  7.2 100.4 %all-gather.9.cloned.1.call-start = ((), (), s32[]{:S(2)}) async-start(), calls=%async_computation.5 | async-start | bytes 4526080 | tf_op jit(solution)/shard_map/all_gather | solution.py:31
  9.0 23.1 %copy-start = (bf16[1,128,8192]{2,1,0:T(8,128)(2,1)S(1)}, bf16[1,128,8192]{2,1,0:T(8,128)(2,1)}, u32[]{:S(2)}) copy-start(bf16[1,128,8192]{2,1,0:T(8,128)(2,1)} %param.10) | copy-start | bytes 6291460
  9.7 44.6 %collective-permute-start = (bf16[128,8192]{1,0:T(8,128)(2,1)}, bf16[128,8192]{1,0:T(8,128)(2,1)}, u32[]{:S(2)}, u32[]{:S(2)}) collective-permute-start(bf16[128,8192]{1,0:T(8,128)(2,1)} %bitcast.51), channel_id=1, source_target_pairs={{0,1},{1,0},{2,3},{3,2},{4,5},{5,4},{6,7},{7,6},{8,9},{9,8},{10,11... | collective-permute-start | bytes 6291464 | tf_op jit(solution)/shard_map/ppermute | solution.py:24
  17.2 101.3 %all-to-all-start = ((bf16[128,16,128]{2,0,1:T(8,128)(2,1)}), bf16[128,16,128]{2,0,1:T(8,128)(2,1)S(1)}, u32[]{:S(2)}, u32[]{:S(2)}) async-start(bf16[128,16,128]{2,0,1:T(8,128)(2,1)} %copy.17), calls=%async_computation | async-start | bytes 1048576 | tf_op jit(solution)/shard_map/all_to_all | solution.py:50
  110.9 5.0 %copy-start.1 = (bf16[16,512,256]{2,1,0:T(8,128)(2,1)}, bf16[16,512,256]{2,1,0:T(8,128)(2,1)S(1)}, u32[]{:S(2)}) copy-start(bf16[16,512,256]{2,1,0:T(8,128)(2,1)S(1)} %slice.85) | copy-start | bytes 12582916
  116.7 9.3 %copy-start.2 = (bf16[128,8192]{1,0:T(8,128)(2,1)S(1)}, bf16[128,8192]{1,0:T(8,128)(2,1)}, u32[]{:S(2)}) copy-start(bf16[128,8192]{1,0:T(8,128)(2,1)} %fusion.2) | copy-start | bytes 6291460
  118.5 115.4 %all-to-all-start.1 = ((bf16[128,16,384]{2,0,1:T(8,128)(2,1)}), bf16[128,16,384]{2,0,1:T(8,128)(2,1)}, u32[]{:S(2)}, u32[]{:S(2)}) async-start(bf16[128,16,384]{2,0,1:T(8,128)(2,1)} %copy.18), calls=%async_computation.1 | async-start | bytes 3145728 | tf_op jit(solution)/shard_map/all_to_all | solution.py:52
  125.9 8.8 %copy-start.4 = (bf16[1,128,512]{2,1,0:T(8,128)(2,1)S(1)}, bf16[1,128,512]{2,1,0:T(8,128)(2,1)}, u32[]{:S(2)}) copy-start(bf16[1,128,512]{2,1,0:T(8,128)(2,1)} %param.11) | copy-start | bytes 393220
  125.9 9.5 %copy-start.3 = (bf16[1,512,512]{2,1,0:T(8,128)(2,1)S(1)}, bf16[1,512,512]{2,1,0:T(8,128)(2,1)}, u32[]{:S(2)}) copy-start(bf16[1,512,512]{2,1,0:T(8,128)(2,1)} %param.12) | copy-start | bytes 1572868
  125.9 108.0 %all-gather.7.cloned.1.call-start = ((), (), s32[]{:S(2)}) async-start(), calls=%async_computation.4 | async-start | bytes 2228224 | tf_op jit(solution)/shard_map/all_gather | solution.py:57
  128.9 5.7 %collective-permute-start.1 = (f32[128,256]{1,0:T(8,128)S(1)}, f32[128,256]{1,0:T(8,128)S(1)}, u32[]{:S(2)}, u32[]{:S(2)}) collective-permute-start(f32[128,256]{1,0:T(8,128)S(1)} %fusion.18), channel_id=1, source_target_pairs={{0,1},{1,0},{2,3},{3,2},{4,5},{5,4},{6,7},{7,6},{8,9},{9,8},{10,11... | collective-permute-start | bytes 393224 | tf_op jit(solution)/shard_map/ppermute | solution.py:39
  233.9 3.7 %copy-start.5 = (bf16[1,512]{1,0:T(2,128)(2,1)S(1)}, bf16[1,512]{1,0:T(2,128)(2,1)}, u32[]{:S(2)}) copy-start(bf16[1,512]{1,0:T(2,128)(2,1)} %param.13) | copy-start | bytes 3076
Sparse Core Ops, SparseCore 0:
  10.1 97.3 all-gather.8
  135.5 98.3 all-gather.6

commit v10 on v8

--- a/solution.py
+++ b/solution.py
@@ -56,20 +56,29 @@
     back = jnp.einsum("th,dh->td", local_delta, w_shard, preferred_element_type=jnp.float32) * scale
     gain_info = jnp.sum(jnp.square(back * local_xhat), axis=0)
 
-    extra = jnp.zeros((rows, 128), jnp.float32)
-    extra = extra.at[:, 0].set(gain_info * g_f).at[:, 1].set(gain_info)
-    pack = jnp.concatenate([fisher * w_shard.astype(jnp.float32), fisher, extra], axis=1)
-    cols = pack.shape[1]
-    piece = rows // (n_t * n_dp)
-    pack = pack.reshape(n_t * n_dp, piece, cols)
+    n_pieces = n_t * n_dp
+    piece = rows // n_pieces
+    flat = piece * heads
+    lane = 128
+    tail_pad = -(2 * piece) % lane
+    pack = jnp.concatenate(
+        [
+            (fisher * w_shard.astype(jnp.float32)).reshape(n_pieces, flat),
+            fisher.reshape(n_pieces, flat),
+            (gain_info * g_f).reshape(n_pieces, piece),
+            gain_info.reshape(n_pieces, piece),
+            jnp.zeros((n_pieces, tail_pad), jnp.float32),
+        ],
+        axis=1,
+    )
     parts = lax.all_to_all(pack, ("dp", "template"), 0, 0, tiled=True)
     total = jnp.sum(parts, axis=0)
-    ratio_block = jnp.zeros((piece, 128), jnp.float32).at[:, 0].set(total[:, 2 * heads] / total[:, 2 * heads + 1])
-    done = jnp.concatenate([total[:, :heads] / total[:, heads : 2 * heads], ratio_block], axis=1)
+    quotient = total[:flat] / total[flat : 2 * flat]
+    gain_quotient = total[2 * flat : 2 * flat + piece] / total[2 * flat + piece : 2 * flat + 2 * piece]
+    done = jnp.concatenate([quotient, gain_quotient, jnp.zeros((-(flat + piece) % lane,), jnp.float32)])
     spread = lax.all_to_all(jnp.broadcast_to(done[None], (n_t,) + done.shape), "template", 0, 0, tiled=True)
-    full = spread.reshape(n_t * piece, done.shape[1])
-    merged = full[:, :heads]
-    merged_gain = full[:, heads]
+    merged = spread[:, :flat].reshape(n_t * piece, heads)
+    merged_gain = spread[:, flat : flat + piece].reshape(n_t * piece)
     return merged, merged_gain
 
 

time: 309 us -> 309 us (level)
  local copies, waits for them, and re-layouts: 12.8 us -> 16 us
    another operation x4 -> x0, other arithmetic: 3.12 us -> none
where the time goes in v10:
time: 309 us; the launch traced here: 308 us
  blocking collectives  171 us (55%)
  waiting for transfers between devices  72.1 us (23%)
  local copies, waits for them, and re-layouts  16 us (5%)
  between operations  14.3 us (5%)
  starting transfers between devices  13.2 us (4%)
  matrix products  11.7 us (4%)
  other arithmetic  9.82 us (3%)
    all_gather x1, blocking collectives, body(): local_ratio = lax.all_gather(ratio, 'fsdp', axis=0, tiled=True)  112 us
    all_to_all x1, blocking collectives, body(): parts = lax.all_to_all(pack, ('dp', 'template'), 0, 0, tiled=True)  43.2 us
    ppermute x1, waiting for transfers between devices, body(): other_hidden = lax.ppermute(token_batch, 'dp', swap)  38.5 us
    all_gather x1, waiting for transfers between devices, body(): gathered = lax.all_gather(w_ext, 'fsdp', axis=0, tiled=False)  30.5 us
    all_to_all x1, blocking collectives, body(): lax.all_to_all(jnp.broadcast_to(done[None], (n_t,) + done.shape), 'templa...  15.7 us
  transfers between devices with their start and end apart: 5, of which 4 were waited for; matrix products, arithmetic and copies ran while one was open for 3% of the time, Pallas kernels for 0%

profile of v10, /device:TPU:1, one launch (start us, length us, event | category | flops | bytes accessed | tf_op | source)
XLA Modules:
  0.0 308.5 jit_solution(17766905705395261467)
XLA Ops:
  7.2 0.0 all-gather.9.cloned.1.call-start
  7.2 0.8 fusion.13
  8.0 1.0 dynamic-slice_bitcast_fusion
  9.0 0.7 maximum_bitcast_fusion
  9.7 0.0 all-gather.9.cloned.1.call-update
  9.7 4.0 %collective-permute-start = (bf16[128,8192]{1,0:T(8,128)(2,1)}, bf16[128,8192]{1,0:T(8,128)(2,1)S(1)}, u32[]{:S(2)}, u32[]{:S(2)}) collective-permute-start(bf16[128,8192]{1,0:T(8,128)(2,1)} %bitcast.48), channel_id=1, source_target_pairs={{0,1},{1,0},{2,3},{3,2},{4,5},{5,4},{6,7},{7,6},{8,9},{9,8},{10,11... | collective-permute-start | bytes 6291464 | tf_op jit(solution)/shard_map/ppermute | solution.py:24
  13.7 2.1 multiply_reduce_fusion.1
  15.8 38.5 %collective-permute-done = bf16[128,8192]{1,0:T(8,128)(2,1)S(1)} collective-permute-done((bf16[128,8192]{1,0:T(8,128)(2,1)}, bf16[128,8192]{1,0:T(8,128)(2,1)S(1)}, u32[]{:S(2)}, u32[]{:S(2)}) %collective-permute-start) | collective-permute-done | bytes 2097184 | tf_op jit(solution)/shard_map/ppermute | solution.py:24
  54.3 1.3 copy-done.2
  55.7 0.5 fusion
  56.2 30.5 %all-gather.9.cloned.1.call-done = bf16[16,514,256]{2,1,0:T(8,128)(2,1)} async-done(((bf16[1,514,256]{2,1,0:T(8,128)(2,1)}), bf16[16,514,256]{2,1,0:T(8,128)(2,1)}) %all-gather.9.cloned.1.call-update) | async-done | bytes 4210704 | tf_op jit(solution)/shard_map/all_gather | solution.py:31
  86.7 0.8 convert_bitcast_fusion
  87.5 0.0 copy-start.1
  87.6 2.6 slice.33
  90.2 0.2 copy-done.1
  90.4 0.8 fusion.4
  91.2 2.2 copy-done.3
  93.3 0.6 fusion.2
  93.9 1.6 copy.14
  95.5 6.1 %all-to-all-start = ((bf16[128,16,512]{2,0,1:T(8,128)(2,1)}), bf16[128,16,512]{2,0,1:T(8,128)(2,1)}, u32[]{:S(2)}, u32[]{:S(2)}) async-start(bf16[128,16,512]{2,0,1:T(8,128)(2,1)} %bitcast.50), calls=%async_computation | async-start | bytes 4194304 | tf_op jit(solution)/shard_map/all_to_all | solution.py:47
  101.6 0.0 copy-start.5
  101.6 0.0 copy-start.6
  101.6 0.0 all-gather.7.cloned.1.call-start
  101.7 2.9 fusion.14
  104.6 3.1 %collective-permute-start.1 = (f32[128,256]{1,0:T(8,128)S(1)}, f32[128,256]{1,0:T(8,128)S(1)}, u32[]{:S(2)}, u32[]{:S(2)}) collective-permute-start(f32[128,256]{1,0:T(8,128)S(1)} %fusion.14), channel_id=1, source_target_pairs={{0,1},{1,0},{2,3},{3,2},{4,5},{5,4},{6,7},{7,6},{8,9},{9,8},{10,11... | collective-permute-start | bytes 393224 | tf_op jit(solution)/shard_map/ppermute | solution.py:39
  107.7 2.6 collective-permute-done.1
  110.3 0.7 fusion.11
  111.0 0.0 all-gather.7.cloned.1.call-update
  111.1 0.1 reshape.101
  111.2 112.5 %all-gather.3 = f32[16,1,128]{2,1,0:T(1,128)S(1)} all-gather(f32[1,1,128]{2,1,0:T(1,128)S(1)} %get-tuple-element.8), channel_id=3, replica_groups=mesh['template'=16,'fsdp'=16,'dp'=2] {'fsdp'}, dimensions={0}, use_global_device_ids=true | all-gather | bytes 8704 | tf_op jit(solution)/shard_map/all_gather | solution.py:48
  223.6 0.0 all-to-all-done
  223.6 2.3 multiply_convert_fusion.1
  225.9 0.4 all-gather.7.cloned.1.call-done
  226.3 4.0 %convert_multiply_fusion.2 = (f32[512,512]{1,0:T(8,128)S(1)}, f32[512,512]{1,0:T(8,128)}) fusion(bf16[1,512,512]{2,1,0:T(8,128)(2,1)} %param.6, bf16[2048,512]{1,0:T(8,128)(2,1)S(1)} %multiply_convert_fusion.1, bf16[2048,512]{1,0:T(8,128)(2,1)} %all-gather.7.cloned.1.call-done), kind=kOutput, calls=%fused_computation.18 | convolution fusion | flops 1077411840 | bytes 6815744 | tf_op jit(solution)/shard_map/td,th->dh/dot_general | solution.py:55
  230.3 0.2 reshape.93
  230.5 4.1 %multiply_reduce_fusion = f32[512]{0:T(512)S(1)} fusion(bf16[128,16,512]{2,0,1:T(8,128)(2,1)} %all-to-all-done, bf16[2048,512]{1,0:T(8,128)(2,1)} %all-gather.7.cloned.1.call-done, f32[2048]{0:T(1024)S(1)} %bitcast.56, bf16[1,512,512]{2,1,0:T(8,128)(2,1)} %param.6), kind=kOutput, calls=%fused_computation.6 | convolution fusion | flops 1080032768 | bytes 4728832 | tf_op jit(solution)/shard_map/th,dh->td/dot_general | solution.py:56
  234.6 0.1 reduce_sum.41
  234.7 1.2 reshape.94
  235.8 2.2 concatenate.14
  238.0 1.4 all_to_all.24
  239.5 43.2 %all_to_all.31 = f32[32,1,16512]{2,1,0:T(1,128)S(1)} all-to-all(f32[32,1,16512]{2,1,0:T(1,128)S(1)} %all_to_all.24), channel_id=1, replica_groups=mesh['template'=16,'fsdp'=16,'dp'=2] {'dp','template'}, dimensions={0} | all-to-all | bytes 4227072 | tf_op jit(solution)/shard_map/all_to_all | solution.py:74
  282.6 1.2 reduce_sum.42
  283.8 0.1 slice_divide_fusion.1
  283.9 0.1 concatenate.15
  284.0 0.3 broadcast_in_dim.8
  284.3 15.7 %all_to_all.32 = f32[16,1,8320]{2,1,0:T(1,128)S(1)} all-to-all(f32[16,1,8320]{2,1,0:T(1,128)S(1)} %broadcast_in_dim.8), channel_id=1, replica_groups=mesh['template'=16,'fsdp'=16,'dp'=2] {'template'}, dimensions={0} | all-to-all | bytes 1064960 | tf_op jit(solution)/shard_map/all_to_all | solution.py:79
  300.1 0.6 reshape.96
  300.8 0.9 reshape.95
  (21 shorter events, 0.2 us)
Async XLA Ops:
  7.2 79.5 %all-gather.9.cloned.1.call-start = ((), (), s32[]{:S(2)}) async-start(), calls=%async_computation.4 | async-start | bytes 4526080 | tf_op jit(solution)/shard_map/all_gather | solution.py:31
  9.7 44.6 %collective-permute-start = (bf16[128,8192]{1,0:T(8,128)(2,1)}, bf16[128,8192]{1,0:T(8,128)(2,1)S(1)}, u32[]{:S(2)}, u32[]{:S(2)}) collective-permute-start(bf16[128,8192]{1,0:T(8,128)(2,1)} %bitcast.48), channel_id=1, source_target_pairs={{0,1},{1,0},{2,3},{3,2},{4,5},{5,4},{6,7},{7,6},{8,9},{9,8},{10,11... | collective-permute-start | bytes 6291464 | tf_op jit(solution)/shard_map/ppermute | solution.py:24
  54.3 1.3 copy-start.2
  87.5 2.9 copy-start.1
  90.2 3.8 %copy-start = (bf16[16,512,256]{2,1,0:T(8,128)(2,1)}, bf16[16,512,256]{2,1,0:T(8,128)(2,1)S(1)}, u32[]{:S(2)}) copy-start(bf16[16,512,256]{2,1,0:T(8,128)(2,1)S(1)} %slice.33) | copy-start | bytes 12582916
  90.2 3.2 %copy-start.3 = (bf16[128,8192]{1,0:T(8,128)(2,1)S(1)}, bf16[128,8192]{1,0:T(8,128)(2,1)}, u32[]{:S(2)}) copy-start(bf16[128,8192]{1,0:T(8,128)(2,1)} %copy-done.2) | copy-start | bytes 6291460
  95.5 128.1 %all-to-all-start = ((bf16[128,16,512]{2,0,1:T(8,128)(2,1)}), bf16[128,16,512]{2,0,1:T(8,128)(2,1)}, u32[]{:S(2)}, u32[]{:S(2)}) async-start(bf16[128,16,512]{2,0,1:T(8,128)(2,1)} %bitcast.50), calls=%async_computation | async-start | bytes 4194304 | tf_op jit(solution)/shard_map/all_to_all | solution.py:47
  101.6 8.7 %copy-start.5 = (bf16[1,128,512]{2,1,0:T(8,128)(2,1)S(1)}, bf16[1,128,512]{2,1,0:T(8,128)(2,1)}, u32[]{:S(2)}) copy-start(bf16[1,128,512]{2,1,0:T(8,128)(2,1)} %param.5) | copy-start | bytes 393220
  101.6 9.4 %copy-start.6 = (bf16[1,512]{1,0:T(2,128)(2,1)S(1)}, bf16[1,512]{1,0:T(2,128)(2,1)}, u32[]{:S(2)}) copy-start(bf16[1,512]{1,0:T(2,128)(2,1)} %param.7) | copy-start | bytes 3076
  101.6 124.7 %all-gather.7.cloned.1.call-start = ((), (), s32[]{:S(2)}) async-start(), calls=%async_computation.3 | async-start | bytes 2228224 | tf_op jit(solution)/shard_map/all_gather | solution.py:49
  104.6 5.7 %collective-permute-start.1 = (f32[128,256]{1,0:T(8,128)S(1)}, f32[128,256]{1,0:T(8,128)S(1)}, u32[]{:S(2)}, u32[]{:S(2)}) collective-permute-start(f32[128,256]{1,0:T(8,128)S(1)} %fusion.14), channel_id=1, source_target_pairs={{0,1},{1,0},{2,3},{3,2},{4,5},{5,4},{6,7},{7,6},{8,9},{9,8},{10,11... | collective-permute-start | bytes 393224 | tf_op jit(solution)/shard_map/ppermute | solution.py:39
  230.5 4.2 %copy-start.4 = (f32[512,512]{1,0:T(8,128)S(1)}, f32[512,512]{1,0:T(8,128)}, u32[]{:S(2)}) copy-start(f32[512,512]{1,0:T(8,128)} %get-tuple-element.11) | copy-start | bytes 3145732
Sparse Core Ops, SparseCore 0:
  10.7 75.9 all-gather.8
  111.2 115.1 all-gather.6

commit v11 on v8

--- a/solution.py
+++ b/solution.py
@@ -29,13 +29,18 @@
     w_cols = lax.dynamic_slice_in_dim(w_shard, dp_at * half, half, 1)
     w_ext = jnp.concatenate([w_cols, g_shard.reshape(-1, half)], axis=0)
     gathered = lax.all_gather(w_ext, "fsdp", axis=0, tiled=False)
-    w_half = gathered[:, :rows, :].reshape(-1, half)
+    w_half = gathered[:, :rows, :]
     g_full = gathered[:, rows:, :].reshape(-1).astype(jnp.float32)
     xhat = hidden_f * ratio
     normed = (xhat * g_full[None, :]).astype(jnp.bfloat16)
     other_normed = (other_f * other_ratio * g_full[None, :]).astype(jnp.bfloat16)
-    mine_half = jnp.dot(normed, w_half, preferred_element_type=jnp.float32)
-    theirs_half = jnp.dot(other_normed, w_half, preferred_element_type=jnp.float32)
+    n_blocks = gathered.shape[0]
+    mine_half = jnp.einsum(
+        "tfr,frh->th", normed.reshape(-1, n_blocks, rows), w_half, preferred_element_type=jnp.float32
+    )
+    theirs_half = jnp.einsum(
+        "tfr,frh->th", other_normed.reshape(-1, n_blocks, rows), w_half, preferred_element_type=jnp.float32
+    )
     from_other = lax.ppermute(theirs_half, "dp", swap)
     both = jnp.stack([mine_half, from_other])
     first = jnp.where(dp_at == 0, both[0], both[1])

time: 309 us -> 308 us (level)
    dot_general x2, matrix products: 3.71 us -> 8.63 us  [the longest x1 5.03 us: body(): jnp.einsum('tfr,frh->th', normed.reshape(-1, n_blocks, rows), w_half, pre...]
    convert_element_type x1, other arithmetic: 0.58 us -> 3.77 us  [body(): (other_f * other_ratio * g_full[None, :]).astype(jnp.bfloat16)]
    unnamed x16 -> x18, local copies, waits for them, and re-layouts: 3.96 us -> 6.88 us
  transfers between devices with their start and end apart: 5 -> 5, of which waited for: 4 -> 4; matrix products, arithmetic and copies ran while one was open for 3% -> 4% of each run, Pallas kernels for 0% -> 0%
where the time goes in v11:
time: 308 us
  blocking collectives  170 us (55%)
  waiting for transfers between devices  71.8 us (23%)
  between operations  14.3 us (5%)
  starting transfers between devices  13.2 us (4%)
  local copies, waits for them, and re-layouts  13.1 us (4%)
  matrix products  13.1 us (4%)
  other arithmetic  12.2 us (4%)
    all_gather x1, blocking collectives, body(): local_ratio = lax.all_gather(ratio, 'fsdp', axis=0, tiled=True)  111 us
    all_to_all x1, blocking collectives, body(): parts = lax.all_to_all(pack, ('dp', 'template'), 0, 0, tiled=True)  43.1 us
    ppermute x1, waiting for transfers between devices, body(): other_hidden = lax.ppermute(token_batch, 'dp', swap)  35.7 us
    all_gather x1, waiting for transfers between devices, body(): gathered = lax.all_gather(w_ext, 'fsdp', axis=0, tiled=False)  30.4 us
    all_to_all x1, blocking collectives, body(): lax.all_to_all(jnp.broadcast_to(done[None], (n_t,) + done.shape), 'templa...  16.6 us
    unnamed x18, local copies, waits for them, and re-layouts  6.88 us
  transfers between devices with their start and end apart: 5, of which 4 were waited for; matrix products, arithmetic and copies ran while one was open for 4% of the time, Pallas kernels for 0%

profile of v11, /device:TPU:1, one launch (start us, length us, event | category | flops | bytes accessed | tf_op | source)
XLA Modules:
  0.0 307.9 jit_solution(13124093446112993716)
XLA Ops:
  7.2 0.0 copy-start
  7.2 0.0 all-gather.9.cloned.1.call-start
  7.2 0.9 fusion.31
  8.1 1.0 dynamic-slice_bitcast_fusion
  9.1 0.7 maximum_bitcast_fusion
  9.8 0.0 all-gather.9.cloned.1.call-update
  9.8 4.0 %collective-permute-start = (bf16[128,8192]{1,0:T(8,128)(2,1)}, bf16[128,8192]{1,0:T(8,128)(2,1)S(1)}, u32[]{:S(2)}, u32[]{:S(2)}) collective-permute-start(bf16[128,8192]{1,0:T(8,128)(2,1)} %bitcast.60), channel_id=1, source_target_pairs={{0,1},{1,0},{2,3},{3,2},{4,5},{5,4},{6,7},{7,6},{8,9},{9,8},{10,11... | collective-permute-start | bytes 6291464 | tf_op jit(solution)/shard_map/ppermute | solution.py:24
  13.8 4.4 %copy.22 = f32[16,8,16,512]{3,2,1,0:T(8,128)} copy(bf16[16,8,16,512]{3,1,2,0:T(8,128)(2,1)} %bitcast.61) | data formatting | bytes 6291456
  18.2 0.5 multiply_reduce_fusion.1
  18.7 35.7 %collective-permute-done = bf16[128,8192]{1,0:T(8,128)(2,1)S(1)} collective-permute-done((bf16[128,8192]{1,0:T(8,128)(2,1)}, bf16[128,8192]{1,0:T(8,128)(2,1)S(1)}, u32[]{:S(2)}, u32[]{:S(2)}) %collective-permute-start) | collective-permute-done | bytes 2097184 | tf_op jit(solution)/shard_map/ppermute | solution.py:24
  54.4 1.3 copy-done.1
  55.7 0.5 fusion
  56.2 30.4 %all-gather.9.cloned.1.call-done = bf16[16,514,256]{2,1,0:T(8,128)(2,1)} async-done(((bf16[1,514,256]{2,1,0:T(8,128)(2,1)}), bf16[16,514,256]{2,1,0:T(8,128)(2,1)}) %all-gather.9.cloned.1.call-update) | async-done | bytes 4210704 | tf_op jit(solution)/shard_map/all_gather | solution.py:31
  86.7 1.0 fusion.29
  87.7 3.8 %fusion.2 = bf16[128,8192]{1,0:T(8,128)(2,1)} fusion(bf16[128,8192]{1,0:T(8,128)(2,1)} %copy-done.1, f32[8192]{0:T(1024)S(1)} %bitcast.69, f32[128]{0:T(128)S(1)} %add_rsqrt_fusion), kind=kLoop, calls=%fused_computation.4 | loop fusion | flops 4194304 | bytes 4227584 | tf_op jit(solution)/shard_map/convert_element_type | solution.py:36
  91.5 0.0 copy-done.2
  91.5 5.0 %fusion.15 = f32[128,256]{1,0:T(8,128)S(1)} fusion(bf16[16,514,256]{2,1,0:T(8,128)(2,1)} %all-gather.9.cloned.1.call-done, f32[128,16,512]{2,1,0:T(8,128)S(1)} %bitcast.65, f32[16,512]{1,0:T(8,128)S(1)} %bitcast.73, f32[128]{0:T(128)S(1)} %get-tuple-element.49), kind=kOutput, calls=%fused_computation.25 | convolution fusion | flops 540016640 | bytes 8552960 | tf_op jit(solution)/shard_map/tfr,frh->th/dot_general | solution.py:38
  96.5 1.5 copy.40
  98.1 6.0 %all-to-all-start = ((bf16[128,16,512]{2,0,1:T(8,128)(2,1)}), bf16[128,16,512]{2,0,1:T(8,128)(2,1)S(1)}, u32[]{:S(2)}, u32[]{:S(2)}) async-start(bf16[128,16,512]{2,0,1:T(8,128)(2,1)} %bitcast.64), calls=%async_computation | async-start | bytes 4194304 | tf_op jit(solution)/shard_map/all_to_all | solution.py:52
  104.1 0.0 all-gather.7.cloned.1.call-start
  104.2 0.0 copy-start.4
  104.2 0.0 copy-start.3
  104.2 3.6 %fusion.20 = f32[128,256]{1,0:T(8,128)S(1)} fusion(bf16[16,514,256]{2,1,0:T(8,128)(2,1)} %all-gather.9.cloned.1.call-done, bf16[16,16,8,512]{3,2,1,0:T(8,128)(2,1)} %bitcast.68), kind=kOutput, calls=%fused_computation.26 | convolution fusion | flops 536870912 | bytes 6422528 | tf_op jit(solution)/shard_map/tfr,frh->th/dot_general | solution.py:41
  107.8 3.1 %collective-permute-start.1 = (f32[128,256]{1,0:T(8,128)S(1)}, f32[128,256]{1,0:T(8,128)S(1)}, u32[]{:S(2)}, u32[]{:S(2)}) collective-permute-start(f32[128,256]{1,0:T(8,128)S(1)} %fusion.20), channel_id=1, source_target_pairs={{0,1},{1,0},{2,3},{3,2},{4,5},{5,4},{6,7},{7,6},{8,9},{9,8},{10,11... | collective-permute-start | bytes 393224 | tf_op jit(solution)/shard_map/ppermute | solution.py:44
  110.9 2.6 collective-permute-done.1
  113.5 0.0 copy-done.4
  113.6 0.7 fusion.27
  114.2 0.0 all-gather.7.cloned.1.call-update
  114.3 0.2 copy.18
  114.5 0.6 compare_reduce_fusion
  115.1 0.6 compare_reduce_fusion.1
  115.8 110.6 %all-gather.3 = f32[16,1,128]{2,1,0:T(1,128)S(1)} all-gather(f32[1,1,128]{2,1,0:T(1,128)S(1)} %get-tuple-element.48), channel_id=3, replica_groups=mesh['template'=16,'fsdp'=16,'dp'=2] {'fsdp'}, dimensions={0}, use_global_device_ids=true | all-gather | bytes 8704 | tf_op jit(solution)/shard_map/all_gather | solution.py:53
  226.4 3.0 all-gather.7.cloned.1.call-done
  229.4 0.0 all-to-all-done
  229.4 3.2 %multiply_reduce_fusion = f32[512]{0:T(512)S(1)} fusion(bf16[128,16,512]{2,0,1:T(8,128)(2,1)S(1)} %all-to-all-done, bf16[2048,512]{1,0:T(8,128)(2,1)} %all-gather.7.cloned.1.call-done, f32[2048]{0:T(1024)S(1)} %bitcast.71, bf16[1,512,512]{2,1,0:T(8,128)(2,1)S(1)} %copy-done.3), kind=kOutput, calls=%fused_computation.9 | convolution fusion | flops 1080032768 | bytes 4728832 | tf_op jit(solution)/shard_map/th,dh->td/dot_general | solution.py:61
  232.6 1.2 broadcast_select_fusion.2
  233.8 0.1 scatter.11
  233.9 0.7 multiply_convert_fusion.1
  234.6 0.9 copy-done.6
  235.5 1.3 convert_multiply_fusion.2
  236.8 0.2 pad_maximum_fusion
  237.0 2.0 copy.19
  239.0 43.1 %all_to_all.23 = f32[32,16,1152]{2,1,0:T(8,128)S(1)} all-to-all(f32[32,16,1152]{2,1,0:T(8,128)} %bitcast.63), channel_id=1, replica_groups=mesh['template'=16,'fsdp'=16,'dp'=2] {'dp','template'}, dimensions={0} | all-to-all | bytes 4718592 | tf_op jit(solution)/shard_map/all_to_all | solution.py:70
  282.1 0.1 reduce_sum.42
  282.2 0.6 fusion.28
  282.9 16.6 %all_to_all.24 = f32[16,16,640]{2,1,0:T(8,128)S(1)} all-to-all(f32[16,16,640]{2,1,0:T(8,128)S(1)} %broadcast_in_dim.2), channel_id=1, replica_groups=mesh['template'=16,'fsdp'=16,'dp'=2] {'template'}, dimensions={0} | all-to-all | bytes 1310720 | tf_op jit(solution)/shard_map/all_to_all | solution.py:74
  299.5 0.9 slice.81
  300.4 0.7 slice_reduce_fusion
  (17 shorter events, 0.2 us)
Async XLA Ops:
  7.2 11.0 %copy-start = (bf16[1,128,8192]{2,1,0:T(8,128)(2,1)S(1)}, bf16[1,128,8192]{2,1,0:T(8,128)(2,1)}, u32[]{:S(2)}) copy-start(bf16[1,128,8192]{2,1,0:T(8,128)(2,1)} %param.10) | copy-start | bytes 6291460
  7.2 79.5 %all-gather.9.cloned.1.call-start = ((), (), s32[]{:S(2)}) async-start(), calls=%async_computation.4 | async-start | bytes 4526080 | tf_op jit(solution)/shard_map/all_gather | solution.py:31
  9.8 44.6 %collective-permute-start = (bf16[128,8192]{1,0:T(8,128)(2,1)}, bf16[128,8192]{1,0:T(8,128)(2,1)S(1)}, u32[]{:S(2)}, u32[]{:S(2)}) collective-permute-start(bf16[128,8192]{1,0:T(8,128)(2,1)} %bitcast.60), channel_id=1, source_target_pairs={{0,1},{1,0},{2,3},{3,2},{4,5},{5,4},{6,7},{7,6},{8,9},{9,8},{10,11... | collective-permute-start | bytes 6291464 | tf_op jit(solution)/shard_map/ppermute | solution.py:24
  54.4 1.3 copy-start.1
  86.7 4.8 %copy-start.2 = (f32[16,8,16,512]{3,2,1,0:T(8,128)S(1)}, f32[16,8,16,512]{3,2,1,0:T(8,128)}, u32[]{:S(2)}) copy-start(f32[16,8,16,512]{3,2,1,0:T(8,128)} %copy.22) | copy-start | bytes 12582916
  98.1 131.3 %all-to-all-start = ((bf16[128,16,512]{2,0,1:T(8,128)(2,1)}), bf16[128,16,512]{2,0,1:T(8,128)(2,1)S(1)}, u32[]{:S(2)}, u32[]{:S(2)}) async-start(bf16[128,16,512]{2,0,1:T(8,128)(2,1)} %bitcast.64), calls=%async_computation | async-start | bytes 4194304 | tf_op jit(solution)/shard_map/all_to_all | solution.py:52
  104.1 125.2 %all-gather.7.cloned.1.call-start = ((), (), s32[]{:S(2)}) async-start(), calls=%async_computation.3 | async-start | bytes 2228224 | tf_op jit(solution)/shard_map/all_gather | solution.py:54
  104.2 9.4 %copy-start.4 = (bf16[1,128,512]{2,1,0:T(8,128)(2,1)S(1)}, bf16[1,128,512]{2,1,0:T(8,128)(2,1)}, u32[]{:S(2)}) copy-start(bf16[1,128,512]{2,1,0:T(8,128)(2,1)} %param.11) | copy-start | bytes 393220
  104.2 10.1 %copy-start.3 = (bf16[1,512,512]{2,1,0:T(8,128)(2,1)S(1)}, bf16[1,512,512]{2,1,0:T(8,128)(2,1)}, u32[]{:S(2)}) copy-start(bf16[1,512,512]{2,1,0:T(8,128)(2,1)} %param.12) | copy-start | bytes 1572868
  107.8 5.7 %collective-permute-start.1 = (f32[128,256]{1,0:T(8,128)S(1)}, f32[128,256]{1,0:T(8,128)S(1)}, u32[]{:S(2)}, u32[]{:S(2)}) collective-permute-start(f32[128,256]{1,0:T(8,128)S(1)} %fusion.20), channel_id=1, source_target_pairs={{0,1},{1,0},{2,3},{3,2},{4,5},{5,4},{6,7},{7,6},{8,9},{9,8},{10,11... | collective-permute-start | bytes 393224 | tf_op jit(solution)/shard_map/ppermute | solution.py:44
  229.4 3.2 %copy-start.5 = (bf16[1,512]{1,0:T(2,128)(2,1)S(1)}, bf16[1,512]{1,0:T(2,128)(2,1)}, u32[]{:S(2)}) copy-start(bf16[1,512]{1,0:T(2,128)(2,1)} %param.13) | copy-start | bytes 3076
  233.9 1.6 copy-start.6
Sparse Core Ops, SparseCore 0:
  10.7 75.9 all-gather.8
  114.4 114.9 all-gather.6

commit v12 on v11

--- a/solution.py
+++ b/solution.py
@@ -48,7 +48,7 @@
     values = jnp.concatenate([first, second], axis=1) * scale
     delta = (values - goal.astype(jnp.float32)).astype(jnp.bfloat16)
 
-    late_batch, _, _ = lax.optimization_barrier((token_batch, mine_half, other_normed))
+    late_batch, _ = lax.optimization_barrier((token_batch, theirs_half))
     local_hidden = lax.all_to_all(late_batch, "fsdp", 1, 0, tiled=True)
     local_ratio = lax.all_gather(ratio, "fsdp", axis=0, tiled=True)
     local_delta = lax.all_gather(delta, "fsdp", axis=0, tiled=True)

time: 308 us -> 304 us (0.987)
  local copies, waits for them, and re-layouts: 13.1 us -> 8.76 us
  waiting for transfers between devices: 71.8 us -> 75 us
    ppermute x1, waiting for transfers between devices: 35.7 us -> 40.6 us  [body(): other_hidden = lax.ppermute(token_batch, 'dp', swap)]
    unnamed x18 -> x16, local copies, waits for them, and re-layouts: 6.88 us -> 2.58 us
    convert_element_type x1, other arithmetic: 3.77 us -> 0.58 us  [body(): (other_f * other_ratio * g_full[None, :]).astype(jnp.bfloat16)]
  transfers between devices with their start and end apart: 5 -> 5, of which waited for: 4 -> 3; matrix products, arithmetic and copies ran while one was open for 4% -> 3% of each run, Pallas kernels for 0% -> 0%
where the time goes in v12:
time: 304 us
  blocking collectives  171 us (56%)
  waiting for transfers between devices  75 us (25%)
  between operations  14.3 us (5%)
  starting transfers between devices  13.2 us (4%)
  matrix products  11 us (4%)
  other arithmetic  10.7 us (4%)
  local copies, waits for them, and re-layouts  8.76 us (3%)
    all_gather x1, blocking collectives, body(): local_ratio = lax.all_gather(ratio, 'fsdp', axis=0, tiled=True)  111 us
    all_to_all x1, blocking collectives, body(): parts = lax.all_to_all(pack, ('dp', 'template'), 0, 0, tiled=True)  43.5 us
    ppermute x1, waiting for transfers between devices, body(): other_hidden = lax.ppermute(token_batch, 'dp', swap)  40.6 us
    all_gather x1, waiting for transfers between devices, body(): gathered = lax.all_gather(w_ext, 'fsdp', axis=0, tiled=False)  31.8 us
    all_to_all x1, blocking collectives, body(): lax.all_to_all(jnp.broadcast_to(done[None], (n_t,) + done.shape), 'templa...  16.6 us
    all_to_all x1, starting transfers between devices, body(): local_hidden = lax.all_to_all(late_batch, 'fsdp', 1, 0, tiled=True)  6.08 us
  transfers between devices with their start and end apart: 5, of which 3 were waited for; matrix products, arithmetic and copies ran while one was open for 3% of the time, Pallas kernels for 0%

profile of v12, /device:TPU:1, one launch (start us, length us, event | category | flops | bytes accessed | tf_op | source)
XLA Modules:
  0.0 303.6 jit_solution(11642701574735450306)
XLA Ops:
  7.2 0.0 all-gather.9.cloned.1.call-start
  7.2 0.8 fusion.31
  8.0 1.0 dynamic-slice_bitcast_fusion
  9.0 0.7 maximum_bitcast_fusion
  9.7 0.0 all-gather.9.cloned.1.call-update
  9.7 4.0 %collective-permute-start = (bf16[128,8192]{1,0:T(8,128)(2,1)}, bf16[128,8192]{1,0:T(8,128)(2,1)S(1)}, u32[]{:S(2)}, u32[]{:S(2)}) collective-permute-start(bf16[128,8192]{1,0:T(8,128)(2,1)} %bitcast.60), channel_id=1, source_target_pairs={{0,1},{1,0},{2,3},{3,2},{4,5},{5,4},{6,7},{7,6},{8,9},{9,8},{10,11... | collective-permute-start | bytes 6291464 | tf_op jit(solution)/shard_map/ppermute | solution.py:24
  13.7 40.6 %collective-permute-done = bf16[128,8192]{1,0:T(8,128)(2,1)S(1)} collective-permute-done((bf16[128,8192]{1,0:T(8,128)(2,1)}, bf16[128,8192]{1,0:T(8,128)(2,1)S(1)}, u32[]{:S(2)}, u32[]{:S(2)}) %collective-permute-start) | collective-permute-done | bytes 2097184 | tf_op jit(solution)/shard_map/ppermute | solution.py:24
  54.3 0.5 fusion
  54.8 31.8 %all-gather.9.cloned.1.call-done = bf16[16,514,256]{2,1,0:T(8,128)(2,1)} async-done(((bf16[1,514,256]{2,1,0:T(8,128)(2,1)}), bf16[16,514,256]{2,1,0:T(8,128)(2,1)}) %all-gather.9.cloned.1.call-update) | async-done | bytes 4210704 | tf_op jit(solution)/shard_map/all_gather | solution.py:31
  86.7 1.0 slice_convert_fusion
  87.7 0.6 fusion.2
  88.3 0.6 copy-done.4
  88.9 0.7 fusion.20
  89.6 0.9 copy-done
  90.5 1.5 copy.40
  92.0 6.1 %all-to-all-start = ((bf16[128,16,512]{2,0,1:T(8,128)(2,1)}), bf16[128,16,512]{2,0,1:T(8,128)(2,1)}, u32[]{:S(2)}, u32[]{:S(2)}) async-start(bf16[128,16,512]{2,0,1:T(8,128)(2,1)} %bitcast.64), calls=%async_computation | async-start | bytes 4194304 | tf_op jit(solution)/shard_map/all_to_all | solution.py:52
  98.1 0.0 all-gather.7.cloned.1.call-start
  98.2 0.8 copy.23
  99.0 0.5 multiply_reduce_fusion.1
  99.5 3.1 %collective-permute-start.1 = (f32[128,256]{1,0:T(8,128)S(1)}, f32[128,256]{1,0:T(8,128)S(1)}, u32[]{:S(2)}, u32[]{:S(2)}) collective-permute-start(f32[128,256]{1,0:T(8,128)S(1)} %fusion.20), channel_id=1, source_target_pairs={{0,1},{1,0},{2,3},{3,2},{4,5},{5,4},{6,7},{7,6},{8,9},{9,8},{10,11... | collective-permute-start | bytes 393224 | tf_op jit(solution)/shard_map/ppermute | solution.py:44
  102.7 0.0 copy-start.2
  102.7 0.0 copy-start.1
  102.7 5.2 %fusion.15 = f32[128,256]{1,0:T(8,128)S(1)} fusion(bf16[16,514,256]{2,1,0:T(8,128)(2,1)} %all-gather.9.cloned.1.call-done, f32[128,16,512]{2,1,0:T(8,128)S(1)} %bitcast.65, f32[16,512]{1,0:T(8,128)S(1)} %bitcast.73, f32[128]{0:T(128)S(1)} %get-tuple-element.49), kind=kOutput, calls=%fused_computation.25 | convolution fusion | flops 540016640 | bytes 8552960 | tf_op jit(solution)/shard_map/tfr,frh->th/dot_general | solution.py:38
  107.8 0.0 collective-permute-done.1
  107.9 0.0 copy-done.2
  107.9 0.7 fusion.27
  108.6 0.0 all-gather.7.cloned.1.call-update
  108.6 0.0 copy-done.1
  108.6 0.2 copy.18
  108.8 0.6 compare_reduce_fusion.1
  109.5 0.6 compare_reduce_fusion
  110.1 110.5 %all-gather.3 = f32[16,1,128]{2,1,0:T(1,128)S(1)} all-gather(f32[1,1,128]{2,1,0:T(1,128)S(1)} %get-tuple-element.48), channel_id=3, replica_groups=mesh['template'=16,'fsdp'=16,'dp'=2] {'fsdp'}, dimensions={0}, use_global_device_ids=true | all-gather | bytes 8704 | tf_op jit(solution)/shard_map/all_gather | solution.py:53
  220.6 2.5 all-gather.7.cloned.1.call-done
  223.1 0.0 all-to-all-done
  223.1 3.8 %multiply_reduce_fusion = f32[512]{0:T(512)S(1)} fusion(bf16[128,16,512]{2,0,1:T(8,128)(2,1)} %all-to-all-done, bf16[2048,512]{1,0:T(8,128)(2,1)} %all-gather.7.cloned.1.call-done, f32[2048]{0:T(1024)S(1)} %bitcast.71, bf16[1,512,512]{2,1,0:T(8,128)(2,1)S(1)} %copy-done.1), kind=kOutput, calls=%fused_computation.9 | convolution fusion | flops 1080032768 | bytes 4728832 | tf_op jit(solution)/shard_map/th,dh->td/dot_general | solution.py:61
  227.0 1.4 broadcast_select_fusion.2
  228.4 0.1 scatter.11
  228.4 2.3 multiply_convert_fusion.1
  230.7 0.0 copy-done.5
  230.7 1.3 convert_multiply_fusion.2
  232.0 0.2 pad_maximum_fusion
  232.2 2.0 copy.19
  234.2 43.5 %all_to_all.23 = f32[32,16,1152]{2,1,0:T(8,128)S(1)} all-to-all(f32[32,16,1152]{2,1,0:T(8,128)} %bitcast.63), channel_id=1, replica_groups=mesh['template'=16,'fsdp'=16,'dp'=2] {'dp','template'}, dimensions={0} | all-to-all | bytes 4718592 | tf_op jit(solution)/shard_map/all_to_all | solution.py:70
  277.8 0.1 reduce_sum.42
  277.9 0.6 fusion.28
  278.6 16.6 %all_to_all.24 = f32[16,16,640]{2,1,0:T(8,128)S(1)} all-to-all(f32[16,16,640]{2,1,0:T(8,128)S(1)} %broadcast_in_dim.2), channel_id=1, replica_groups=mesh['template'=16,'fsdp'=16,'dp'=2] {'template'}, dimensions={0} | all-to-all | bytes 1310720 | tf_op jit(solution)/shard_map/all_to_all | solution.py:74
  295.2 0.9 slice.81
  296.1 0.7 slice_reduce_fusion
  (15 shorter events, 0.2 us)
Async XLA Ops:
  7.2 79.5 %all-gather.9.cloned.1.call-start = ((), (), s32[]{:S(2)}) async-start(), calls=%async_computation.4 | async-start | bytes 4526080 | tf_op jit(solution)/shard_map/all_gather | solution.py:31
  9.7 44.6 %collective-permute-start = (bf16[128,8192]{1,0:T(8,128)(2,1)}, bf16[128,8192]{1,0:T(8,128)(2,1)S(1)}, u32[]{:S(2)}, u32[]{:S(2)}) collective-permute-start(bf16[128,8192]{1,0:T(8,128)(2,1)} %bitcast.60), channel_id=1, source_target_pairs={{0,1},{1,0},{2,3},{3,2},{4,5},{5,4},{6,7},{7,6},{8,9},{9,8},{10,11... | collective-permute-start | bytes 6291464 | tf_op jit(solution)/shard_map/ppermute | solution.py:24
  86.7 2.2 copy-start.4
  88.9 1.6 copy-start
  92.0 131.1 %all-to-all-start = ((bf16[128,16,512]{2,0,1:T(8,128)(2,1)}), bf16[128,16,512]{2,0,1:T(8,128)(2,1)}, u32[]{:S(2)}, u32[]{:S(2)}) async-start(bf16[128,16,512]{2,0,1:T(8,128)(2,1)} %bitcast.64), calls=%async_computation | async-start | bytes 4194304 | tf_op jit(solution)/shard_map/all_to_all | solution.py:52
  98.1 125.0 %all-gather.7.cloned.1.call-start = ((), (), s32[]{:S(2)}) async-start(), calls=%async_computation.3 | async-start | bytes 2228224 | tf_op jit(solution)/shard_map/all_gather | solution.py:54
  99.5 8.3 %collective-permute-start.1 = (f32[128,256]{1,0:T(8,128)S(1)}, f32[128,256]{1,0:T(8,128)S(1)}, u32[]{:S(2)}, u32[]{:S(2)}) collective-permute-start(f32[128,256]{1,0:T(8,128)S(1)} %fusion.20), channel_id=1, source_target_pairs={{0,1},{1,0},{2,3},{3,2},{4,5},{5,4},{6,7},{7,6},{8,9},{9,8},{10,11... | collective-permute-start | bytes 393224 | tf_op jit(solution)/shard_map/ppermute | solution.py:44
  102.7 5.2 %copy-start.2 = (bf16[1,128,512]{2,1,0:T(8,128)(2,1)S(1)}, bf16[1,128,512]{2,1,0:T(8,128)(2,1)}, u32[]{:S(2)}) copy-start(bf16[1,128,512]{2,1,0:T(8,128)(2,1)} %param.11) | copy-start | bytes 393220
  102.7 5.9 %copy-start.1 = (bf16[1,512,512]{2,1,0:T(8,128)(2,1)S(1)}, bf16[1,512,512]{2,1,0:T(8,128)(2,1)}, u32[]{:S(2)}) copy-start(bf16[1,512,512]{2,1,0:T(8,128)(2,1)} %param.12) | copy-start | bytes 1572868
  223.1 3.9 %copy-start.3 = (bf16[1,512]{1,0:T(2,128)(2,1)S(1)}, bf16[1,512]{1,0:T(2,128)(2,1)}, u32[]{:S(2)}) copy-start(bf16[1,512]{1,0:T(2,128)(2,1)} %param.13) | copy-start | bytes 3076
  227.0 3.8 %copy-start.5 = (bf16[2048,512]{1,0:T(8,128)(2,1)S(1)}, bf16[2048,512]{1,0:T(8,128)(2,1)}, u32[]{:S(2)}) copy-start(bf16[2048,512]{1,0:T(8,128)(2,1)} %all-gather.7.cloned.1.call-done) | copy-start | bytes 6291460
Sparse Core Ops, SparseCore 0:
  10.7 75.9 all-gather.8
  108.7 114.3 all-gather.6

commit v13 on v12

--- a/solution.py
+++ b/solution.py
@@ -48,8 +48,10 @@
     values = jnp.concatenate([first, second], axis=1) * scale
     delta = (values - goal.astype(jnp.float32)).astype(jnp.bfloat16)
 
-    late_batch, _ = lax.optimization_barrier((token_batch, theirs_half))
-    local_hidden = lax.all_to_all(late_batch, "fsdp", 1, 0, tiled=True)
+    n_f = lax.axis_size("fsdp")
+    by_dest = jnp.transpose(token_batch.reshape(token_batch.shape[0], n_f, rows), (1, 0, 2))
+    late_batch, _ = lax.optimization_barrier((by_dest, theirs_half))
+    local_hidden = lax.all_to_all(late_batch, "fsdp", 0, 0, tiled=True).reshape(-1, rows)
     local_ratio = lax.all_gather(ratio, "fsdp", axis=0, tiled=True)
     local_delta = lax.all_gather(delta, "fsdp", axis=0, tiled=True)
     local_xhat = local_hidden.astype(jnp.float32) * local_ratio

time: 304 us -> 302 us (level)
  waiting for transfers between devices: 75 us -> 68.4 us
  local copies, waits for them, and re-layouts: 8.76 us -> 12 us
    ppermute x1, waiting for transfers between devices: 40.6 us -> 34.3 us  [body(): other_hidden = lax.ppermute(token_batch, 'dp', swap)]
  transfers between devices with their start and end apart: 5 -> 5, of which waited for: 3 -> 3; matrix products, arithmetic and copies ran while one was open for 3% -> 5% of each run, Pallas kernels for 0% -> 0%
where the time goes in v13:
time: 302 us; the launch traced here: 301 us
  blocking collectives  172 us (57%)
  waiting for transfers between devices  68.4 us (23%)
  between operations  14.3 us (5%)
  matrix products  13.4 us (4%)
  starting transfers between devices  13.3 us (4%)
  local copies, waits for them, and re-layouts  12 us (4%)
  other arithmetic  8.25 us (3%)
    all_gather x1, blocking collectives, body(): local_ratio = lax.all_gather(ratio, 'fsdp', axis=0, tiled=True)  111 us
    all_to_all x1, blocking collectives, body(): parts = lax.all_to_all(pack, ('dp', 'template'), 0, 0, tiled=True)  43.6 us
    ppermute x1, waiting for transfers between devices, body(): other_hidden = lax.ppermute(token_batch, 'dp', swap)  34.3 us
    all_gather x1, waiting for transfers between devices, body(): gathered = lax.all_gather(w_ext, 'fsdp', axis=0, tiled=False)  31.8 us
    all_to_all x1, blocking collectives, body(): lax.all_to_all(jnp.broadcast_to(done[None], (n_t,) + done.shape), 'templa...  16.6 us
    all_to_all x1, starting transfers between devices, body(): lax.all_to_all(late_batch, 'fsdp', 0, 0, tiled=True).reshape(-1, rows)  6.22 us
  transfers between devices with their start and end apart: 5, of which 3 were waited for; matrix products, arithmetic and copies ran while one was open for 5% of the time, Pallas kernels for 0%

profile of v13, /device:TPU:1, one launch (start us, length us, event | category | flops | bytes accessed | tf_op | source)
XLA Modules:
  0.0 301.3 jit_solution(15434402891482876748)
XLA Ops:
  7.2 0.0 all-gather.9.cloned.1.call-start
  7.2 0.8 fusion.35
  8.0 1.0 dynamic-slice_bitcast_fusion
  9.0 0.7 maximum_bitcast_fusion
  9.7 0.0 all-gather.9.cloned.1.call-update
  9.7 4.0 %collective-permute-start = (bf16[128,8192]{1,0:T(8,128)(2,1)}, bf16[128,8192]{1,0:T(8,128)(2,1)S(1)}, u32[]{:S(2)}, u32[]{:S(2)}) collective-permute-start(bf16[128,8192]{1,0:T(8,128)(2,1)} %bitcast.50), channel_id=1, source_target_pairs={{0,1},{1,0},{2,3},{3,2},{4,5},{5,4},{6,7},{7,6},{8,9},{9,8},{10,11... | collective-permute-start | bytes 6291464 | tf_op jit(solution)/shard_map/ppermute | solution.py:24
  13.7 2.4 copy.21
  16.1 0.0 copy-start.1
  16.1 1.3 copy-done.1
  17.5 2.5 copy.37
  20.0 34.3 %collective-permute-done = bf16[128,8192]{1,0:T(8,128)(2,1)S(1)} collective-permute-done((bf16[128,8192]{1,0:T(8,128)(2,1)}, bf16[128,8192]{1,0:T(8,128)(2,1)S(1)}, u32[]{:S(2)}, u32[]{:S(2)}) %collective-permute-start) | collective-permute-done | bytes 2097184 | tf_op jit(solution)/shard_map/ppermute | solution.py:24
  54.3 0.5 fusion
  54.8 31.8 %all-gather.9.cloned.1.call-done = bf16[16,514,256]{2,1,0:T(8,128)(2,1)} async-done(((bf16[1,514,256]{2,1,0:T(8,128)(2,1)}), bf16[16,514,256]{2,1,0:T(8,128)(2,1)}) %all-gather.9.cloned.1.call-update) | async-done | bytes 4210704 | tf_op jit(solution)/shard_map/all_gather | solution.py:31
  86.7 1.0 slice_convert_fusion
  87.7 0.6 fusion.2
  88.3 0.6 copy-done.5
  88.9 0.7 fusion.24
  89.6 0.0 copy-start
  89.6 6.2 %all-to-all-start = ((bf16[16,128,512]{2,1,0:T(8,128)(2,1)}), bf16[16,128,512]{2,1,0:T(8,128)(2,1)}, u32[]{:S(2)}, u32[]{:S(2)}) async-start(bf16[16,128,512]{2,1,0:T(8,128)(2,1)} %bitcast.52), calls=%async_computation | async-start | bytes 4194304 | tf_op jit(solution)/shard_map/all_to_all | solution.py:54
  95.9 0.0 all-gather.7.cloned.1.call-start
  95.9 0.0 copy-done
  95.9 0.5 multiply_reduce_fusion
  96.4 3.1 %collective-permute-start.1 = (f32[128,256]{1,0:T(8,128)S(1)}, f32[128,256]{1,0:T(8,128)S(1)}, u32[]{:S(2)}, u32[]{:S(2)}) collective-permute-start(f32[128,256]{1,0:T(8,128)S(1)} %fusion.24), channel_id=1, source_target_pairs={{0,1},{1,0},{2,3},{3,2},{4,5},{5,4},{6,7},{7,6},{8,9},{9,8},{10,11... | collective-permute-start | bytes 393224 | tf_op jit(solution)/shard_map/ppermute | solution.py:44
  99.6 0.0 copy-start.3
  99.6 0.0 copy-start.2
  99.6 5.5 %fusion.21 = f32[128,256]{1,0:T(8,128)S(1)} fusion(bf16[16,514,256]{2,1,0:T(8,128)(2,1)} %all-gather.9.cloned.1.call-done, f32[16,512]{1,0:T(8,128)S(1)} %bitcast.60, f32[128]{0:T(128)S(1)} %get-tuple-element.49, bf16[128,16,512]{2,1,0:T(8,128)(2,1)} %bitcast.54), kind=kOutput, calls=%fused_computation.29 | convolution fusion | flops 541065216 | bytes 6455808 | tf_op jit(solution)/shard_map/tfr,frh->th/dot_general | solution.py:38
  105.1 0.0 collective-permute-done.1
  105.1 0.0 copy-done.3
  105.1 0.7 fusion.31
  105.8 0.0 all-gather.7.cloned.1.call-update
  105.8 0.2 copy.18
  106.1 0.6 compare_reduce_fusion.1
  106.7 0.6 compare_reduce_fusion
  107.3 111.4 %all-gather.3 = f32[16,1,128]{2,1,0:T(1,128)S(1)} all-gather(f32[1,1,128]{2,1,0:T(1,128)S(1)} %get-tuple-element.48), channel_id=3, replica_groups=mesh['template'=16,'fsdp'=16,'dp'=2] {'fsdp'}, dimensions={0}, use_global_device_ids=true | all-gather | bytes 8704 | tf_op jit(solution)/shard_map/all_gather | solution.py:55
  218.7 2.2 all-gather.7.cloned.1.call-done
  220.9 0.0 all-to-all-done
  220.9 4.0 %fusion.7 = f32[512]{0:T(512)S(1)} fusion(bf16[2048,512]{1,0:T(8,128)(2,1)} %bitcast.16, bf16[2048,512]{1,0:T(8,128)(2,1)} %all-gather.7.cloned.1.call-done, f32[2048]{0:T(1024)S(1)} %bitcast.61, bf16[1,512,512]{2,1,0:T(8,128)(2,1)S(1)} %copy-done.2), kind=kOutput, calls=%fused_computation.10 | convolution fusion | flops 1080032768 | bytes 4728832 | tf_op jit(solution)/shard_map/th,dh->td/dot_general | solution.py:63
  224.9 1.2 broadcast_select_fusion.2
  226.1 0.2 scatter.11
  226.4 3.3 %convert_multiply_fusion.3 = (f32[512,512]{0,1:T(8,128)S(1)}, f32[512,512]{0,1:T(8,128)S(1)}) fusion(bf16[1,512,512]{1,2,0:T(8,128)(2,1)S(1)} %copy.18, bf16[2048,512]{1,0:T(8,128)(2,1)S(1)} %copy-done.6, bf16[2048,512]{1,0:T(8,128)(2,1)} %bitcast.16, f32[2048]{0:T(1024)S(1)} %bitcast.62, f32[512]{0:T(512)S(1)} %bitcast.63), kind=kOutput, calls=%fused_computation.31 | convolution fusion | flops 1084751872 | bytes 6825984 | tf_op jit(solution)/shard_map/td,th->dh/dot_general | solution.py:62
  229.7 0.2 pad_maximum_fusion
  229.9 2.0 copy.19
  231.9 43.6 %all_to_all.15 = f32[32,16,1152]{2,1,0:T(8,128)S(1)} all-to-all(f32[32,16,1152]{2,1,0:T(8,128)} %bitcast.49), channel_id=1, replica_groups=mesh['template'=16,'fsdp'=16,'dp'=2] {'dp','template'}, dimensions={0} | all-to-all | bytes 4718592 | tf_op jit(solution)/shard_map/all_to_all | solution.py:72
  275.5 0.1 reduce_sum.42
  275.6 0.6 fusion.32
  276.3 16.6 %all_to_all.16 = f32[16,16,640]{2,1,0:T(8,128)S(1)} all-to-all(f32[16,16,640]{2,1,0:T(8,128)S(1)} %broadcast_in_dim.2), channel_id=1, replica_groups=mesh['template'=16,'fsdp'=16,'dp'=2] {'template'}, dimensions={0} | all-to-all | bytes 1310720 | tf_op jit(solution)/shard_map/all_to_all | solution.py:76
  293.0 0.9 slice.81
  293.8 0.7 slice_reduce_fusion
  (16 shorter events, 0.2 us)
Async XLA Ops:
  7.2 79.5 %all-gather.9.cloned.1.call-start = ((), (), s32[]{:S(2)}) async-start(), calls=%async_computation.4 | async-start | bytes 4526080 | tf_op jit(solution)/shard_map/all_gather | solution.py:31
  9.7 44.6 %collective-permute-start = (bf16[128,8192]{1,0:T(8,128)(2,1)}, bf16[128,8192]{1,0:T(8,128)(2,1)S(1)}, u32[]{:S(2)}, u32[]{:S(2)}) collective-permute-start(bf16[128,8192]{1,0:T(8,128)(2,1)} %bitcast.50), channel_id=1, source_target_pairs={{0,1},{1,0},{2,3},{3,2},{4,5},{5,4},{6,7},{7,6},{8,9},{9,8},{10,11... | collective-permute-start | bytes 6291464 | tf_op jit(solution)/shard_map/ppermute | solution.py:24
  16.1 1.4 copy-start.1
  86.7 2.2 copy-start.5
  89.6 6.3 %copy-start = (bf16[1,128,8192]{2,1,0:T(8,128)(2,1)S(1)}, bf16[1,128,8192]{2,1,0:T(8,128)(2,1)}, u32[]{:S(2)}) copy-start(bf16[1,128,8192]{2,1,0:T(8,128)(2,1)} %param.10) | copy-start | bytes 6291460
  89.6 131.3 %all-to-all-start = ((bf16[16,128,512]{2,1,0:T(8,128)(2,1)}), bf16[16,128,512]{2,1,0:T(8,128)(2,1)}, u32[]{:S(2)}, u32[]{:S(2)}) async-start(bf16[16,128,512]{2,1,0:T(8,128)(2,1)} %bitcast.52), calls=%async_computation | async-start | bytes 4194304 | tf_op jit(solution)/shard_map/all_to_all | solution.py:54
  95.9 125.0 %all-gather.7.cloned.1.call-start = ((), (), s32[]{:S(2)}) async-start(), calls=%async_computation.3 | async-start | bytes 2228224 | tf_op jit(solution)/shard_map/all_gather | solution.py:56
  96.4 8.6 %collective-permute-start.1 = (f32[128,256]{1,0:T(8,128)S(1)}, f32[128,256]{1,0:T(8,128)S(1)}, u32[]{:S(2)}, u32[]{:S(2)}) collective-permute-start(f32[128,256]{1,0:T(8,128)S(1)} %fusion.24), channel_id=1, source_target_pairs={{0,1},{1,0},{2,3},{3,2},{4,5},{5,4},{6,7},{7,6},{8,9},{9,8},{10,11... | collective-permute-start | bytes 393224 | tf_op jit(solution)/shard_map/ppermute | solution.py:44
  99.6 5.6 %copy-start.3 = (bf16[1,128,512]{2,1,0:T(8,128)(2,1)S(1)}, bf16[1,128,512]{2,1,0:T(8,128)(2,1)}, u32[]{:S(2)}) copy-start(bf16[1,128,512]{2,1,0:T(8,128)(2,1)} %param.11) | copy-start | bytes 393220
  99.6 6.3 %copy-start.2 = (bf16[1,512,512]{2,1,0:T(8,128)(2,1)S(1)}, bf16[1,512,512]{2,1,0:T(8,128)(2,1)}, u32[]{:S(2)}) copy-start(bf16[1,512,512]{2,1,0:T(8,128)(2,1)} %param.12) | copy-start | bytes 1572868
  220.9 4.0 %copy-start.4 = (bf16[1,512]{1,0:T(2,128)(2,1)S(1)}, bf16[1,512]{1,0:T(2,128)(2,1)}, u32[]{:S(2)}) copy-start(bf16[1,512]{1,0:T(2,128)(2,1)} %param.13) | copy-start | bytes 3076
  220.9 5.5 %copy-start.6 = (bf16[2048,512]{1,0:T(8,128)(2,1)S(1)}, bf16[2048,512]{1,0:T(8,128)(2,1)}, u32[]{:S(2)}) copy-start(bf16[2048,512]{1,0:T(8,128)(2,1)} %all-gather.7.cloned.1.call-done) | copy-start | bytes 6291460
Sparse Core Ops, SparseCore 0:
  10.7 75.9 all-gather.8
  106.0 114.8 all-gather.6

commit v14 on v13

--- a/solution.py
+++ b/solution.py
@@ -26,7 +26,7 @@
     other_ratio = lax.rsqrt(jnp.mean(jnp.square(other_f), axis=1, keepdims=True) + 1e-05)
     half = heads // n_dp
     dp_at = lax.axis_index("dp")
-    w_cols = lax.dynamic_slice_in_dim(w_shard, dp_at * half, half, 1)
+    w_cols = jnp.where(dp_at == 0, w_shard[:, :half], w_shard[:, half:])
     w_ext = jnp.concatenate([w_cols, g_shard.reshape(-1, half)], axis=0)
     gathered = lax.all_gather(w_ext, "fsdp", axis=0, tiled=False)
     w_half = gathered[:, :rows, :]
@@ -63,8 +63,9 @@
     back = jnp.einsum("th,dh->td", local_delta, w_shard, preferred_element_type=jnp.float32) * scale
     gain_info = jnp.sum(jnp.square(back * local_xhat), axis=0)
 
-    extra = jnp.zeros((rows, 128), jnp.float32)
-    extra = extra.at[:, 0].set(gain_info * g_f).at[:, 1].set(gain_info)
+    extra = jnp.concatenate(
+        [(gain_info * g_f)[:, None], gain_info[:, None], jnp.zeros((rows, 126), jnp.float32)], axis=1
+    )
     pack = jnp.concatenate([fisher * w_shard.astype(jnp.float32), fisher, extra], axis=1)
     cols = pack.shape[1]
     piece = rows // (n_t * n_dp)

time: 302 us -> 303 us (level)
  blocking collectives: 172 us -> 130 us
  waiting for transfers between devices: 68.4 us -> 99.5 us
  starting transfers between devices: 13.3 us -> 25.8 us
    all_to_all x1 -> x0, blocking collectives: 43.6 us -> none  [body(): parts = lax.all_to_all(pack, ('dp', 'template'), 0, 0, tiled=True)]
    all_to_all x0 -> x1, waiting for transfers between devices: none -> 31.1 us  [body(): parts = lax.all_to_all(pack, ('dp', 'template'), 0, 0, tiled=True)]
    all_to_all x0 -> x1, starting transfers between devices: none -> 12.4 us  [body(): parts = lax.all_to_all(pack, ('dp', 'template'), 0, 0, tiled=True)]
  transfers between devices with their start and end apart: 5 -> 6, of which waited for: 3 -> 4; matrix products, arithmetic and copies ran while one was open for 5% -> 4% of each run, Pallas kernels for 0% -> 0%
where the time goes in v14:
time: 303 us
  blocking collectives  130 us (43%)
  waiting for transfers between devices  99.5 us (33%)
  starting transfers between devices  25.8 us (9%)
  between operations  14.3 us (5%)
  matrix products  13.8 us (5%)
  local copies, waits for them, and re-layouts  11.6 us (4%)
  other arithmetic  7.44 us (2%)
    all_gather x1, blocking collectives, body(): local_ratio = lax.all_gather(ratio, 'fsdp', axis=0, tiled=True)  113 us
    ppermute x1, waiting for transfers between devices, body(): other_hidden = lax.ppermute(token_batch, 'dp', swap)  34.3 us
    all_gather x1, waiting for transfers between devices, body(): gathered = lax.all_gather(w_ext, 'fsdp', axis=0, tiled=False)  31.7 us
    all_to_all x1, waiting for transfers between devices, body(): parts = lax.all_to_all(pack, ('dp', 'template'), 0, 0, tiled=True)  31.1 us
    all_to_all x1, blocking collectives, body(): lax.all_to_all(jnp.broadcast_to(done[None], (n_t,) + done.shape), 'templa...  17.8 us
    all_to_all x1, starting transfers between devices, body(): parts = lax.all_to_all(pack, ('dp', 'template'), 0, 0, tiled=True)  12.4 us
    all_to_all x1, starting transfers between devices, body(): lax.all_to_all(late_batch, 'fsdp', 0, 0, tiled=True).reshape(-1, rows)  6.22 us
  transfers between devices with their start and end apart: 6, of which 4 were waited for; matrix products, arithmetic and copies ran while one was open for 4% of the time, Pallas kernels for 0%

profile of v14, /device:TPU:1, one launch (start us, length us, event | category | flops | bytes accessed | tf_op | source)
XLA Modules:
  0.0 302.8 jit_solution(13098973714080095189)
XLA Ops:
  7.2 0.0 all-gather.9.cloned.1.call-start
  7.2 0.8 fusion.35
  8.0 1.1 slice_select_fusion
  9.1 0.7 maximum_bitcast_fusion
  9.8 0.0 all-gather.9.cloned.1.call-update
  9.8 4.0 %collective-permute-start = (bf16[128,8192]{1,0:T(8,128)(2,1)}, bf16[128,8192]{1,0:T(8,128)(2,1)S(1)}, u32[]{:S(2)}, u32[]{:S(2)}) collective-permute-start(bf16[128,8192]{1,0:T(8,128)(2,1)} %bitcast.42), channel_id=1, source_target_pairs={{0,1},{1,0},{2,3},{3,2},{4,5},{5,4},{6,7},{7,6},{8,9},{9,8},{10,11... | collective-permute-start | bytes 6291464 | tf_op jit(solution)/shard_map/ppermute | solution.py:24
  13.8 2.4 copy.21
  16.2 0.0 copy-start.1
  16.2 1.3 copy-done.1
  17.6 2.5 copy.37
  20.1 34.3 %collective-permute-done = bf16[128,8192]{1,0:T(8,128)(2,1)S(1)} collective-permute-done((bf16[128,8192]{1,0:T(8,128)(2,1)}, bf16[128,8192]{1,0:T(8,128)(2,1)S(1)}, u32[]{:S(2)}, u32[]{:S(2)}) %collective-permute-start) | collective-permute-done | bytes 2097184 | tf_op jit(solution)/shard_map/ppermute | solution.py:24
  54.4 0.5 fusion
  54.9 31.7 %all-gather.9.cloned.1.call-done = bf16[16,514,256]{2,1,0:T(8,128)(2,1)} async-done(((bf16[1,514,256]{2,1,0:T(8,128)(2,1)}), bf16[16,514,256]{2,1,0:T(8,128)(2,1)}) %all-gather.9.cloned.1.call-update) | async-done | bytes 4210704 | tf_op jit(solution)/shard_map/all_gather | solution.py:31
  86.7 1.0 slice_convert_fusion
  87.7 0.6 fusion.2
  88.4 0.5 copy-done.5
  88.9 0.7 fusion.24
  89.6 0.0 copy-start
  89.6 6.2 %all-to-all-start = ((bf16[16,128,512]{2,1,0:T(8,128)(2,1)}), bf16[16,128,512]{2,1,0:T(8,128)(2,1)}, u32[]{:S(2)}, u32[]{:S(2)}) async-start(bf16[16,128,512]{2,1,0:T(8,128)(2,1)} %bitcast.44), calls=%async_computation | async-start | bytes 4194304 | tf_op jit(solution)/shard_map/all_to_all | solution.py:54
  95.9 0.0 all-gather.7.cloned.1.call-start
  95.9 0.5 multiply_reduce_fusion
  96.4 3.1 %collective-permute-start.1 = (f32[128,256]{1,0:T(8,128)S(1)}, f32[128,256]{1,0:T(8,128)S(1)}, u32[]{:S(2)}, u32[]{:S(2)}) collective-permute-start(f32[128,256]{1,0:T(8,128)S(1)} %fusion.24), channel_id=1, source_target_pairs={{0,1},{1,0},{2,3},{3,2},{4,5},{5,4},{6,7},{7,6},{8,9},{9,8},{10,11... | collective-permute-start | bytes 393224 | tf_op jit(solution)/shard_map/ppermute | solution.py:44
  99.5 0.0 copy-start.3
  99.6 0.0 copy-start.4
  99.6 0.0 copy-start.2
  99.6 5.5 %fusion.21 = f32[128,256]{1,0:T(8,128)S(1)} fusion(bf16[16,514,256]{2,1,0:T(8,128)(2,1)} %all-gather.9.cloned.1.call-done, f32[16,512]{1,0:T(8,128)S(1)} %bitcast.55, f32[128]{0:T(128)S(1)} %get-tuple-element.23, bf16[128,16,512]{2,1,0:T(8,128)(2,1)} %bitcast.46), kind=kOutput, calls=%fused_computation.28 | convolution fusion | flops 541065216 | bytes 6455808 | tf_op jit(solution)/shard_map/tfr,frh->th/dot_general | solution.py:38
  105.1 0.0 collective-permute-done.1
  105.1 0.0 copy-done.3
  105.1 0.7 fusion.30
  105.8 0.0 all-gather.7.cloned.1.call-update
  105.9 0.1 reshape.132
  106.0 112.6 %all-gather.3 = f32[16,1,128]{2,1,0:T(1,128)S(1)} all-gather(f32[1,1,128]{2,1,0:T(1,128)S(1)} %get-tuple-element.22), channel_id=3, replica_groups=mesh['template'=16,'fsdp'=16,'dp'=2] {'fsdp'}, dimensions={0}, use_global_device_ids=true | all-gather | bytes 8704 | tf_op jit(solution)/shard_map/all_gather | solution.py:55
  218.6 2.3 all-gather.7.cloned.1.call-done
  220.8 0.0 all-to-all-done
  220.8 3.8 %fusion.7 = f32[512]{0:T(512)S(1)} fusion(bf16[2048,512]{1,0:T(8,128)(2,1)} %bitcast.14, bf16[2048,512]{1,0:T(8,128)(2,1)} %all-gather.7.cloned.1.call-done, f32[2048]{0:T(1024)S(1)} %bitcast.56, bf16[1,512,512]{2,1,0:T(8,128)(2,1)S(1)} %copy-done.2), kind=kOutput, calls=%fused_computation.10 | convolution fusion | flops 1080032768 | bytes 4728832 | tf_op jit(solution)/shard_map/th,dh->td/dot_general | solution.py:63
  224.7 0.1 reduce_sum.41
  224.8 0.3 copy.19
  225.0 0.3 copy.18
  225.3 3.8 %convert_multiply_fusion.3 = (f32[512,512]{1,0:T(8,128)S(1)}, f32[512,512]{1,0:T(8,128)S(1)}) fusion(bf16[1,512,512]{2,1,0:T(8,128)(2,1)S(1)} %copy-done.2, bf16[2048,512]{1,0:T(8,128)(2,1)} %all-gather.7.cloned.1.call-done, bf16[2048,512]{1,0:T(8,128)(2,1)} %bitcast.14, f32[2048]{0:T(1024)S(1)} %bitcast.57, f32[512]{0:T(512)S(1)} %bitcast.58), kind=kOutput, calls=%fused_computation.30 | convolution fusion | flops 1084751872 | bytes 6825984 | tf_op jit(solution)/shard_map/td,th->dh/dot_general | solution.py:62
  229.1 2.4 concatenate.23
  231.5 12.4 %all-to-all-start.1 = ((f32[32,16,1152]{2,1,0:T(8,128)}), f32[32,16,1152]{2,1,0:T(8,128)S(1)}, u32[]{:S(2)}, u32[]{:S(2)}) async-start(f32[32,16,1152]{2,1,0:T(8,128)} %concatenate.23), calls=%async_computation.1 | async-start | bytes 4718592 | tf_op jit(solution)/shard_map/all_to_all | solution.py:73
  244.0 0.6 compare_reduce_fusion
  244.6 31.1 %all-to-all-done.1 = f32[32,16,1152]{2,1,0:T(8,128)S(1)} async-done(((f32[32,16,1152]{2,1,0:T(8,128)}), f32[32,16,1152]{2,1,0:T(8,128)S(1)}, u32[]{:S(2)}, u32[]{:S(2)}) %all-to-all-start.1) | async-done | bytes 2359328 | tf_op jit(solution)/shard_map/all_to_all | solution.py:73
  275.7 0.1 reduce_sum.42
  275.8 0.7 fusion.31
  276.6 17.8 %all_to_all.15 = f32[16,16,640]{2,1,0:T(8,128)S(1)} all-to-all(f32[16,16,640]{2,1,0:T(8,128)S(1)} %broadcast_in_dim.5), channel_id=1, replica_groups=mesh['template'=16,'fsdp'=16,'dp'=2] {'template'}, dimensions={0} | all-to-all | bytes 1310720 | tf_op jit(solution)/shard_map/all_to_all | solution.py:77
  294.5 0.9 slice.62
  295.3 0.7 slice_reduce_fusion
  (16 shorter events, 0.2 us)
Async XLA Ops:
  7.2 79.5 %all-gather.9.cloned.1.call-start = ((), (), s32[]{:S(2)}) async-start(), calls=%async_computation.4 | async-start | bytes 4526080 | tf_op jit(solution)/shard_map/all_gather | solution.py:31
  9.8 44.6 %collective-permute-start = (bf16[128,8192]{1,0:T(8,128)(2,1)}, bf16[128,8192]{1,0:T(8,128)(2,1)S(1)}, u32[]{:S(2)}, u32[]{:S(2)}) collective-permute-start(bf16[128,8192]{1,0:T(8,128)(2,1)} %bitcast.42), channel_id=1, source_target_pairs={{0,1},{1,0},{2,3},{3,2},{4,5},{5,4},{6,7},{7,6},{8,9},{9,8},{10,11... | collective-permute-start | bytes 6291464 | tf_op jit(solution)/shard_map/ppermute | solution.py:24
  16.2 1.4 copy-start.1
  86.7 2.2 copy-start.5
  89.6 6.3 %copy-start = (bf16[1,128,8192]{2,1,0:T(8,128)(2,1)S(1)}, bf16[1,128,8192]{2,1,0:T(8,128)(2,1)}, u32[]{:S(2)}) copy-start(bf16[1,128,8192]{2,1,0:T(8,128)(2,1)} %param.6) | copy-start | bytes 6291460
  89.6 131.2 %all-to-all-start = ((bf16[16,128,512]{2,1,0:T(8,128)(2,1)}), bf16[16,128,512]{2,1,0:T(8,128)(2,1)}, u32[]{:S(2)}, u32[]{:S(2)}) async-start(bf16[16,128,512]{2,1,0:T(8,128)(2,1)} %bitcast.44), calls=%async_computation | async-start | bytes 4194304 | tf_op jit(solution)/shard_map/all_to_all | solution.py:54
  95.9 125.0 %all-gather.7.cloned.1.call-start = ((), (), s32[]{:S(2)}) async-start(), calls=%async_computation.3 | async-start | bytes 2228224 | tf_op jit(solution)/shard_map/all_gather | solution.py:56
  96.4 8.7 %collective-permute-start.1 = (f32[128,256]{1,0:T(8,128)S(1)}, f32[128,256]{1,0:T(8,128)S(1)}, u32[]{:S(2)}, u32[]{:S(2)}) collective-permute-start(f32[128,256]{1,0:T(8,128)S(1)} %fusion.24), channel_id=1, source_target_pairs={{0,1},{1,0},{2,3},{3,2},{4,5},{5,4},{6,7},{7,6},{8,9},{9,8},{10,11... | collective-permute-start | bytes 393224 | tf_op jit(solution)/shard_map/ppermute | solution.py:44
  99.5 5.6 %copy-start.3 = (bf16[1,128,512]{2,1,0:T(8,128)(2,1)S(1)}, bf16[1,128,512]{2,1,0:T(8,128)(2,1)}, u32[]{:S(2)}) copy-start(bf16[1,128,512]{2,1,0:T(8,128)(2,1)} %param.7) | copy-start | bytes 393220
  99.6 6.3 %copy-start.4 = (bf16[1,512]{1,0:T(2,128)(2,1)S(1)}, bf16[1,512]{1,0:T(2,128)(2,1)}, u32[]{:S(2)}) copy-start(bf16[1,512]{1,0:T(2,128)(2,1)} %param.9) | copy-start | bytes 3076
  99.6 121.3 %copy-start.2 = (bf16[1,512,512]{2,1,0:T(8,128)(2,1)S(1)}, bf16[1,512,512]{2,1,0:T(8,128)(2,1)}, u32[]{:S(2)}) copy-start(bf16[1,512,512]{2,1,0:T(8,128)(2,1)} %param.8) | copy-start | bytes 1572868
  231.5 44.2 %all-to-all-start.1 = ((f32[32,16,1152]{2,1,0:T(8,128)}), f32[32,16,1152]{2,1,0:T(8,128)S(1)}, u32[]{:S(2)}, u32[]{:S(2)}) async-start(f32[32,16,1152]{2,1,0:T(8,128)} %concatenate.23), calls=%async_computation.1 | async-start | bytes 4718592 | tf_op jit(solution)/shard_map/all_to_all | solution.py:73
Sparse Core Ops, SparseCore 0:
  10.7 75.9 all-gather.8
  106.0 114.8 all-gather.6

commit v15 on v13

--- a/solution.py
+++ b/solution.py
@@ -52,8 +52,17 @@
     by_dest = jnp.transpose(token_batch.reshape(token_batch.shape[0], n_f, rows), (1, 0, 2))
     late_batch, _ = lax.optimization_barrier((by_dest, theirs_half))
     local_hidden = lax.all_to_all(late_batch, "fsdp", 0, 0, tiled=True).reshape(-1, rows)
-    local_ratio = lax.all_gather(ratio, "fsdp", axis=0, tiled=True)
-    local_delta = lax.all_gather(delta, "fsdp", axis=0, tiled=True)
+    r_hi = ratio[:, 0].astype(jnp.bfloat16)
+    r_rest = ratio[:, 0] - r_hi.astype(jnp.float32)
+    r_mid = r_rest.astype(jnp.bfloat16)
+    r_lo = (r_rest - r_mid.astype(jnp.float32)).astype(jnp.bfloat16)
+    n_tok = delta.shape[0]
+    side = jnp.concatenate([r_hi, r_mid, r_lo, jnp.zeros((heads - 3 * n_tok,), jnp.bfloat16)])
+    side = jnp.concatenate([side[None, :], jnp.zeros((15, heads), jnp.bfloat16)], axis=0)
+    carried = lax.all_gather(jnp.concatenate([delta, side], axis=0), "fsdp", axis=0, tiled=False)
+    local_delta = carried[:, :n_tok, :].reshape(-1, heads)
+    parts = carried[:, n_tok, : 3 * n_tok].astype(jnp.float32).reshape(-1, 3, n_tok)
+    local_ratio = ((parts[:, 0] + parts[:, 1]) + parts[:, 2]).reshape(-1, 1)
     local_xhat = local_hidden.astype(jnp.float32) * local_ratio
     g_f = g_shard.astype(jnp.float32)
     local_normed = (local_xhat * g_f[None, :]).astype(jnp.bfloat16)

time: 302 us -> 307 us (1.017)
  waiting for transfers between devices: 68.4 us -> 184 us
  blocking collectives: 172 us -> 59.2 us
    all_gather x1, waiting for transfers between devices: 2.18 us -> 116 us  [body(): lax.all_gather(jnp.concatenate([delta, side], axis=0), 'fsdp', axis=0, ti...]
    all_gather x1 -> x0, blocking collectives: 111 us -> none  [body(): local_ratio = lax.all_gather(ratio, 'fsdp', axis=0, tiled=True)]
where the time goes in v15:
time: 307 us; the launch traced here: 306 us
  waiting for transfers between devices  184 us (60%)
  blocking collectives  59.2 us (19%)
  between operations  14.4 us (5%)
  starting transfers between devices  13.3 us (4%)
  matrix products  13.3 us (4%)
  local copies, waits for them, and re-layouts  12.5 us (4%)
  other arithmetic  9.4 us (3%)
    all_gather x1, waiting for transfers between devices, body(): lax.all_gather(jnp.concatenate([delta, side], axis=0), 'fsdp', axis=0, ti...  116 us
    all_to_all x1, blocking collectives, body(): parts = lax.all_to_all(pack, ('dp', 'template'), 0, 0, tiled=True)  42.6 us
    ppermute x1, waiting for transfers between devices, body(): other_hidden = lax.ppermute(token_batch, 'dp', swap)  35.7 us
    all_gather x1, waiting for transfers between devices, body(): gathered = lax.all_gather(w_ext, 'fsdp', axis=0, tiled=False)  31.8 us
    all_to_all x1, blocking collectives, body(): lax.all_to_all(jnp.broadcast_to(done[None], (n_t,) + done.shape), 'templa...  16.6 us
    all_to_all x1, starting transfers between devices, body(): lax.all_to_all(late_batch, 'fsdp', 0, 0, tiled=True).reshape(-1, rows)  6.22 us
  transfers between devices with their start and end apart: 5, of which 3 were waited for; matrix products, arithmetic and copies ran while one was open for 5% of the time, Pallas kernels for 0%

profile of v15, /device:TPU:1, one launch (start us, length us, event | category | flops | bytes accessed | tf_op | source)
XLA Modules:
  0.0 306.1 jit_solution(15643957758069955183)
XLA Ops:
  7.2 0.0 all-gather.8.cloned.1.call-start
  7.2 0.8 fusion.37
  8.0 1.0 dynamic-slice_bitcast_fusion
  9.0 0.7 maximum_bitcast_fusion
  9.7 0.0 all-gather.8.cloned.1.call-update
  9.7 4.0 %collective-permute-start = (bf16[128,8192]{1,0:T(8,128)(2,1)}, bf16[128,8192]{1,0:T(8,128)(2,1)S(1)}, u32[]{:S(2)}, u32[]{:S(2)}) collective-permute-start(bf16[128,8192]{1,0:T(8,128)(2,1)} %bitcast.59), channel_id=1, source_target_pairs={{0,1},{1,0},{2,3},{3,2},{4,5},{5,4},{6,7},{7,6},{8,9},{9,8},{10,11... | collective-permute-start | bytes 6291464 | tf_op jit(solution)/shard_map/ppermute | solution.py:24
  13.7 2.4 copy.28
  16.1 0.0 copy-start.1
  16.1 2.5 copy.44
  18.6 35.7 %collective-permute-done = bf16[128,8192]{1,0:T(8,128)(2,1)S(1)} collective-permute-done((bf16[128,8192]{1,0:T(8,128)(2,1)}, bf16[128,8192]{1,0:T(8,128)(2,1)S(1)}, u32[]{:S(2)}, u32[]{:S(2)}) %collective-permute-start) | collective-permute-done | bytes 2097184 | tf_op jit(solution)/shard_map/ppermute | solution.py:24
  54.3 0.5 fusion
  54.8 31.8 %all-gather.8.cloned.1.call-done = bf16[16,514,256]{2,1,0:T(8,128)(2,1)} async-done(((bf16[1,514,256]{2,1,0:T(8,128)(2,1)}), bf16[16,514,256]{2,1,0:T(8,128)(2,1)}) %all-gather.8.cloned.1.call-update) | async-done | bytes 4210704 | tf_op jit(solution)/shard_map/all_gather | solution.py:31
  86.7 1.0 slice_convert_fusion.1
  87.7 0.6 fusion.2
  88.4 0.5 copy-done.5
  88.9 0.7 fusion.22
  89.6 0.0 copy-start
  89.6 6.2 %all-to-all-start = ((bf16[16,128,512]{2,1,0:T(8,128)(2,1)}), bf16[16,128,512]{2,1,0:T(8,128)(2,1)}, u32[]{:S(2)}, u32[]{:S(2)}) async-start(bf16[16,128,512]{2,1,0:T(8,128)(2,1)} %bitcast.61), calls=%async_computation | async-start | bytes 4194304 | tf_op jit(solution)/shard_map/all_to_all | solution.py:54
  95.9 0.0 all-gather.6.cloned.1.call-start
  95.9 0.5 multiply_reduce_fusion
  96.5 0.1 pad.15.clone
  96.6 3.1 %collective-permute-start.1 = (f32[128,256]{1,0:T(8,128)S(1)}, f32[128,256]{1,0:T(8,128)S(1)}, u32[]{:S(2)}, u32[]{:S(2)}) collective-permute-start(f32[128,256]{1,0:T(8,128)S(1)} %fusion.22), channel_id=1, source_target_pairs={{0,1},{1,0},{2,3},{3,2},{4,5},{5,4},{6,7},{7,6},{8,9},{9,8},{10,11... | collective-permute-start | bytes 393224 | tf_op jit(solution)/shard_map/ppermute | solution.py:44
  99.7 0.0 copy-start.3
  99.7 0.0 copy-start.2
  99.7 5.5 %fusion.19 = f32[128,256]{1,0:T(8,128)S(1)} fusion(bf16[16,514,256]{2,1,0:T(8,128)(2,1)} %all-gather.8.cloned.1.call-done, f32[16,512]{1,0:T(8,128)S(1)} %bitcast.73, f32[128]{0:T(128)S(1)} %get-tuple-element.41, bf16[128,16,512]{2,1,0:T(8,128)(2,1)} %bitcast.63), kind=kOutput, calls=%fused_computation.29 | convolution fusion | flops 541065216 | bytes 6455808 | tf_op jit(solution)/shard_map/tfr,frh->th/dot_general | solution.py:38
  105.2 0.0 collective-permute-done.1
  105.3 0.8 maximum_maximum_fusion
  106.0 0.0 all-gather.6.cloned.1.call-update
  106.1 0.2 copy.24
  106.3 0.6 compare_reduce_fusion.1
  106.9 0.6 compare_reduce_fusion
  107.6 116.5 %all-gather.6.cloned.1.call-done = bf16[2304,512]{1,0:T(8,128)(2,1)} async-done(((bf16[144,512]{1,0:T(8,128)(2,1)}), bf16[2304,512]{1,0:T(8,128)(2,1)}) %all-gather.6.cloned.1.call-update) | async-done | bytes 2359312 | tf_op jit(solution)/shard_map/all_gather | solution.py:62
  224.1 1.8 slice.101
  225.8 1.0 fusion.31
  226.9 0.0 all-to-all-done
  226.9 0.0 copy-start.4
  226.9 3.2 %fusion.5 = f32[512]{0:T(512)S(1)} fusion(bf16[2048,512]{1,0:T(8,128)(2,1)S(1)} %bitcast.66, f32[2048]{0:T(1024)S(1)} %bitcast.74, bf16[16,128,512]{2,1,0:T(8,128)(2,1)} %all-to-all-done, bf16[1,512,512]{2,1,0:T(8,128)(2,1)S(1)} %copy-done.2), kind=kOutput, calls=%fused_computation.8 | convolution fusion | flops 1080032768 | bytes 4728832 | tf_op jit(solution)/shard_map/th,dh->td/dot_general | solution.py:72
  230.1 1.2 broadcast_select_fusion.2
  231.3 0.2 scatter.11
  231.6 3.9 %convert_multiply_fusion.2 = (f32[512,512]{0,1:T(8,128)S(1)}, f32[512,512]{0,1:T(8,128)S(1)}) fusion(bf16[1,512,512]{1,2,0:T(8,128)(2,1)S(1)} %copy.24, bf16[16,144,512]{2,1,0:T(8,128)(2,1)} %bitcast.70, f32[512]{0:T(512)S(1)} %bitcast.76, f32[16,128]{1,0:T(8,128)S(1)} %bitcast.75, bf16[16,128,512]{2,1,0:T(8,128)(2,1)} %all-to-all-done), kind=kOutput, calls=%fused_computation.31 | convolution fusion | flops 1084751872 | bytes 6825984 | tf_op jit(solution)/shard_map/td,th->dh/dot_general | solution.py:71
  235.5 0.2 pad_maximum_fusion
  235.7 2.0 copy.25
  237.7 42.6 %all_to_all.15 = f32[32,16,1152]{2,1,0:T(8,128)S(1)} all-to-all(f32[32,16,1152]{2,1,0:T(8,128)} %bitcast.58), channel_id=1, replica_groups=mesh['template'=16,'fsdp'=16,'dp'=2] {'dp','template'}, dimensions={0} | all-to-all | bytes 4718592 | tf_op jit(solution)/shard_map/all_to_all | solution.py:81
  280.3 0.1 reduce_sum.42
  280.4 0.6 fusion.32
  281.1 16.6 %all_to_all.16 = f32[16,16,640]{2,1,0:T(8,128)S(1)} all-to-all(f32[16,16,640]{2,1,0:T(8,128)S(1)} %broadcast_in_dim.11), channel_id=1, replica_groups=mesh['template'=16,'fsdp'=16,'dp'=2] {'template'}, dimensions={0} | all-to-all | bytes 1310720 | tf_op jit(solution)/shard_map/all_to_all | solution.py:85
  297.7 0.9 slice.106
  298.6 0.7 slice_reduce_fusion
  (24 shorter events, 0.3 us)
Async XLA Ops:
  7.2 79.5 %all-gather.8.cloned.1.call-start = ((), (), s32[]{:S(2)}) async-start(), calls=%async_computation.4 | async-start | bytes 4526080 | tf_op jit(solution)/shard_map/all_gather | solution.py:31
  9.7 44.6 %collective-permute-start = (bf16[128,8192]{1,0:T(8,128)(2,1)}, bf16[128,8192]{1,0:T(8,128)(2,1)S(1)}, u32[]{:S(2)}, u32[]{:S(2)}) collective-permute-start(bf16[128,8192]{1,0:T(8,128)(2,1)} %bitcast.59), channel_id=1, source_target_pairs={{0,1},{1,0},{2,3},{3,2},{4,5},{5,4},{6,7},{7,6},{8,9},{9,8},{10,11... | collective-permute-start | bytes 6291464 | tf_op jit(solution)/shard_map/ppermute | solution.py:24
  16.1 38.7 %copy-start.1 = (bf16[16,8,16,512]{3,2,1,0:T(8,128)(2,1)}, bf16[16,8,16,512]{3,2,1,0:T(8,128)(2,1)S(1)}, u32[]{:S(2)}) copy-start(bf16[16,8,16,512]{3,2,1,0:T(8,128)(2,1)S(1)} %copy.28) | copy-start | bytes 6291460
  86.7 2.2 copy-start.5
  89.6 6.3 %copy-start = (bf16[1,128,8192]{2,1,0:T(8,128)(2,1)S(1)}, bf16[1,128,8192]{2,1,0:T(8,128)(2,1)}, u32[]{:S(2)}) copy-start(bf16[1,128,8192]{2,1,0:T(8,128)(2,1)} %param.10) | copy-start | bytes 6291460
  89.6 137.2 %all-to-all-start = ((bf16[16,128,512]{2,1,0:T(8,128)(2,1)}), bf16[16,128,512]{2,1,0:T(8,128)(2,1)}, u32[]{:S(2)}, u32[]{:S(2)}) async-start(bf16[16,128,512]{2,1,0:T(8,128)(2,1)} %bitcast.61), calls=%async_computation | async-start | bytes 4194304 | tf_op jit(solution)/shard_map/all_to_all | solution.py:54
  95.9 128.2 %all-gather.6.cloned.1.call-start = ((), (), s32[]{:S(2)}) async-start(), calls=%async_computation.3 | async-start | bytes 2506752 | tf_op jit(solution)/shard_map/all_gather | solution.py:62
  96.6 8.6 %collective-permute-start.1 = (f32[128,256]{1,0:T(8,128)S(1)}, f32[128,256]{1,0:T(8,128)S(1)}, u32[]{:S(2)}, u32[]{:S(2)}) collective-permute-start(f32[128,256]{1,0:T(8,128)S(1)} %fusion.22), channel_id=1, source_target_pairs={{0,1},{1,0},{2,3},{3,2},{4,5},{5,4},{6,7},{7,6},{8,9},{9,8},{10,11... | collective-permute-start | bytes 393224 | tf_op jit(solution)/shard_map/ppermute | solution.py:44
  99.7 5.6 %copy-start.3 = (bf16[1,128,512]{2,1,0:T(8,128)(2,1)S(1)}, bf16[1,128,512]{2,1,0:T(8,128)(2,1)}, u32[]{:S(2)}) copy-start(bf16[1,128,512]{2,1,0:T(8,128)(2,1)} %param.11) | copy-start | bytes 393220
  99.7 6.4 %copy-start.2 = (bf16[1,512,512]{2,1,0:T(8,128)(2,1)S(1)}, bf16[1,512,512]{2,1,0:T(8,128)(2,1)}, u32[]{:S(2)}) copy-start(bf16[1,512,512]{2,1,0:T(8,128)(2,1)} %param.12) | copy-start | bytes 1572868
  226.9 3.2 %copy-start.4 = (bf16[1,512]{1,0:T(2,128)(2,1)S(1)}, bf16[1,512]{1,0:T(2,128)(2,1)}, u32[]{:S(2)}) copy-start(bf16[1,512]{1,0:T(2,128)(2,1)} %param.13) | copy-start | bytes 3076
Sparse Core Ops, SparseCore 0:
  10.7 75.9 all-gather.7
  106.2 117.8 all-gather.5

commit v16 on v13

--- a/solution.py
+++ b/solution.py
@@ -63,14 +63,25 @@
     back = jnp.einsum("th,dh->td", local_delta, w_shard, preferred_element_type=jnp.float32) * scale
     gain_info = jnp.sum(jnp.square(back * local_xhat), axis=0)
 
-    extra = jnp.zeros((rows, 128), jnp.float32)
-    extra = extra.at[:, 0].set(gain_info * g_f).at[:, 1].set(gain_info)
-    pack = jnp.concatenate([fisher * w_shard.astype(jnp.float32), fisher, extra], axis=1)
-    cols = pack.shape[1]
-    piece = rows // (n_t * n_dp)
-    pack = pack.reshape(n_t * n_dp, piece, cols)
+    n_pieces = n_t * n_dp
+    piece = rows // n_pieces
+    flat = piece * heads
+    pack = jnp.concatenate(
+        [
+            (fisher * w_shard.astype(jnp.float32)).reshape(n_pieces, flat),
+            fisher.reshape(n_pieces, flat),
+            (gain_info * g_f).reshape(n_pieces, piece),
+            gain_info.reshape(n_pieces, piece),
+            jnp.zeros((n_pieces, -(2 * piece) % 128), jnp.float32),
+        ],
+        axis=1,
+    )
     parts = lax.all_to_all(pack, ("dp", "template"), 0, 0, tiled=True)
-    total = jnp.sum(parts, axis=0)
+    sums = jnp.sum(parts, axis=0)
+    total = jnp.concatenate(
+        [sums[:flat].reshape(piece, heads), sums[flat : 2 * flat].reshape(piece, heads),
+         sums[2 * flat : 2 * flat + 2 * piece].reshape(2, piece).T], axis=1
+    )
     ratio_block = jnp.zeros((piece, 128), jnp.float32).at[:, 0].set(total[:, 2 * heads] / total[:, 2 * heads + 1])
     done = jnp.concatenate([total[:, :heads] / total[:, heads : 2 * heads], ratio_block], axis=1)
     spread = lax.all_to_all(jnp.broadcast_to(done[None], (n_t,) + done.shape), "template", 0, 0, tiled=True)

time: 302 us -> 305 us (level)
  blocking collectives: 172 us -> 130 us
  waiting for transfers between devices: 68.4 us -> 96.7 us
  starting transfers between devices: 13.3 us -> 25.7 us
  local copies, waits for them, and re-layouts: 12 us -> 16.1 us
    all_to_all x1 -> x0, blocking collectives: 43.6 us -> none  [body(): parts = lax.all_to_all(pack, ('dp', 'template'), 0, 0, tiled=True)]
    all_to_all x0 -> x1, waiting for transfers between devices: none -> 28.1 us  [body(): parts = lax.all_to_all(pack, ('dp', 'template'), 0, 0, tiled=True)]
    all_to_all x0 -> x1, starting transfers between devices: none -> 12.4 us  [body(): parts = lax.all_to_all(pack, ('dp', 'template'), 0, 0, tiled=True)]
  transfers between devices with their start and end apart: 5 -> 6, of which waited for: 3 -> 4; matrix products, arithmetic and copies ran while one was open for 5% -> 4% of each run, Pallas kernels for 0% -> 0%
where the time goes in v16:
time: 305 us; the launch traced here: 304 us
  blocking collectives  130 us (43%)
  waiting for transfers between devices  96.7 us (32%)
  starting transfers between devices  25.7 us (8%)
  local copies, waits for them, and re-layouts  16.1 us (5%)
  between operations  14.3 us (5%)
  matrix products  13.8 us (5%)
  other arithmetic  7.39 us (2%)
    all_gather x1, blocking collectives, body(): local_ratio = lax.all_gather(ratio, 'fsdp', axis=0, tiled=True)  113 us
    ppermute x1, waiting for transfers between devices, body(): other_hidden = lax.ppermute(token_batch, 'dp', swap)  34.3 us
    all_gather x1, waiting for transfers between devices, body(): gathered = lax.all_gather(w_ext, 'fsdp', axis=0, tiled=False)  31.8 us
    all_to_all x1, waiting for transfers between devices, body(): parts = lax.all_to_all(pack, ('dp', 'template'), 0, 0, tiled=True)  28.1 us
    all_to_all x1, blocking collectives, body(): lax.all_to_all(jnp.broadcast_to(done[None], (n_t,) + done.shape), 'templa...  17.7 us
    all_to_all x1, starting transfers between devices, body(): parts = lax.all_to_all(pack, ('dp', 'template'), 0, 0, tiled=True)  12.4 us
    all_to_all x1, starting transfers between devices, body(): lax.all_to_all(late_batch, 'fsdp', 0, 0, tiled=True).reshape(-1, rows)  6.22 us
  transfers between devices with their start and end apart: 6, of which 4 were waited for; matrix products, arithmetic and copies ran while one was open for 4% of the time, Pallas kernels for 0%

profile of v16, /device:TPU:1, one launch (start us, length us, event | category | flops | bytes accessed | tf_op | source)
XLA Modules:
  0.0 304.4 jit_solution(16682913711652332466)
XLA Ops:
  7.2 0.0 all-gather.9.cloned.1.call-start
  7.2 0.8 fusion.34
  8.0 1.0 dynamic-slice_bitcast_fusion
  9.0 0.7 maximum_bitcast_fusion
  9.7 0.0 all-gather.9.cloned.1.call-update
  9.7 4.0 %collective-permute-start = (bf16[128,8192]{1,0:T(8,128)(2,1)}, bf16[128,8192]{1,0:T(8,128)(2,1)S(1)}, u32[]{:S(2)}, u32[]{:S(2)}) collective-permute-start(bf16[128,8192]{1,0:T(8,128)(2,1)} %bitcast.43), channel_id=1, source_target_pairs={{0,1},{1,0},{2,3},{3,2},{4,5},{5,4},{6,7},{7,6},{8,9},{9,8},{10,11... | collective-permute-start | bytes 6291464 | tf_op jit(solution)/shard_map/ppermute | solution.py:24
  13.7 2.4 copy.20
  16.1 1.3 copy-done.1
  17.5 2.5 copy.36
  20.0 34.3 %collective-permute-done = bf16[128,8192]{1,0:T(8,128)(2,1)S(1)} collective-permute-done((bf16[128,8192]{1,0:T(8,128)(2,1)}, bf16[128,8192]{1,0:T(8,128)(2,1)S(1)}, u32[]{:S(2)}, u32[]{:S(2)}) %collective-permute-start) | collective-permute-done | bytes 2097184 | tf_op jit(solution)/shard_map/ppermute | solution.py:24
  54.3 0.5 fusion
  54.8 31.8 %all-gather.9.cloned.1.call-done = bf16[16,514,256]{2,1,0:T(8,128)(2,1)} async-done(((bf16[1,514,256]{2,1,0:T(8,128)(2,1)}), bf16[16,514,256]{2,1,0:T(8,128)(2,1)}) %all-gather.9.cloned.1.call-update) | async-done | bytes 4210704 | tf_op jit(solution)/shard_map/all_gather | solution.py:31
  86.7 1.0 slice_convert_fusion
  87.7 0.6 fusion.2
  88.4 0.5 copy-done.5
  88.9 0.7 fusion.24
  89.6 0.0 copy-start
  89.6 6.2 %all-to-all-start = ((bf16[16,128,512]{2,1,0:T(8,128)(2,1)}), bf16[16,128,512]{2,1,0:T(8,128)(2,1)}, u32[]{:S(2)}, u32[]{:S(2)}) async-start(bf16[16,128,512]{2,1,0:T(8,128)(2,1)} %bitcast.45), calls=%async_computation | async-start | bytes 4194304 | tf_op jit(solution)/shard_map/all_to_all | solution.py:54
  95.9 0.0 all-gather.7.cloned.1.call-start
  95.9 0.5 multiply_reduce_fusion
  96.4 3.1 %collective-permute-start.1 = (f32[128,256]{1,0:T(8,128)S(1)}, f32[128,256]{1,0:T(8,128)S(1)}, u32[]{:S(2)}, u32[]{:S(2)}) collective-permute-start(f32[128,256]{1,0:T(8,128)S(1)} %fusion.24), channel_id=1, source_target_pairs={{0,1},{1,0},{2,3},{3,2},{4,5},{5,4},{6,7},{7,6},{8,9},{9,8},{10,11... | collective-permute-start | bytes 393224 | tf_op jit(solution)/shard_map/ppermute | solution.py:44
  99.6 0.0 copy-start.3
  99.6 0.0 copy-start.4
  99.6 0.0 copy-start.2
  99.6 5.5 %fusion.21 = f32[128,256]{1,0:T(8,128)S(1)} fusion(bf16[16,514,256]{2,1,0:T(8,128)(2,1)} %all-gather.9.cloned.1.call-done, f32[16,512]{1,0:T(8,128)S(1)} %bitcast.53, f32[128]{0:T(128)S(1)} %get-tuple-element.23, bf16[128,16,512]{2,1,0:T(8,128)(2,1)} %bitcast.47), kind=kOutput, calls=%fused_computation.28 | convolution fusion | flops 541065216 | bytes 6455808 | tf_op jit(solution)/shard_map/tfr,frh->th/dot_general | solution.py:38
  105.1 0.0 collective-permute-done.1
  105.1 0.7 fusion.31
  105.8 0.0 all-gather.7.cloned.1.call-update
  105.9 0.1 reshape.133
  105.9 112.7 %all-gather.3 = f32[16,1,128]{2,1,0:T(1,128)S(1)} all-gather(f32[1,1,128]{2,1,0:T(1,128)S(1)} %get-tuple-element.22), channel_id=3, replica_groups=mesh['template'=16,'fsdp'=16,'dp'=2] {'fsdp'}, dimensions={0}, use_global_device_ids=true | all-gather | bytes 8704 | tf_op jit(solution)/shard_map/all_gather | solution.py:55
  218.6 2.3 all-gather.7.cloned.1.call-done
  220.9 3.8 %fusion.7 = f32[512]{0:T(512)S(1)} fusion(bf16[2048,512]{1,0:T(8,128)(2,1)} %bitcast.14, bf16[2048,512]{1,0:T(8,128)(2,1)} %all-gather.7.cloned.1.call-done, f32[2048]{0:T(1024)S(1)} %bitcast.54, bf16[1,512,512]{2,1,0:T(8,128)(2,1)S(1)} %copy-done.2), kind=kOutput, calls=%fused_computation.10 | convolution fusion | flops 1080032768 | bytes 4728832 | tf_op jit(solution)/shard_map/th,dh->td/dot_general | solution.py:63
  224.7 0.1 reduce_sum.41
  224.8 3.8 %convert_multiply_fusion.3 = (f32[512,512]{1,0:T(8,128)S(1)}, f32[512,512]{1,0:T(8,128)S(1)}) fusion(bf16[1,512,512]{2,1,0:T(8,128)(2,1)S(1)} %copy-done.2, bf16[2048,512]{1,0:T(8,128)(2,1)} %all-gather.7.cloned.1.call-done, bf16[2048,512]{1,0:T(8,128)(2,1)} %bitcast.14, f32[2048]{0:T(1024)S(1)} %bitcast.55, f32[512]{0:T(512)S(1)} %bitcast.56), kind=kOutput, calls=%fused_computation.30 | convolution fusion | flops 1084751872 | bytes 6825984 | tf_op jit(solution)/shard_map/td,th->dh/dot_general | solution.py:62
  228.6 0.2 reshape.124
  228.8 1.2 reshape.125
  230.0 2.2 concatenate.16
  232.2 2.8 all_to_all.13
  235.0 12.4 %all-to-all-start.1 = ((f32[32,1,16512]{2,1,0:T(1,128)}), f32[32,1,16512]{2,1,0:T(1,128)S(1)}, u32[]{:S(2)}, u32[]{:S(2)}) async-start(f32[32,1,16512]{2,1,0:T(1,128)} %all_to_all.13), calls=%async_computation.1 | async-start | bytes 4227072 | tf_op jit(solution)/shard_map/all_to_all | solution.py:79
  247.4 0.6 compare_reduce_fusion
  248.0 28.1 %all-to-all-done.1 = f32[32,1,16512]{2,1,0:T(1,128)S(1)} async-done(((f32[32,1,16512]{2,1,0:T(1,128)}), f32[32,1,16512]{2,1,0:T(1,128)S(1)}, u32[]{:S(2)}, u32[]{:S(2)}) %all-to-all-start.1) | async-done | bytes 2113568 | tf_op jit(solution)/shard_map/all_to_all | solution.py:79
  276.2 1.2 reduce_sum.42
  277.4 0.1 reshape.126
  277.5 0.7 broadcast_select_fusion.2
  278.2 0.1 copy.18
  278.3 17.7 %all_to_all.19 = f32[16,16,640]{2,1,0:T(8,128)S(1)} all-to-all(f32[16,16,640]{2,1,0:T(8,128)S(1)} %broadcast_in_dim.5), channel_id=1, replica_groups=mesh['template'=16,'fsdp'=16,'dp'=2] {'template'}, dimensions={0} | all-to-all | bytes 1310720 | tf_op jit(solution)/shard_map/all_to_all | solution.py:87
  296.0 0.9 slice.63
  296.9 0.7 slice_reduce_fusion
  (21 shorter events, 0.2 us)
Async XLA Ops:
  7.2 79.5 %all-gather.9.cloned.1.call-start = ((), (), s32[]{:S(2)}) async-start(), calls=%async_computation.4 | async-start | bytes 4526080 | tf_op jit(solution)/shard_map/all_gather | solution.py:31
  9.7 44.6 %collective-permute-start = (bf16[128,8192]{1,0:T(8,128)(2,1)}, bf16[128,8192]{1,0:T(8,128)(2,1)S(1)}, u32[]{:S(2)}, u32[]{:S(2)}) collective-permute-start(bf16[128,8192]{1,0:T(8,128)(2,1)} %bitcast.43), channel_id=1, source_target_pairs={{0,1},{1,0},{2,3},{3,2},{4,5},{5,4},{6,7},{7,6},{8,9},{9,8},{10,11... | collective-permute-start | bytes 6291464 | tf_op jit(solution)/shard_map/ppermute | solution.py:24
  16.1 1.4 copy-start.1
  86.7 2.2 copy-start.5
  89.6 6.3 %copy-start = (bf16[1,128,8192]{2,1,0:T(8,128)(2,1)S(1)}, bf16[1,128,8192]{2,1,0:T(8,128)(2,1)}, u32[]{:S(2)}) copy-start(bf16[1,128,8192]{2,1,0:T(8,128)(2,1)} %param.6) | copy-start | bytes 6291460
  89.6 131.3 %all-to-all-start = ((bf16[16,128,512]{2,1,0:T(8,128)(2,1)}), bf16[16,128,512]{2,1,0:T(8,128)(2,1)}, u32[]{:S(2)}, u32[]{:S(2)}) async-start(bf16[16,128,512]{2,1,0:T(8,128)(2,1)} %bitcast.45), calls=%async_computation | async-start | bytes 4194304 | tf_op jit(solution)/shard_map/all_to_all | solution.py:54
  95.9 125.0 %all-gather.7.cloned.1.call-start = ((), (), s32[]{:S(2)}) async-start(), calls=%async_computation.3 | async-start | bytes 2228224 | tf_op jit(solution)/shard_map/all_gather | solution.py:56
  96.4 8.6 %collective-permute-start.1 = (f32[128,256]{1,0:T(8,128)S(1)}, f32[128,256]{1,0:T(8,128)S(1)}, u32[]{:S(2)}, u32[]{:S(2)}) collective-permute-start(f32[128,256]{1,0:T(8,128)S(1)} %fusion.24), channel_id=1, source_target_pairs={{0,1},{1,0},{2,3},{3,2},{4,5},{5,4},{6,7},{7,6},{8,9},{9,8},{10,11... | collective-permute-start | bytes 393224 | tf_op jit(solution)/shard_map/ppermute | solution.py:44
  99.6 5.6 %copy-start.3 = (bf16[1,128,512]{2,1,0:T(8,128)(2,1)S(1)}, bf16[1,128,512]{2,1,0:T(8,128)(2,1)}, u32[]{:S(2)}) copy-start(bf16[1,128,512]{2,1,0:T(8,128)(2,1)} %param.7) | copy-start | bytes 393220
  99.6 6.3 %copy-start.4 = (bf16[1,512]{1,0:T(2,128)(2,1)S(1)}, bf16[1,512]{1,0:T(2,128)(2,1)}, u32[]{:S(2)}) copy-start(bf16[1,512]{1,0:T(2,128)(2,1)} %param.9) | copy-start | bytes 3076
  99.6 121.3 %copy-start.2 = (bf16[1,512,512]{2,1,0:T(8,128)(2,1)S(1)}, bf16[1,512,512]{2,1,0:T(8,128)(2,1)}, u32[]{:S(2)}) copy-start(bf16[1,512,512]{2,1,0:T(8,128)(2,1)} %param.8) | copy-start | bytes 1572868
  235.0 41.2 %all-to-all-start.1 = ((f32[32,1,16512]{2,1,0:T(1,128)}), f32[32,1,16512]{2,1,0:T(1,128)S(1)}, u32[]{:S(2)}, u32[]{:S(2)}) async-start(f32[32,1,16512]{2,1,0:T(1,128)} %all_to_all.13), calls=%async_computation.1 | async-start | bytes 4227072 | tf_op jit(solution)/shard_map/all_to_all | solution.py:79
Sparse Core Ops, SparseCore 0:
  10.7 75.9 all-gather.8
  106.0 114.8 all-gather.6

commit v17 on v13

--- a/solution.py
+++ b/solution.py
@@ -50,7 +50,7 @@
 
     n_f = lax.axis_size("fsdp")
     by_dest = jnp.transpose(token_batch.reshape(token_batch.shape[0], n_f, rows), (1, 0, 2))
-    late_batch, _ = lax.optimization_barrier((by_dest, theirs_half))
+    late_batch, _ = lax.optimization_barrier((by_dest, other_normed))
     local_hidden = lax.all_to_all(late_batch, "fsdp", 0, 0, tiled=True).reshape(-1, rows)
     local_ratio = lax.all_gather(ratio, "fsdp", axis=0, tiled=True)
     local_delta = lax.all_gather(delta, "fsdp", axis=0, tiled=True)

time: 302 us -> 303 us (level)
  other arithmetic: 8.25 us -> 11.3 us
    convert_element_type x1, other arithmetic: 0.58 us -> 3.63 us  [body(): (other_f * other_ratio * g_full[None, :]).astype(jnp.bfloat16)]
where the time goes in v17:
time: 303 us
  blocking collectives  169 us (56%)
  waiting for transfers between devices  68.1 us (22%)
  between operations  14.3 us (5%)
  matrix products  14 us (5%)
  starting transfers between devices  13.2 us (4%)
  local copies, waits for them, and re-layouts  12.7 us (4%)
  other arithmetic  11.3 us (4%)
    all_gather x1, blocking collectives, body(): local_ratio = lax.all_gather(ratio, 'fsdp', axis=0, tiled=True)  110 us
    all_to_all x1, blocking collectives, body(): parts = lax.all_to_all(pack, ('dp', 'template'), 0, 0, tiled=True)  42.7 us
    ppermute x1, waiting for transfers between devices, body(): other_hidden = lax.ppermute(token_batch, 'dp', swap)  34.4 us
    all_gather x1, waiting for transfers between devices, body(): gathered = lax.all_gather(w_ext, 'fsdp', axis=0, tiled=False)  30.5 us
    all_to_all x1, blocking collectives, body(): lax.all_to_all(jnp.broadcast_to(done[None], (n_t,) + done.shape), 'templa...  16.6 us
    all_to_all x1, starting transfers between devices, body(): lax.all_to_all(late_batch, 'fsdp', 0, 0, tiled=True).reshape(-1, rows)  6.08 us
  transfers between devices with their start and end apart: 5, of which 3 were waited for; matrix products, arithmetic and copies ran while one was open for 5% of the time, Pallas kernels for 0%

profile of v17, /device:TPU:1, one launch (start us, length us, event | category | flops | bytes accessed | tf_op | source)
XLA Modules:
  0.0 302.9 jit_solution(13930834446381041680)
XLA Ops:
  7.2 0.0 all-gather.9.cloned.1.call-start
  7.2 0.8 fusion.35
  8.0 1.0 dynamic-slice_bitcast_fusion
  9.0 0.7 maximum_bitcast_fusion
  9.7 0.0 all-gather.9.cloned.1.call-update
  9.7 4.0 %collective-permute-start = (bf16[128,8192]{1,0:T(8,128)(2,1)}, bf16[128,8192]{1,0:T(8,128)(2,1)S(1)}, u32[]{:S(2)}, u32[]{:S(2)}) collective-permute-start(bf16[128,8192]{1,0:T(8,128)(2,1)} %bitcast.50), channel_id=1, source_target_pairs={{0,1},{1,0},{2,3},{3,2},{4,5},{5,4},{6,7},{7,6},{8,9},{9,8},{10,11... | collective-permute-start | bytes 6291464 | tf_op jit(solution)/shard_map/ppermute | solution.py:24
  13.7 2.4 copy.21
  16.1 1.3 copy-done.1
  17.5 2.5 copy.37
  20.0 34.4 %collective-permute-done = bf16[128,8192]{1,0:T(8,128)(2,1)S(1)} collective-permute-done((bf16[128,8192]{1,0:T(8,128)(2,1)}, bf16[128,8192]{1,0:T(8,128)(2,1)S(1)}, u32[]{:S(2)}, u32[]{:S(2)}) %collective-permute-start) | collective-permute-done | bytes 2097184 | tf_op jit(solution)/shard_map/ppermute | solution.py:24
  54.3 1.3 copy-done.3
  55.7 0.5 fusion
  56.2 30.5 %all-gather.9.cloned.1.call-done = bf16[16,514,256]{2,1,0:T(8,128)(2,1)} async-done(((bf16[1,514,256]{2,1,0:T(8,128)(2,1)}), bf16[16,514,256]{2,1,0:T(8,128)(2,1)}) %all-gather.9.cloned.1.call-update) | async-done | bytes 4210704 | tf_op jit(solution)/shard_map/all_gather | solution.py:31
  86.7 0.9 slice_convert_fusion
  87.6 0.0 copy-start
  87.6 3.6 %fusion.2 = bf16[128,8192]{1,0:T(8,128)(2,1)} fusion(bf16[128,8192]{1,0:T(8,128)(2,1)} %copy-done.3, f32[8192]{0:T(1024)S(1)} %bitcast.58, f32[128]{0:T(128)S(1)} %add_rsqrt_fusion.1), kind=kLoop, calls=%fused_computation.4 | loop fusion | flops 4194304 | bytes 4227584 | tf_op jit(solution)/shard_map/convert_element_type | solution.py:36
  91.2 6.1 %all-to-all-start = ((bf16[16,128,512]{2,1,0:T(8,128)(2,1)}), bf16[16,128,512]{2,1,0:T(8,128)(2,1)}, u32[]{:S(2)}, u32[]{:S(2)}) async-start(bf16[16,128,512]{2,1,0:T(8,128)(2,1)} %bitcast.52), calls=%async_computation | async-start | bytes 4194304 | tf_op jit(solution)/shard_map/all_to_all | solution.py:54
  97.3 0.0 all-gather.7.cloned.1.call-start
  97.4 0.5 multiply_reduce_fusion
  97.9 3.7 %fusion.24 = f32[128,256]{1,0:T(8,128)S(1)} fusion(bf16[16,514,256]{2,1,0:T(8,128)(2,1)} %all-gather.9.cloned.1.call-done, bf16[16,16,8,512]{3,2,1,0:T(8,128)(2,1)} %bitcast.57), kind=kOutput, calls=%fused_computation.30 | convolution fusion | flops 536870912 | bytes 6422528 | tf_op jit(solution)/shard_map/tfr,frh->th/dot_general | solution.py:41
  101.6 3.1 %collective-permute-start.1 = (f32[128,256]{1,0:T(8,128)S(1)}, f32[128,256]{1,0:T(8,128)S(1)}, u32[]{:S(2)}, u32[]{:S(2)}) collective-permute-start(f32[128,256]{1,0:T(8,128)S(1)} %fusion.24), channel_id=1, source_target_pairs={{0,1},{1,0},{2,3},{3,2},{4,5},{5,4},{6,7},{7,6},{8,9},{9,8},{10,11... | collective-permute-start | bytes 393224 | tf_op jit(solution)/shard_map/ppermute | solution.py:44
  104.7 0.0 copy-done.2
  104.7 0.0 copy-done.7
  104.7 0.0 copy-start.5
  104.7 0.0 copy-start.4
  104.7 2.6 fusion.21
  107.3 0.0 collective-permute-done.1
  107.4 0.0 copy-done.5
  107.4 0.7 fusion.31
  108.1 0.0 all-gather.7.cloned.1.call-update
  108.1 0.2 copy.18
  108.3 0.7 compare_reduce_fusion.1
  109.0 0.6 compare_reduce_fusion
  109.6 110.0 %all-gather.3 = f32[16,1,128]{2,1,0:T(1,128)S(1)} all-gather(f32[1,1,128]{2,1,0:T(1,128)S(1)} %get-tuple-element.48), channel_id=3, replica_groups=mesh['template'=16,'fsdp'=16,'dp'=2] {'fsdp'}, dimensions={0}, use_global_device_ids=true | all-gather | bytes 8704 | tf_op jit(solution)/shard_map/all_gather | solution.py:55
  219.6 3.2 %all-gather.7.cloned.1.call-done = bf16[2048,512]{1,0:T(8,128)(2,1)} async-done(((bf16[128,512]{1,0:T(8,128)(2,1)}), bf16[2048,512]{1,0:T(8,128)(2,1)}) %all-gather.7.cloned.1.call-update) | async-done | bytes 2097168 | tf_op jit(solution)/shard_map/all_gather | solution.py:56
  222.8 0.0 all-to-all-done
  222.8 3.8 %fusion.7 = f32[512]{0:T(512)S(1)} fusion(bf16[2048,512]{1,0:T(8,128)(2,1)} %bitcast.16, bf16[2048,512]{1,0:T(8,128)(2,1)} %all-gather.7.cloned.1.call-done, f32[2048]{0:T(1024)S(1)} %bitcast.61, bf16[1,512,512]{2,1,0:T(8,128)(2,1)S(1)} %copy-done.4), kind=kOutput, calls=%fused_computation.10 | convolution fusion | flops 1080032768 | bytes 4728832 | tf_op jit(solution)/shard_map/th,dh->td/dot_general | solution.py:63
  226.6 1.3 broadcast_select_fusion.2
  227.9 0.2 scatter.11
  228.2 3.9 %convert_multiply_fusion.3 = (f32[512,512]{0,1:T(8,128)S(1)}, f32[512,512]{0,1:T(8,128)S(1)}) fusion(bf16[1,512,512]{1,2,0:T(8,128)(2,1)S(1)} %copy.18, bf16[2048,512]{1,0:T(8,128)(2,1)} %all-gather.7.cloned.1.call-done, bf16[2048,512]{1,0:T(8,128)(2,1)} %bitcast.16, f32[2048]{0:T(1024)S(1)} %bitcast.62, f32[512]{0:T(512)S(1)} %bitcast.63), kind=kOutput, calls=%fused_computation.31 | convolution fusion | flops 1084751872 | bytes 6825984 | tf_op jit(solution)/shard_map/td,th->dh/dot_general | solution.py:62
  232.1 0.2 pad_maximum_fusion
  232.3 2.0 copy.19
  234.3 42.7 %all_to_all.15 = f32[32,16,1152]{2,1,0:T(8,128)S(1)} all-to-all(f32[32,16,1152]{2,1,0:T(8,128)} %bitcast.49), channel_id=1, replica_groups=mesh['template'=16,'fsdp'=16,'dp'=2] {'dp','template'}, dimensions={0} | all-to-all | bytes 4718592 | tf_op jit(solution)/shard_map/all_to_all | solution.py:72
  276.9 0.1 reduce_sum.42
  277.1 0.7 fusion.32
  277.8 16.6 %all_to_all.16 = f32[16,16,640]{2,1,0:T(8,128)S(1)} all-to-all(f32[16,16,640]{2,1,0:T(8,128)S(1)} %broadcast_in_dim.2), channel_id=1, replica_groups=mesh['template'=16,'fsdp'=16,'dp'=2] {'template'}, dimensions={0} | all-to-all | bytes 1310720 | tf_op jit(solution)/shard_map/all_to_all | solution.py:76
  294.5 0.9 slice.81
  295.3 0.7 slice_reduce_fusion
  (18 shorter events, 0.2 us)
Async XLA Ops:
  7.2 79.5 %all-gather.9.cloned.1.call-start = ((), (), s32[]{:S(2)}) async-start(), calls=%async_computation.4 | async-start | bytes 4526080 | tf_op jit(solution)/shard_map/all_gather | solution.py:31
  9.7 44.6 %collective-permute-start = (bf16[128,8192]{1,0:T(8,128)(2,1)}, bf16[128,8192]{1,0:T(8,128)(2,1)S(1)}, u32[]{:S(2)}, u32[]{:S(2)}) collective-permute-start(bf16[128,8192]{1,0:T(8,128)(2,1)} %bitcast.50), channel_id=1, source_target_pairs={{0,1},{1,0},{2,3},{3,2},{4,5},{5,4},{6,7},{7,6},{8,9},{9,8},{10,11... | collective-permute-start | bytes 6291464 | tf_op jit(solution)/shard_map/ppermute | solution.py:24
  16.1 1.4 copy-start.1
  54.3 1.3 copy-start.3
  87.6 9.8 %copy-start = (bf16[1,128,8192]{2,1,0:T(8,128)(2,1)S(1)}, bf16[1,128,8192]{2,1,0:T(8,128)(2,1)}, u32[]{:S(2)}) copy-start(bf16[1,128,8192]{2,1,0:T(8,128)(2,1)} %param.10) | copy-start | bytes 6291460
  91.2 131.6 %all-to-all-start = ((bf16[16,128,512]{2,1,0:T(8,128)(2,1)}), bf16[16,128,512]{2,1,0:T(8,128)(2,1)}, u32[]{:S(2)}, u32[]{:S(2)}) async-start(bf16[16,128,512]{2,1,0:T(8,128)(2,1)} %bitcast.52), calls=%async_computation | async-start | bytes 4194304 | tf_op jit(solution)/shard_map/all_to_all | solution.py:54
  97.3 125.5 %all-gather.7.cloned.1.call-start = ((), (), s32[]{:S(2)}) async-start(), calls=%async_computation.3 | async-start | bytes 2228224 | tf_op jit(solution)/shard_map/all_gather | solution.py:56
  97.9 6.8 %copy-start.2 = (bf16[16,8,16,512]{3,2,1,0:T(8,128)(2,1)S(1)}, bf16[16,8,16,512]{3,2,1,0:T(8,128)(2,1)}, u32[]{:S(2)}) copy-start(bf16[16,8,16,512]{3,2,1,0:T(8,128)(2,1)} %copy-done.1) | copy-start | bytes 6291460
  97.9 6.8 %copy-start.7 = (bf16[16,514,256]{2,1,0:T(8,128)(2,1)S(1)}, bf16[16,514,256]{2,1,0:T(8,128)(2,1)}, u32[]{:S(2)}) copy-start(bf16[16,514,256]{2,1,0:T(8,128)(2,1)} %all-gather.9.cloned.1.call-done) | copy-start | bytes 12632068
  101.6 5.8 %collective-permute-start.1 = (f32[128,256]{1,0:T(8,128)S(1)}, f32[128,256]{1,0:T(8,128)S(1)}, u32[]{:S(2)}, u32[]{:S(2)}) collective-permute-start(f32[128,256]{1,0:T(8,128)S(1)} %fusion.24), channel_id=1, source_target_pairs={{0,1},{1,0},{2,3},{3,2},{4,5},{5,4},{6,7},{7,6},{8,9},{9,8},{10,11... | collective-permute-start | bytes 393224 | tf_op jit(solution)/shard_map/ppermute | solution.py:44
  104.7 2.7 copy-start.5
  104.7 3.4 %copy-start.4 = (bf16[1,512,512]{2,1,0:T(8,128)(2,1)S(1)}, bf16[1,512,512]{2,1,0:T(8,128)(2,1)}, u32[]{:S(2)}) copy-start(bf16[1,512,512]{2,1,0:T(8,128)(2,1)} %param.12) | copy-start | bytes 1572868
  222.8 3.8 %copy-start.6 = (bf16[1,512]{1,0:T(2,128)(2,1)S(1)}, bf16[1,512]{1,0:T(2,128)(2,1)}, u32[]{:S(2)}) copy-start(bf16[1,512]{1,0:T(2,128)(2,1)} %param.13) | copy-start | bytes 3076
Sparse Core Ops, SparseCore 0:
  10.7 75.9 all-gather.8
  108.2 114.4 all-gather.6

commit v18 on v8

--- a/solution.py
+++ b/solution.py
@@ -43,8 +43,10 @@
     values = jnp.concatenate([first, second], axis=1) * scale
     delta = (values - goal.astype(jnp.float32)).astype(jnp.bfloat16)
 
-    late_batch, _, _ = lax.optimization_barrier((token_batch, mine_half, other_normed))
-    local_hidden = lax.all_to_all(late_batch, "fsdp", 1, 0, tiled=True)
+    n_f = lax.axis_size("fsdp")
+    by_dest = jnp.transpose(token_batch.reshape(token_batch.shape[0], n_f, rows), (1, 0, 2))
+    late_batch, _ = lax.optimization_barrier((by_dest, theirs_half))
+    local_hidden = lax.all_to_all(late_batch, "fsdp", 0, 0, tiled=True).reshape(-1, rows)
     local_ratio = lax.all_gather(ratio, "fsdp", axis=0, tiled=True)
     local_delta = lax.all_gather(delta, "fsdp", axis=0, tiled=True)
     local_xhat = local_hidden.astype(jnp.float32) * local_ratio

time: 309 us -> 306 us (level)
  waiting for transfers between devices: 74.3 us -> 68.1 us
  other arithmetic: 12 us -> 7.52 us
  blocking collectives: 171 us -> 175 us
  transfers between devices with their start and end apart: 5 -> 5, of which waited for: 4 -> 3; matrix products, arithmetic and copies ran while one was open for 3% -> 4% of each run, Pallas kernels for 0% -> 0%
where the time goes in v18:
time: 306 us; the launch traced here: 305 us
  blocking collectives  175 us (57%)
  waiting for transfers between devices  68.1 us (22%)
  local copies, waits for them, and re-layouts  15.7 us (5%)
  between operations  14.3 us (5%)
  starting transfers between devices  13.3 us (4%)
  matrix products  11.5 us (4%)
  other arithmetic  7.52 us (2%)
    all_gather x1, blocking collectives, body(): local_ratio = lax.all_gather(ratio, 'fsdp', axis=0, tiled=True)  114 us
    all_to_all x1, blocking collectives, body(): parts = lax.all_to_all(pack, ('dp', 'template'), 0, 0, tiled=True)  44.3 us
    ppermute x1, waiting for transfers between devices, body(): other_hidden = lax.ppermute(token_batch, 'dp', swap)  35.7 us
    all_gather x1, waiting for transfers between devices, body(): gathered = lax.all_gather(w_ext, 'fsdp', axis=0, tiled=False)  30.5 us
    all_to_all x1, blocking collectives, body(): lax.all_to_all(jnp.broadcast_to(done[None], (n_t,) + done.shape), 'templa...  16.6 us
  transfers between devices with their start and end apart: 5, of which 3 were waited for; matrix products, arithmetic and copies ran while one was open for 4% of the time, Pallas kernels for 0%

profile of v18, /device:TPU:1, one launch (start us, length us, event | category | flops | bytes accessed | tf_op | source)
XLA Modules:
  0.0 305.2 jit_solution(10751523112263301250)
XLA Ops:
  7.2 0.0 all-gather.9.cloned.1.call-start
  7.2 0.8 fusion.26
  8.0 1.0 dynamic-slice_bitcast_fusion
  9.0 0.7 maximum_bitcast_fusion
  9.7 0.0 all-gather.9.cloned.1.call-update
  9.7 4.0 %collective-permute-start = (bf16[128,8192]{1,0:T(8,128)(2,1)}, bf16[128,8192]{1,0:T(8,128)(2,1)S(1)}, u32[]{:S(2)}, u32[]{:S(2)}) collective-permute-start(bf16[128,8192]{1,0:T(8,128)(2,1)} %bitcast.44), channel_id=1, source_target_pairs={{0,1},{1,0},{2,3},{3,2},{4,5},{5,4},{6,7},{7,6},{8,9},{9,8},{10,11... | collective-permute-start | bytes 6291464 | tf_op jit(solution)/shard_map/ppermute | solution.py:24
  13.7 2.4 copy.14
  16.1 2.5 copy.17
  18.6 35.7 %collective-permute-done = bf16[128,8192]{1,0:T(8,128)(2,1)S(1)} collective-permute-done((bf16[128,8192]{1,0:T(8,128)(2,1)}, bf16[128,8192]{1,0:T(8,128)(2,1)S(1)}, u32[]{:S(2)}, u32[]{:S(2)}) %collective-permute-start) | collective-permute-done | bytes 2097184 | tf_op jit(solution)/shard_map/ppermute | solution.py:24
  54.3 1.3 copy-done.2
  55.7 0.5 fusion
  56.2 30.5 %all-gather.9.cloned.1.call-done = bf16[16,514,256]{2,1,0:T(8,128)(2,1)} async-done(((bf16[1,514,256]{2,1,0:T(8,128)(2,1)}), bf16[16,514,256]{2,1,0:T(8,128)(2,1)}) %all-gather.9.cloned.1.call-update) | async-done | bytes 4210704 | tf_op jit(solution)/shard_map/all_gather | solution.py:31
  86.7 0.8 convert_bitcast_fusion
  87.5 0.0 copy-start.3
  87.6 2.6 slice.76
  90.2 0.0 copy-start.1
  90.2 1.9 copy-done.1
  92.1 0.0 copy-done.3
  92.1 0.8 fusion.13
  92.9 6.1 %all-to-all-start = ((bf16[16,128,512]{2,1,0:T(8,128)(2,1)}), bf16[16,128,512]{2,1,0:T(8,128)(2,1)}, u32[]{:S(2)}, u32[]{:S(2)}) async-start(bf16[16,128,512]{2,1,0:T(8,128)(2,1)} %bitcast.46), calls=%async_computation | async-start | bytes 4194304 | tf_op jit(solution)/shard_map/all_to_all | solution.py:49
  99.0 0.0 all-gather.7.cloned.1.call-start
  99.0 0.0 copy-done
  99.0 0.5 multiply_reduce_fusion
  99.5 0.0 copy-start.5
  99.6 3.2 %collective-permute-start.1 = (f32[128,256]{1,0:T(8,128)S(1)}, f32[128,256]{1,0:T(8,128)S(1)}, u32[]{:S(2)}, u32[]{:S(2)}) collective-permute-start(f32[128,256]{1,0:T(8,128)S(1)} %fusion.13), channel_id=1, source_target_pairs={{0,1},{1,0},{2,3},{3,2},{4,5},{5,4},{6,7},{7,6},{8,9},{9,8},{10,11... | collective-permute-start | bytes 393224 | tf_op jit(solution)/shard_map/ppermute | solution.py:39
  102.8 0.0 copy-start.4
  102.8 3.0 fusion.10
  105.8 0.0 collective-permute-done.1
  105.9 0.7 fusion.23
  106.6 0.0 all-gather.7.cloned.1.call-update
  106.6 0.2 copy.12
  106.8 0.6 compare_reduce_fusion.1
  107.4 0.6 compare_reduce_fusion
  108.1 113.9 %all-gather.3 = f32[16,1,128]{2,1,0:T(1,128)S(1)} all-gather(f32[1,1,128]{2,1,0:T(1,128)S(1)} %get-tuple-element.46), channel_id=3, replica_groups=mesh['template'=16,'fsdp'=16,'dp'=2] {'fsdp'}, dimensions={0}, use_global_device_ids=true | all-gather | bytes 8704 | tf_op jit(solution)/shard_map/all_gather | solution.py:50
  222.0 1.8 all-gather.7.cloned.1.call-done
  223.8 0.0 all-to-all-done
  223.8 3.8 %fusion.7 = f32[512]{0:T(512)S(1)} fusion(bf16[2048,512]{1,0:T(8,128)(2,1)} %bitcast.16, bf16[2048,512]{1,0:T(8,128)(2,1)} %all-gather.7.cloned.1.call-done, f32[2048]{0:T(1024)S(1)} %bitcast.54, bf16[1,512,512]{2,1,0:T(8,128)(2,1)S(1)} %copy-done.4), kind=kOutput, calls=%fused_computation.10 | convolution fusion | flops 1080032768 | bytes 4728832 | tf_op jit(solution)/shard_map/th,dh->td/dot_general | solution.py:58
  227.6 1.2 broadcast_select_fusion.2
  228.9 0.1 scatter.11
  229.0 3.9 %convert_multiply_fusion.3 = (f32[512,512]{0,1:T(8,128)S(1)}, f32[512,512]{0,1:T(8,128)S(1)}) fusion(bf16[1,512,512]{1,2,0:T(8,128)(2,1)S(1)} %copy.12, bf16[2048,512]{1,0:T(8,128)(2,1)} %all-gather.7.cloned.1.call-done, bf16[2048,512]{1,0:T(8,128)(2,1)} %bitcast.16, f32[2048]{0:T(1024)S(1)} %bitcast.55, f32[512]{0:T(512)S(1)} %bitcast.56), kind=kOutput, calls=%fused_computation.27 | convolution fusion | flops 1084751872 | bytes 6825984 | tf_op jit(solution)/shard_map/td,th->dh/dot_general | solution.py:57
  232.9 0.2 pad_maximum_fusion
  233.1 2.0 copy.13
  235.0 44.3 %all_to_all.15 = f32[32,16,1152]{2,1,0:T(8,128)S(1)} all-to-all(f32[32,16,1152]{2,1,0:T(8,128)} %bitcast.43), channel_id=1, replica_groups=mesh['template'=16,'fsdp'=16,'dp'=2] {'dp','template'}, dimensions={0} | all-to-all | bytes 4718592 | tf_op jit(solution)/shard_map/all_to_all | solution.py:67
  279.4 0.1 reduce_sum.42
  279.5 0.6 fusion.24
  280.2 16.6 %all_to_all.16 = f32[16,16,640]{2,1,0:T(8,128)S(1)} all-to-all(f32[16,16,640]{2,1,0:T(8,128)S(1)} %broadcast_in_dim.2), channel_id=1, replica_groups=mesh['template'=16,'fsdp'=16,'dp'=2] {'template'}, dimensions={0} | all-to-all | bytes 1310720 | tf_op jit(solution)/shard_map/all_to_all | solution.py:71
  296.8 0.9 slice.81
  297.7 0.7 slice_reduce_fusion
  (15 shorter events, 0.2 us)
Async XLA Ops:
  7.2 79.5 %all-gather.9.cloned.1.call-start = ((), (), s32[]{:S(2)}) async-start(), calls=%async_computation.4 | async-start | bytes 4526080 | tf_op jit(solution)/shard_map/all_gather | solution.py:31
  9.7 44.6 %collective-permute-start = (bf16[128,8192]{1,0:T(8,128)(2,1)}, bf16[128,8192]{1,0:T(8,128)(2,1)S(1)}, u32[]{:S(2)}, u32[]{:S(2)}) collective-permute-start(bf16[128,8192]{1,0:T(8,128)(2,1)} %bitcast.44), channel_id=1, source_target_pairs={{0,1},{1,0},{2,3},{3,2},{4,5},{5,4},{6,7},{7,6},{8,9},{9,8},{10,11... | collective-permute-start | bytes 6291464 | tf_op jit(solution)/shard_map/ppermute | solution.py:24
  54.3 1.3 copy-start.2
  87.5 4.6 %copy-start.3 = (bf16[128,8192]{1,0:T(8,128)(2,1)S(1)}, bf16[128,8192]{1,0:T(8,128)(2,1)}, u32[]{:S(2)}) copy-start(bf16[128,8192]{1,0:T(8,128)(2,1)} %copy-done.2) | copy-start | bytes 6291460
  90.2 1.9 copy-start.1
  92.1 6.9 %copy-start = (bf16[1,128,8192]{2,1,0:T(8,128)(2,1)S(1)}, bf16[1,128,8192]{2,1,0:T(8,128)(2,1)}, u32[]{:S(2)}) copy-start(bf16[1,128,8192]{2,1,0:T(8,128)(2,1)} %param.10) | copy-start | bytes 6291460
  92.9 130.9 %all-to-all-start = ((bf16[16,128,512]{2,1,0:T(8,128)(2,1)}), bf16[16,128,512]{2,1,0:T(8,128)(2,1)}, u32[]{:S(2)}, u32[]{:S(2)}) async-start(bf16[16,128,512]{2,1,0:T(8,128)(2,1)} %bitcast.46), calls=%async_computation | async-start | bytes 4194304 | tf_op jit(solution)/shard_map/all_to_all | solution.py:49
  99.0 124.8 %all-gather.7.cloned.1.call-start = ((), (), s32[]{:S(2)}) async-start(), calls=%async_computation.3 | async-start | bytes 2228224 | tf_op jit(solution)/shard_map/all_gather | solution.py:51
  99.5 6.3 %copy-start.5 = (bf16[1,128,512]{2,1,0:T(8,128)(2,1)S(1)}, bf16[1,128,512]{2,1,0:T(8,128)(2,1)}, u32[]{:S(2)}) copy-start(bf16[1,128,512]{2,1,0:T(8,128)(2,1)} %param.11) | copy-start | bytes 393220
  99.6 6.3 %collective-permute-start.1 = (f32[128,256]{1,0:T(8,128)S(1)}, f32[128,256]{1,0:T(8,128)S(1)}, u32[]{:S(2)}, u32[]{:S(2)}) collective-permute-start(f32[128,256]{1,0:T(8,128)S(1)} %fusion.13), channel_id=1, source_target_pairs={{0,1},{1,0},{2,3},{3,2},{4,5},{5,4},{6,7},{7,6},{8,9},{9,8},{10,11... | collective-permute-start | bytes 393224 | tf_op jit(solution)/shard_map/ppermute | solution.py:39
  102.8 3.8 %copy-start.4 = (bf16[1,512,512]{2,1,0:T(8,128)(2,1)S(1)}, bf16[1,512,512]{2,1,0:T(8,128)(2,1)}, u32[]{:S(2)}) copy-start(bf16[1,512,512]{2,1,0:T(8,128)(2,1)} %param.12) | copy-start | bytes 1572868
  223.8 3.8 %copy-start.6 = (bf16[1,512]{1,0:T(2,128)(2,1)S(1)}, bf16[1,512]{1,0:T(2,128)(2,1)}, u32[]{:S(2)}) copy-start(bf16[1,512]{1,0:T(2,128)(2,1)} %param.13) | copy-start | bytes 3076
Sparse Core Ops, SparseCore 0:
  10.7 75.9 all-gather.8
  106.7 117.0 all-gather.6
